TPU v7x, 256 devices: a whole 4x4x8 slice. The times are simulated.
256 devices in a mesh: dp: 64 (over x, z_lo, y, core), fsdp: 4 (over z_hi).
Axes of the slice: x: 4, y: 4, z: 8 (z_hi: 4, z_lo: 2; z = z_hi * 2 + z_lo), core: 2. Of those that a mesh axis runs over, the one named last changes fastest.
Arguments:
- bag_ids: int32 [32768, 64, 4], P(('dp', 'fsdp')), may hold values from 0 to 8191
- bag_counts: int32 [32768, 64], P(('dp', 'fsdp')), may hold values from 1 to 4
- emb_table: bfloat16 [8192, 8192], P(None, 'dp'), may hold values from -3 to 3
- cross_down: bfloat16 [8192, 512], P('fsdp'), may hold values from -0.0625 to 0.0625
- cross_up: bfloat16 [512, 8192], P(None, 'fsdp'), may hold values from -0.25 to 0.25
- cross_bias: float32 [8192], replicated, may hold values from -2 to 2
- cotangent: bfloat16 [32768, 8192], P(('dp', 'fsdp')), may hold values from -4 to 4
Outputs:
- table_grad: float32 [8192, 8192], P('fsdp', 'dp')
Inputs may be any that keep to these rules, and one draw needn't show every extreme that they name: `bag_ids`: ids at positions at or past a bag's count are read by no step.
All inputs are finite; a program needn't handle non-finite values.
Results may differ from a plain program's by a relative error of at most 0.0045.
Values may be sent and summed in bfloat16 or wider, within the bound.
No kernel may reach another device: no remote copies, remote signals or barrier semaphores. Data moves between devices by JAX's collectives and lax.ppermute only.
A program may use at most 192 MiB of HBM per device.

v0:
```python
import jax
import jax.numpy as jnp
from jax import lax
from jax.sharding import PartitionSpec as P


def scatter_rows(height, index_rows, grads, table_count, slot_count, embed_width, offset):
    sample_count = index_rows.shape[0]
    local_rows = index_rows.reshape(sample_count, table_count, slot_count) - offset
    inside = (local_rows >= 0) & (local_rows < height)
    table_iota = lax.broadcasted_iota(jnp.int32, local_rows.shape, 1)
    flat_rows = jnp.where(inside, local_rows * table_count + table_iota, height * table_count)
    column_grads = grads.reshape(sample_count, table_count, 1, embed_width).astype(jnp.float32)
    updates = jnp.broadcast_to(column_grads, (sample_count, table_count, slot_count, embed_width))
    target = jnp.zeros((height * table_count, embed_width), jnp.float32)
    target = target.at[flat_rows.reshape(-1)].add(updates.reshape(-1, embed_width), mode="drop")
    return target


def on_device(bag_ids, bag_counts, emb_table, cross_down, cross_up, cross_bias, cotangent):
    row_count, table_count, slot_count = bag_ids.shape
    vocab_rows, col_piece = emb_table.shape
    dp_size = lax.axis_size("dp")
    local_tables = table_count // dp_size
    embed_width = col_piece // local_tables
    slot_iota = lax.broadcasted_iota(jnp.int32, bag_ids.shape, 2)
    live_ids = jnp.where(slot_iota < bag_counts[:, :, None], bag_ids, vocab_rows)
    send_ids = live_ids.reshape(row_count, table_count * slot_count)
    got_ids = lax.all_to_all(send_ids, "dp", split_axis=1, concat_axis=0, tiled=True)
    sample_count = got_ids.shape[0]
    table_iota = lax.broadcasted_iota(jnp.int32, (sample_count, local_tables, slot_count), 1)
    flat_ids = got_ids.reshape(sample_count, local_tables, slot_count) * local_tables + table_iota
    picked = jnp.take(emb_table, flat_ids, axis=0, mode="fill", fill_value=0)
    pooled_local = jnp.sum(picked.astype(jnp.float32), axis=2).astype(jnp.bfloat16)
    pooled_local = pooled_local.reshape(sample_count, col_piece)
    pooled = lax.all_to_all(pooled_local, "dp", split_axis=0, concat_axis=1, tiled=True)
    upstream = cotangent.astype(jnp.float32)
    grad_gate = (upstream * pooled.astype(jnp.float32)).astype(jnp.bfloat16)
    down_full, up_full = (
        lax.all_gather(cross_down, "fsdp", axis=0, tiled=True),
        lax.all_gather(cross_up, "fsdp", axis=1, tiled=True),
    )
    low_rank = jnp.dot(pooled, down_full, preferred_element_type=jnp.float32).astype(jnp.bfloat16)
    gate_value = jnp.dot(low_rank, up_full, preferred_element_type=jnp.float32) + cross_bias
    grad_low = lax.dot_general(
        grad_gate, up_full, (((1,), (1,)), ((), ())), preferred_element_type=jnp.float32
    ).astype(jnp.bfloat16)
    back_term = lax.dot_general(
        grad_low, down_full, (((1,), (1,)), ((), ())), preferred_element_type=jnp.float32
    )
    grad_pooled = (upstream * (gate_value + 1.0) + back_term).astype(jnp.bfloat16)
    grad_local = lax.all_to_all(grad_pooled, "dp", split_axis=1, concat_axis=0, tiled=True)
    partial_value = scatter_rows(
        vocab_rows, got_ids, grad_local, local_tables, slot_count, embed_width, 0
    )
    return lax.psum_scatter(partial_value, "fsdp", scatter_dimension=0, tiled=True)


def solution(mesh):
    placed = (
        P(("dp", "fsdp"), None, None),
        P(("dp", "fsdp"), None),
        P(None, "dp"),
        P("fsdp", None),
        P(None, "fsdp"),
        P(),
        P(("dp", "fsdp"), None),
    )
    return jax.shard_map(
        on_device, mesh=mesh, in_specs=placed, out_specs=P("fsdp", "dp"), check_vma=False
    )
```

profile of v0, /device:TPU:1, one launch (start us, length us, event | category | flops | bytes accessed | tf_op | source)
XLA Modules:
  0.0 684.7 jit_solution(626548155860651845)
XLA Ops:
  6.5 0.0 copy-start
  6.5 0.0 copy-start.2
  6.5 0.0 copy-start.4
  6.5 0.0 all-gather.3.cloned.1.call-start
  6.5 0.7 all-gather.3.cloned.1.call-update
  7.3 0.0 all-gather.5.cloned.1.call-start
  7.3 0.7 all-gather.5.cloned.1.call-update
  8.0 0.0 copy-done.2
  8.0 0.0 copy-done.4
  8.1 18.7 %all_to_all.45 = s32[128,64,4]{0,2,1:T(4,128)S(1)} all-to-all(s32[128,64,4]{0,2,1:T(4,128)S(1)} %fusion.24), channel_id=1, replica_groups=mesh['dp'=64,'fsdp'=4] {'dp'}, dimensions={1} | all-to-all | bytes 262144 | tf_op jit(solution)/shard_map/all_to_all | solution.py:29
  26.8 2.7 copy.10
  29.5 5.1 reshape.183
  34.5 0.1 compare_and_fusion
  34.6 1.7 copy.9
  36.4 0.0 copy-done
  36.4 114.2 %gather_fusion = bf16[32768,128]{1,0:T(8,128)(2,1)} fusion(bf16[8192,128]{1,0:T(8,128)(2,1)S(1)} %copy-done, s32[32768]{0:T(1024)S(1)} %broadcast_clamp_fusion), kind=kCustom, calls=%fused_computation | custom fusion | bytes 16908288 | tf_op jit(solution)/shard_map/jit(_take)/gather | solution.py:33
  150.6 47.3 %select_reduce_fusion = bf16[8192,128]{1,0:T(8,128)(2,1)} fusion(bf16[8192,1,4,128]{3,2,0,1:T(4,128)(2,1)} %bitcast.54, pred[8192,4]{1,0:T(8,128)(4,1)S(1)} %copy.9), kind=kLoop, calls=%fused_computation.7 | loop fusion | flops 7340032 | bytes 10518528 | tf_op jit(solution)/shard_map/reduce_sum | solution.py:34
  197.9 4.6 all-to-all-start.1
  202.5 0.0 copy-start.3
  202.5 2.7 copy.8
  205.2 6.1 reshape.176
  211.3 86.5 %all-to-all-done.1 = bf16[64,128,128]{2,1,0:T(8,128)(2,1)S(1)} async-done(((bf16[64,128,128]{2,1,0:T(8,128)(2,1)}), bf16[64,128,128]{2,1,0:T(8,128)(2,1)S(1)}, u32[]{:S(2)}, u32[]{:S(2)}) %all-to-all-start.1) | async-done | bytes 2097184 | tf_op jit(solution)/shard_map/all_to_all | solution.py:36
  297.8 0.0 all-gather.3.cloned.1.call-done
  297.8 49.2 %all-gather.5.cloned.1.call-done = bf16[512,8192]{1,0:T(8,128)(2,1)} async-done(((bf16[512,2048]{1,0:T(8,128)(2,1)}), bf16[512,8192]{1,0:T(8,128)(2,1)}) %all-gather.5.cloned.1.call-update) | async-done | bytes 8388624 | tf_op jit(solution)/shard_map/all_gather | solution.py:41
  347.0 0.0 copy-done.3
  347.0 11.1 %fusion.1 = f32[128,8192]{1,0:T(8,128)} fusion(bf16[512,8192]{1,0:T(8,128)(2,1)} %all-gather.5.cloned.1.call-done, bf16[128,8192]{1,0:T(8,128)(2,1)} %param.13, f32[8192]{0:T(1024)S(1)} %copy-done.3, bf16[8192,512]{1,0:T(8,128)(2,1)} %all-gather.3.cloned.1.call-done, bf16[64,128,128]{2,1,0:T(8,128)(2,1)S(1)} %all-to-all-done.1), kind=kOutput, calls=%fused_computation.5 | convolution fusion | flops 2151743488 | bytes 25198592 | tf_op jit(solution)/shard_map/dot_general | solution.py:44
  358.1 15.4 %fusion.13 = bf16[16,64,8,128]{3,2,1,0:T(8,128)(2,1)} fusion(f32[128,8192]{1,0:T(8,128)} %fusion.1, bf16[8192,512]{1,0:T(8,128)(2,1)} %all-gather.3.cloned.1.call-done, bf16[512,8192]{1,0:T(8,128)(2,1)} %all-gather.5.cloned.1.call-done, bf16[128,8192]{1,0:T(8,128)(2,1)} %param.13, bf16[64,128,128]{2,1,0:T(8,128)(2,1)S(1)} %all-to-all-done.1), kind=kOutput, calls=%fused_computation.19 | convolution fusion | flops 2153840640 | bytes 27262976 | tf_op jit(solution)/shard_map/dot_general | solution.py:48
  373.5 3.5 copy.32
  377.0 7.7 %all-to-all-start.2 = ((bf16[128,64,128]{2,0,1:T(8,128)(2,1)}), bf16[128,64,128]{2,0,1:T(8,128)(2,1)S(1)}, u32[]{:S(2)}, u32[]{:S(2)}) async-start(bf16[128,64,128]{2,0,1:T(8,128)(2,1)} %bitcast.57), calls=%async_computation.2 | async-start | bytes 4194304 | tf_op jit(solution)/shard_map/all_to_all | solution.py:52
  384.8 0.3 reduce-scatter.2.cloned.1.call-start
  385.0 0.2 compare_select_fusion
  385.3 28.5 %all-to-all-done.2 = bf16[128,64,128]{2,0,1:T(8,128)(2,1)S(1)} async-done(((bf16[128,64,128]{2,0,1:T(8,128)(2,1)}), bf16[128,64,128]{2,0,1:T(8,128)(2,1)S(1)}, u32[]{:S(2)}, u32[]{:S(2)}) %all-to-all-start.2) | async-done | bytes 2097184 | tf_op jit(solution)/shard_map/all_to_all | solution.py:52
  413.8 0.5 convert_element_type.44
  414.3 7.4 %broadcast_in_dim.31 = f32[8192,1,4,128]{3,2,0,1:T(4,128)} broadcast(f32[8192,128]{1,0:T(8,128)S(1)} %bitcast.56), dimensions={0,3} | broadcast | bytes 20971520 | tf_op jit(solution)/shard_map/broadcast_in_dim | solution.py:14
  421.8 0.0 copy-start.1
  421.8 176.5 %scatter_custom_fusion = f32[8192,128]{1,0:T(8,128)} fusion(s32[32768]{0:T(1024)S(1)} %bitcast.60, f32[32768,128]{1,0:T(8,128)} %bitcast.55, f32[]{:T(128)} %constant.7.clone.1), kind=kCustom, calls=%fused_computation.15 | custom fusion | flops 4194304 | bytes 4194816 | tf_op jit(solution)/shard_map/scatter-add | solution.py:16
  598.3 0.0 reduce-scatter.2.cloned.1.call-update
  598.3 79.8 %reduce-scatter.2.cloned.1.call-done = f32[2048,128]{1,0:T(8,128)} async-done(((f32[8192,128]{1,0:T(8,128)}), f32[2048,128]{1,0:T(8,128)}) %reduce-scatter.2.cloned.1.call-update) | async-done | bytes 1048592 | tf_op jit(solution)/shard_map/reduce_scatter | solution.py:56
  678.1 0.0 copy-done.1
  (3 shorter events, 0.1 us)
Async XLA Ops:
  6.5 29.9 %copy-start = (bf16[8192,128]{1,0:T(8,128)(2,1)S(1)}, bf16[8192,128]{1,0:T(8,128)(2,1)}, u32[]{:S(2)}) copy-start(bf16[8192,128]{1,0:T(8,128)(2,1)} %param.9) | copy-start | bytes 6291460
  6.5 1.5 copy-start.2
  6.5 1.5 copy-start.4
  6.5 291.3 %all-gather.3.cloned.1.call-start = ((), (), s32[]{:S(2)}) async-start(), calls=%async_computation.4 | async-start | bytes 10485760 | tf_op jit(solution)/shard_map/all_gather | solution.py:40
  7.3 339.7 %all-gather.5.cloned.1.call-start = ((), (), s32[]{:S(2)}) async-start(), calls=%async_computation.5 | async-start | bytes 10485760 | tf_op jit(solution)/shard_map/all_gather | solution.py:41
  197.9 99.9 %all-to-all-start.1 = ((bf16[64,128,128]{2,1,0:T(8,128)(2,1)}), bf16[64,128,128]{2,1,0:T(8,128)(2,1)S(1)}, u32[]{:S(2)}, u32[]{:S(2)}) async-start(bf16[64,128,128]{2,1,0:T(8,128)(2,1)} %bitcast.58), calls=%async_computation.1 | async-start | bytes 4194304 | tf_op jit(solution)/shard_map/all_to_all | solution.py:36
  202.5 144.5 %copy-start.3 = (f32[8192]{0:T(1024)S(1)}, f32[8192]{0:T(1024)}, u32[]{:S(2)}) copy-start(f32[8192]{0:T(1024)} %param.12) | copy-start | bytes 98308
  377.0 36.8 %all-to-all-start.2 = ((bf16[128,64,128]{2,0,1:T(8,128)(2,1)}), bf16[128,64,128]{2,0,1:T(8,128)(2,1)S(1)}, u32[]{:S(2)}, u32[]{:S(2)}) async-start(bf16[128,64,128]{2,0,1:T(8,128)(2,1)} %bitcast.57), calls=%async_computation.2 | async-start | bytes 4194304 | tf_op jit(solution)/shard_map/all_to_all | solution.py:52
  384.8 293.4 %reduce-scatter.2.cloned.1.call-start = ((), (), s32[]{:S(2)}) async-start(), calls=%async_computation.6 | async-start | bytes 5242880 | tf_op jit(solution)/shard_map/reduce_scatter | solution.py:56
  421.8 256.4 %copy-start.1 = (bf16[8192,128]{1,0:T(8,128)(2,1)S(1)}, bf16[8192,128]{1,0:T(8,128)(2,1)}, u32[]{:S(2)}) copy-start(bf16[8192,128]{1,0:T(8,128)(2,1)} %param.9) | copy-start | bytes 6291460
Sparse Core Ops, SparseCore 0:
  9.2 159.0 all-gather.2
  170.1 176.8 all-gather.4
  598.4 79.6 reduce-scatter.1
where the time goes:
time: 685 us
  waiting for transfers between devices  245 us (36%)
  other arithmetic  225 us (33%)
  local copies, waits for them, and re-layouts  143 us (21%)
  matrix products  26.5 us (4%)
  blocking collectives  18.7 us (3%)
  between operations  13.2 us (2%)
  starting transfers between devices  12.6 us (2%)
    scatter-add x1, other arithmetic, scatter_rows(): target.at[flat_rows.reshape(-1)]  177 us
    gather x1, local copies, waits for them, and re-layouts, on_device(): picked = jnp.take(emb_table, flat_ids, axis=0, mode='fill', fill_value=0)  114 us
    all_to_all x1, waiting for transfers between devices, on_device(): lax.all_to_all(pooled_local, 'dp', split_axis=0, concat_axis=1, tiled=True)  86.5 us
    reduce_scatter x1, waiting for transfers between devices, on_device(): lax.psum_scatter(partial_value, 'fsdp', scatter_dimension=0, tiled=True)  79.8 us
    all_gather x1, waiting for transfers between devices, on_device(): lax.all_gather(cross_up, 'fsdp', axis=1, tiled=True)  49.2 us
    reduce_sum x1, other arithmetic, on_device(): jnp.sum(picked.astype(jnp.float32), axis=2).astype(jnp.bfloat16)  47.3 us
    all_to_all x1, waiting for transfers between devices, on_device(): lax.all_to_all(grad_pooled, 'dp', split_axis=1, concat_axis=0, tiled=True)  28.5 us
    all_to_all x1, blocking collectives, on_device(): lax.all_to_all(send_ids, 'dp', split_axis=1, concat_axis=0, tiled=True)  18.7 us
  transfers between devices with their start and end apart: 5, of which 4 were waited for; matrix products, arithmetic and copies ran while one was open for 26% of the time, Pallas kernels for 0%

commit v1 on v0

v1 whole, which is shorter than its diff:
```python
import functools

import jax
import jax.numpy as jnp
from jax import lax
from jax.experimental import pallas as pl
from jax.experimental.pallas import tpu as pltpu
from jax.sharding import PartitionSpec as P

SCATTER_ACCS = 8
ZERO_ROWS = 8


def pool_kernel(ids_ref, tab_ref, out_ref, acc_ref, *, blk, slots):
    i = pl.program_id(0)

    def body(j, carry):
        s = i * blk + j
        r = tab_ref[pl.ds(ids_ref[s * slots], 1), :]
        for h in range(1, slots):
            r = r + tab_ref[pl.ds(ids_ref[s * slots + h], 1), :]
        acc_ref[pl.ds(j, 1), :] = r
        return carry

    lax.fori_loop(0, blk, body, 0, unroll=8)
    out_ref[...] = acc_ref[...].astype(out_ref.dtype)


def pool_rows(ids_flat, table_f32, slots, blk=512):
    count = ids_flat.shape[0] // slots
    width = table_f32.shape[1]
    return pl.pallas_call(
        functools.partial(pool_kernel, blk=blk, slots=slots),
        grid_spec=pltpu.PrefetchScalarGridSpec(
            num_scalar_prefetch=1,
            grid=(count // blk,),
            in_specs=[pl.BlockSpec(table_f32.shape, lambda i, ids: (0, 0))],
            out_specs=pl.BlockSpec((blk, width), lambda i, ids: (i, 0)),
            scratch_shapes=[pltpu.VMEM((blk, width), jnp.float32)],
        ),
        out_shape=jax.ShapeDtypeStruct((count, width), jnp.bfloat16),
    )(ids_flat, table_f32)


def scatter_kernel(ids_ref, g_ref, out_ref, *accs, slots):
    nacc = len(accs)
    count = g_ref.shape[0]
    rows = out_ref.shape[0]
    for a in accs:
        a[...] = jnp.zeros(a.shape, jnp.float32)

    def body(s2, carry):
        for k in range(2):
            s = s2 * 2 + k
            row = g_ref[pl.ds(s, 1), :]
            for h in range(slots):
                a = accs[(k * slots + h) % nacc]
                idx = ids_ref[s * slots + h]
                a[pl.ds(idx, 1), :] = a[pl.ds(idx, 1), :] + row
        return carry

    lax.fori_loop(0, count // 2, body, 0, unroll=4)
    total = accs[0][pl.ds(0, rows), :]
    for a in accs[1:]:
        total = total + a[pl.ds(0, rows), :]
    out_ref[...] = total


def scatter_rows(ids_flat, g_f32, rows, slots):
    count, width = g_f32.shape
    return pl.pallas_call(
        functools.partial(scatter_kernel, slots=slots),
        grid_spec=pltpu.PrefetchScalarGridSpec(
            num_scalar_prefetch=1,
            grid=(1,),
            in_specs=[pl.BlockSpec((count, width), lambda i, ids: (0, 0))],
            out_specs=pl.BlockSpec((rows, width), lambda i, ids: (0, 0)),
            scratch_shapes=[
                pltpu.VMEM((rows + ZERO_ROWS, width), jnp.float32)
                for _ in range(SCATTER_ACCS)
            ],
        ),
        out_shape=jax.ShapeDtypeStruct((rows, width), jnp.float32),
        compiler_params=pltpu.CompilerParams(vmem_limit_bytes=62 * 1024 * 1024),
    )(ids_flat, g_f32)


def on_device(bag_ids, bag_counts, emb_table, cross_down, cross_up, cross_bias, cotangent):
    row_count, table_count, slot_count = bag_ids.shape
    vocab_rows, col_piece = emb_table.shape
    dp_size = lax.axis_size("dp")
    rank = cross_down.shape[1]
    half = rank // 2

    dp_idx = lax.axis_index("dp")
    core = dp_idx % 2
    down_mine = lax.dynamic_slice_in_dim(cross_down, core * half, half, 1)
    up_mine = lax.dynamic_slice_in_dim(cross_up, core * half, half, 0)
    down_mine = lax.all_gather(down_mine, "fsdp", axis=0, tiled=True)
    up_mine = lax.all_gather(up_mine, "fsdp", axis=1, tiled=True)
    partner = [(i, i ^ 1) for i in range(dp_size)]
    down_other = lax.ppermute(down_mine, "dp", partner)
    up_other = lax.ppermute(up_mine, "dp", partner)

    slot_iota = lax.broadcasted_iota(jnp.int32, bag_ids.shape, 2)
    live_ids = jnp.where(slot_iota < bag_counts[:, :, None], bag_ids, vocab_rows)
    send_ids = live_ids.reshape(row_count, table_count * slot_count)
    got_ids = lax.all_to_all(send_ids, "dp", split_axis=1, concat_axis=0, tiled=True)
    sample_count = got_ids.shape[0]
    ids_flat = got_ids.reshape(-1)

    table_f32 = jnp.concatenate(
        [emb_table.astype(jnp.float32), jnp.zeros((ZERO_ROWS, col_piece), jnp.float32)]
    )
    pooled_local = pool_rows(ids_flat, table_f32, slot_count)
    pooled = lax.all_to_all(pooled_local, "dp", split_axis=0, concat_axis=1, tiled=True)

    upstream = cotangent.astype(jnp.float32)
    grad_gate = (upstream * pooled.astype(jnp.float32)).astype(jnp.bfloat16)
    low_mine = jnp.dot(pooled, down_mine, preferred_element_type=jnp.float32).astype(jnp.bfloat16)
    low_other = jnp.dot(pooled, down_other, preferred_element_type=jnp.float32).astype(jnp.bfloat16)
    gate_value = (
        jnp.dot(low_mine, up_mine, preferred_element_type=jnp.float32)
        + jnp.dot(low_other, up_other, preferred_element_type=jnp.float32)
        + cross_bias
    )
    contract = (((1,), (1,)), ((), ()))
    grad_low_mine = lax.dot_general(
        grad_gate, up_mine, contract, preferred_element_type=jnp.float32
    ).astype(jnp.bfloat16)
    grad_low_other = lax.dot_general(
        grad_gate, up_other, contract, preferred_element_type=jnp.float32
    ).astype(jnp.bfloat16)
    back_term = lax.dot_general(
        grad_low_mine, down_mine, contract, preferred_element_type=jnp.float32
    ) + lax.dot_general(grad_low_other, down_other, contract, preferred_element_type=jnp.float32)
    grad_pooled = (upstream * (gate_value + 1.0) + back_term).astype(jnp.bfloat16)
    grad_local = lax.all_to_all(grad_pooled, "dp", split_axis=1, concat_axis=0, tiled=True)
    partial_value = scatter_rows(
        ids_flat, grad_local.astype(jnp.float32), vocab_rows, slot_count
    )
    return lax.psum_scatter(partial_value, "fsdp", scatter_dimension=0, tiled=True)


def solution(mesh):
    placed = (
        P(("dp", "fsdp"), None, None),
        P(("dp", "fsdp"), None),
        P(None, "dp"),
        P("fsdp", None),
        P(None, "fsdp"),
        P(),
        P(("dp", "fsdp"), None),
    )
    return jax.shard_map(
        on_device, mesh=mesh, in_specs=placed, out_specs=P("fsdp", "dp"), check_vma=False
    )
```

time: 685 us -> 405 us (0.59)
  other arithmetic: 225 us -> 5.35 us
  local copies, waits for them, and re-layouts: 143 us -> 15.1 us
  Pallas kernels: 0 us -> 84.7 us
  waiting for transfers between devices: 245 us -> 183 us
  blocking collectives: 18.7 us -> 46.4 us
  matrix products: 26.5 us -> 40.6 us
    scatter-add x1 -> x0, other arithmetic: 177 us -> none  [scatter_rows(): target.at[flat_rows.reshape(-1)]]
    gather x1 -> x0, local copies, waits for them, and re-layouts: 114 us -> none  [on_device(): picked = jnp.take(emb_table, flat_ids, axis=0, mode='fill', fill_value=0)]
    all_to_all x1, waiting for transfers between devices: 86.5 us -> 0.01 us  [on_device(): lax.all_to_all(pooled_local, 'dp', split_axis=0, concat_axis=1, tiled=True)]
    pallas_call x0 -> x2, Pallas kernels: none -> 84.7 us  [the longest x1 42.4 us: scatter_rows(): pl.pallas_call(functools.partial(scatter_kernel, slots=slots), grid_spec=...]
    all_gather x2, waiting for transfers between devices: 49.2 us -> 98.5 us  [the longest x1 98.4 us: on_device(): down_mine = lax.all_gather(down_mine, 'fsdp', axis=0, tiled=True)]
    reduce_sum x1 -> x0, other arithmetic: 47.3 us -> none  [on_device(): jnp.sum(picked.astype(jnp.float32), axis=2).astype(jnp.bfloat16)]
    all_to_all x1, blocking collectives: 18.7 us -> 46.4 us  [on_device(): lax.all_to_all(grad_pooled, 'dp', split_axis=1, concat_axis=0, tiled=True)]
    all_to_all x1, waiting for transfers between devices: 28.5 us -> 6.35 us  [on_device(): lax.all_to_all(send_ids, 'dp', split_axis=1, concat_axis=0, tiled=True)]
  transfers between devices with their start and end apart: 5 -> 7, of which waited for: 4 -> 3; matrix products, arithmetic and copies ran while one was open for 26% -> 8% of each run, Pallas kernels for 0% -> 10%
where the time goes in v1:
time: 405 us
  waiting for transfers between devices  183 us (45%)
  Pallas kernels  84.7 us (21%)
  blocking collectives  46.4 us (11%)
  matrix products  40.6 us (10%)
  starting transfers between devices  16.3 us (4%)
  local copies, waits for them, and re-layouts  15.1 us (4%)
  between operations  13.2 us (3%)
  other arithmetic  5.35 us (1%)
    all_gather x1, waiting for transfers between devices, on_device(): down_mine = lax.all_gather(down_mine, 'fsdp', axis=0, tiled=True)  98.4 us
    reduce_scatter x1, waiting for transfers between devices, on_device(): lax.psum_scatter(partial_value, 'fsdp', scatter_dimension=0, tiled=True)  78.2 us
    all_to_all x1, blocking collectives, on_device(): lax.all_to_all(grad_pooled, 'dp', split_axis=1, concat_axis=0, tiled=True)  46.4 us
    pallas_call x1, Pallas kernels, scatter_rows(): pl.pallas_call(functools.partial(scatter_kernel, slots=slots), grid_spec=...  42.4 us
    pallas_call x1, Pallas kernels, pool_rows(): pl.pallas_call(functools.partial(pool_kernel, blk=blk, slots=slots), grid...  42.4 us
    dot_general x1, matrix products, on_device(): lax.dot_general(grad_low_other, down_other, contract, preferred_element_t...  12.5 us
    dot_general x1, matrix products, on_device(): lax.dot_general(grad_low_mine, down_mine, contract, preferred_element_typ...  10.7 us
    all_to_all x1, starting transfers between devices, on_device(): lax.all_to_all(send_ids, 'dp', split_axis=1, concat_axis=0, tiled=True)  10.3 us
  transfers between devices with their start and end apart: 7, of which 3 were waited for; matrix products, arithmetic and copies ran while one was open for 8% of the time, Pallas kernels for 10%

profile of v1, /device:TPU:1, one launch (start us, length us, event | category | flops | bytes accessed | tf_op | source)
XLA Modules:
  0.0 404.8 jit_solution(8277894684144322277)
XLA Ops:
  6.5 0.0 copy-start.3
  6.5 0.0 copy-start.1
  6.5 0.0 copy-start
  6.5 0.0 all-gather.5.cloned.1.call-start
  6.5 2.5 constant_dynamic-slice_fusion
  9.0 0.0 all-gather.5.cloned.1.call-update
  9.0 0.0 all-gather.3.cloned.1.call-start
  9.1 2.3 constant_dynamic-slice_fusion.1
  11.4 0.0 all-gather.3.cloned.1.call-update
  11.4 0.0 copy-done.3
  11.4 0.0 copy-done.1
  11.5 0.7 fusion.29
  12.2 10.3 %all-to-all-start = ((s32[128,64,4]{0,2,1:T(4,128)}), s32[128,64,4]{0,2,1:T(4,128)S(1)}, u32[]{:S(2)}, u32[]{:S(2)}) async-start(s32[128,64,4]{0,2,1:T(4,128)} %fusion.29), calls=%async_computation | async-start | bytes 262144 | tf_op jit(solution)/shard_map/all_to_all | solution.py:108
  22.5 0.0 copy-done
  22.5 2.2 pad_convert_fusion.tab_ref
  24.7 6.3 %all-to-all-done = s32[128,64,4]{0,2,1:T(4,128)S(1)} async-done(((s32[128,64,4]{0,2,1:T(4,128)}), s32[128,64,4]{0,2,1:T(4,128)S(1)}, u32[]{:S(2)}, u32[]{:S(2)}) %all-to-all-start) | async-done | bytes 131104 | tf_op jit(solution)/shard_map/all_to_all | solution.py:108
  31.0 2.7 copy.10
  33.7 5.5 %reshape.19.ids_ref = s32[32768]{0:T(1024)} reshape(s32[64,128,4]{2,1,0:T(8,128)} %copy.10) | data formatting | bytes 262144 | tf_op jit(solution)/shard_map/reshape | solution.py:110
  39.2 42.4 %shard_map.73 = bf16[8192,128]{1,0:T(8,128)(2,1)} custom-call(s32[32768]{0:T(1024)} %reshape.19.ids_ref, f32[8200,128]{1,0:T(8,128)} %pad_convert_fusion.tab_ref), custom_call_target="tpu_custom_call" | custom-call | tf_op jit(solution)/shard_map/pallas_call | solution.py:32
  81.5 4.5 %all-to-all-start.1 = ((bf16[64,128,128]{2,1,0:T(8,128)(2,1)}), bf16[64,128,128]{2,1,0:T(8,128)(2,1)S(1)}, u32[]{:S(2)}, u32[]{:S(2)}) async-start(bf16[64,128,128]{2,1,0:T(8,128)(2,1)} %bitcast.56), calls=%async_computation.1 | async-start | bytes 4194304 | tf_op jit(solution)/shard_map/all_to_all | solution.py:116
  86.1 0.0 reduce-scatter.2.cloned.1.call-start
  86.1 0.0 all-gather.5.cloned.1.call-done
  86.1 0.7 collective-permute-start.1
  86.8 98.4 %all-gather.3.cloned.1.call-done = bf16[8192,256]{1,0:T(8,128)(2,1)} async-done(((bf16[2048,256]{1,0:T(8,128)(2,1)}), bf16[8192,256]{1,0:T(8,128)(2,1)}) %all-gather.3.cloned.1.call-update) | async-done | bytes 4194320 | tf_op jit(solution)/shard_map/all_gather | solution.py:99
  185.2 0.7 collective-permute-start
  185.9 0.0 all-to-all-done.1
  185.9 7.8 %fusion.21 = f32[128,8192]{1,0:T(8,128)} fusion(bf16[256,8192]{1,0:T(8,128)(2,1)} %all-gather.5.cloned.1.call-done, bf16[8192,256]{1,0:T(8,128)(2,1)} %all-gather.3.cloned.1.call-done, bf16[64,128,128]{2,1,0:T(8,128)(2,1)S(1)} %all-to-all-done.1), kind=kOutput, calls=%fused_computation.23 | convolution fusion | flops 1073774592 | bytes 14680064 | tf_op jit(solution)/shard_map/dot_general | solution.py:123
  193.7 0.0 copy-start.2
  193.7 10.7 %fusion.19 = f32[128,8192]{1,0:T(8,128)} fusion(bf16[8192,256]{1,0:T(8,128)(2,1)} %all-gather.3.cloned.1.call-done, bf16[256,8192]{1,0:T(8,128)(2,1)} %all-gather.5.cloned.1.call-done, bf16[128,8192]{1,0:T(8,128)(2,1)} %param.13, bf16[64,128,128]{2,1,0:T(8,128)(2,1)S(1)} %all-to-all-done.1), kind=kOutput, calls=%fused_computation.22 | convolution fusion | flops 1077968896 | bytes 16777216 | tf_op jit(solution)/shard_map/dot_general | solution.py:134
  204.5 0.0 collective-permute-done.1
  204.5 0.0 collective-permute-done
  204.5 0.0 copy-done.2
  204.5 9.6 %fusion.3 = f32[128,8192]{1,0:T(8,128)} fusion(f32[128,8192]{1,0:T(8,128)} %fusion.21, bf16[256,8192]{1,0:T(8,128)(2,1)} %collective-permute-done.1, bf16[128,8192]{1,0:T(8,128)(2,1)} %param.13, f32[8192]{0:T(1024)S(1)} %copy-done.2, bf16[8192,256]{1,0:T(8,128)(2,1)} %collective-permute-done, bf16[64,128,128]{2,1,0:T(8,128)(2,1)S(1)} %all-to-all-done.1), kind=kOutput, calls=%fused_computation.5 | convolution fusion | flops 1079017472 | bytes 21004288 | tf_op jit(solution)/shard_map/dot_general | solution.py:124
  214.1 12.5 %fusion.10 = bf16[16,64,8,128]{3,2,1,0:T(8,128)(2,1)} fusion(f32[128,8192]{1,0:T(8,128)} %fusion.3, f32[128,8192]{1,0:T(8,128)} %fusion.19, bf16[8192,256]{1,0:T(8,128)(2,1)} %collective-permute-done, bf16[256,8192]{1,0:T(8,128)(2,1)} %collective-permute-done.1, bf16[128,8192]{1,0:T(8,128)(2,1)} %param.13, bf16[64,128,128]{2,1,0:T(8,128)(2,1)S(1)} %all-to-all-done.1), kind=kOutput, calls=%fused_computation.15 | convolution fusion | flops 1081114624 | bytes 23068672 | tf_op jit(solution)/shard_map/dot_general | solution.py:136
  226.6 2.2 copy.37
  228.7 46.4 %all_to_all.45 = bf16[128,64,128]{2,0,1:T(8,128)(2,1)S(1)} all-to-all(bf16[128,64,128]{2,0,1:T(8,128)(2,1)S(1)} %bitcast.55), channel_id=1, replica_groups=mesh['dp'=64,'fsdp'=4] {'dp'}, dimensions={1} | all-to-all | bytes 4194304 | tf_op jit(solution)/shard_map/all_to_all | solution.py:138
  275.1 2.5 convert_element_type.44
  277.6 42.4 %shard_map.74 = f32[8192,128]{1,0:T(8,128)} custom-call(s32[32768]{0:T(1024)} %reshape.19.ids_ref, f32[8192,128]{1,0:T(8,128)} %bitcast.54), custom_call_target="tpu_custom_call" | custom-call | tf_op jit(solution)/shard_map/pallas_call | solution.py:71
  320.0 0.0 reduce-scatter.2.cloned.1.call-update
  320.0 78.2 %reduce-scatter.2.cloned.1.call-done = f32[2048,128]{1,0:T(8,128)} async-done(((f32[8192,128]{1,0:T(8,128)}), f32[2048,128]{1,0:T(8,128)}) %reduce-scatter.2.cloned.1.call-update) | async-done | bytes 1048592 | tf_op jit(solution)/shard_map/reduce_scatter | solution.py:142
Async XLA Ops:
  6.5 4.9 %copy-start.3 = (s32[128,64]{0,1:T(8,128)S(1)}, s32[128,64]{0,1:T(8,128)}, u32[]{:S(2)}) copy-start(s32[128,64]{0,1:T(8,128)} %param.8) | copy-start | bytes 98308
  6.5 4.9 %copy-start.1 = (s32[128,64,4]{0,2,1:T(4,128)S(1)}, s32[128,64,4]{0,2,1:T(4,128)}, u32[]{:S(2)}) copy-start(s32[128,64,4]{0,2,1:T(4,128)} %param.7) | copy-start | bytes 393220
  6.5 16.0 %copy-start = (bf16[8192,128]{1,0:T(8,128)(2,1)S(1)}, bf16[8192,128]{1,0:T(8,128)(2,1)}, u32[]{:S(2)}) copy-start(bf16[8192,128]{1,0:T(8,128)(2,1)} %param.9) | copy-start | bytes 6291460
  6.5 79.6 %all-gather.5.cloned.1.call-start = ((), (), s32[]{:S(2)}) async-start(), calls=%async_computation.5 | async-start | bytes 5242880 | tf_op jit(solution)/shard_map/all_gather | solution.py:100
  9.0 176.2 %all-gather.3.cloned.1.call-start = ((), (), s32[]{:S(2)}) async-start(), calls=%async_computation.4 | async-start | bytes 5242880 | tf_op jit(solution)/shard_map/all_gather | solution.py:99
  12.2 18.9 %all-to-all-start = ((s32[128,64,4]{0,2,1:T(4,128)}), s32[128,64,4]{0,2,1:T(4,128)S(1)}, u32[]{:S(2)}, u32[]{:S(2)}) async-start(s32[128,64,4]{0,2,1:T(4,128)} %fusion.29), calls=%async_computation | async-start | bytes 262144 | tf_op jit(solution)/shard_map/all_to_all | solution.py:108
  81.5 104.4 %all-to-all-start.1 = ((bf16[64,128,128]{2,1,0:T(8,128)(2,1)}), bf16[64,128,128]{2,1,0:T(8,128)(2,1)S(1)}, u32[]{:S(2)}, u32[]{:S(2)}) async-start(bf16[64,128,128]{2,1,0:T(8,128)(2,1)} %bitcast.56), calls=%async_computation.1 | async-start | bytes 4194304 | tf_op jit(solution)/shard_map/all_to_all | solution.py:116
  86.1 312.2 %reduce-scatter.2.cloned.1.call-start = ((), (), s32[]{:S(2)}) async-start(), calls=%async_computation.6 | async-start | bytes 5242880 | tf_op jit(solution)/shard_map/reduce_scatter | solution.py:142
  86.1 118.3 %collective-permute-start.1 = (bf16[256,8192]{1,0:T(8,128)(2,1)}, bf16[256,8192]{1,0:T(8,128)(2,1)}, u32[]{:S(2)}, u32[]{:S(2)}) collective-permute-start(bf16[256,8192]{1,0:T(8,128)(2,1)} %all-gather.5.cloned.1.call-done), channel_id=1, source_target_pairs={{0,4},{4,0},{8,12},{12,8},{16,20},{20,16},{24,28},{28,24},{32,36},... | collective-permute-start | bytes 12582920 | tf_op jit(solution)/shard_map/ppermute | solution.py:103
  185.2 19.2 %collective-permute-start = (bf16[8192,256]{1,0:T(8,128)(2,1)}, bf16[8192,256]{1,0:T(8,128)(2,1)}, u32[]{:S(2)}, u32[]{:S(2)}) collective-permute-start(bf16[8192,256]{1,0:T(8,128)(2,1)} %all-gather.3.cloned.1.call-done), channel_id=1, source_target_pairs={{0,4},{4,0},{8,12},{12,8},{16,20},{20,16},{24,28},{28,24},{32,36},... | collective-permute-start | bytes 12582920 | tf_op jit(solution)/shard_map/ppermute | solution.py:102
  193.7 10.8 %copy-start.2 = (f32[8192]{0:T(1024)S(1)}, f32[8192]{0:T(1024)}, u32[]{:S(2)}) copy-start(f32[8192]{0:T(1024)} %param.12) | copy-start | bytes 98308
Sparse Core Ops, SparseCore 0:
  9.2 76.0 all-gather.4
  87.1 98.1 all-gather.2
  320.1 78.0 reduce-scatter.1

commit v2 on v1

--- a/solution.py
+++ b/solution.py
@@ -63,7 +63,7 @@
     total = accs[0][pl.ds(0, rows), :]
     for a in accs[1:]:
         total = total + a[pl.ds(0, rows), :]
-    out_ref[...] = total
+    out_ref[...] = total.astype(out_ref.dtype)
 
 
 def scatter_rows(ids_flat, g_f32, rows, slots):
@@ -80,7 +80,7 @@
                 for _ in range(SCATTER_ACCS)
             ],
         ),
-        out_shape=jax.ShapeDtypeStruct((rows, width), jnp.float32),
+        out_shape=jax.ShapeDtypeStruct((rows, width), jnp.bfloat16),
         compiler_params=pltpu.CompilerParams(vmem_limit_bytes=62 * 1024 * 1024),
     )(ids_flat, g_f32)
 
@@ -139,7 +139,10 @@
     partial_value = scatter_rows(
         ids_flat, grad_local.astype(jnp.float32), vocab_rows, slot_count
     )
-    return lax.psum_scatter(partial_value, "fsdp", scatter_dimension=0, tiled=True)
+    summed = lax.psum_scatter(
+        partial_value, "fsdp", scatter_dimension=0, tiled=True
+    )
+    return summed.astype(jnp.float32)
 
 
 def solution(mesh):

time: 405 us -> 373 us (0.921)
  waiting for transfers between devices: 183 us -> 149 us
    reduce_scatter x1, waiting for transfers between devices: 78.2 us -> 44.3 us  [on_device(): lax.psum_scatter(partial_value, 'fsdp', scatter_dimension=0, tiled=True)]
  transfers between devices with their start and end apart: 7 -> 7, of which waited for: 3 -> 3; matrix products, arithmetic and copies ran while one was open for 8% -> 9% of each run, Pallas kernels for 10% -> 11%
where the time goes in v2:
time: 373 us; the launch traced here: 372 us
  waiting for transfers between devices  149 us (40%)
  Pallas kernels  84.1 us (23%)
  blocking collectives  46.4 us (12%)
  matrix products  40.6 us (11%)
  starting transfers between devices  16.3 us (4%)
  local copies, waits for them, and re-layouts  15.1 us (4%)
  between operations  13.2 us (4%)
  other arithmetic  7.51 us (2%)
    all_gather x1, waiting for transfers between devices, on_device(): down_mine = lax.all_gather(down_mine, 'fsdp', axis=0, tiled=True)  98.4 us
    all_to_all x1, blocking collectives, on_device(): lax.all_to_all(grad_pooled, 'dp', split_axis=1, concat_axis=0, tiled=True)  46.4 us
    reduce_scatter x1, waiting for transfers between devices, on_device(): lax.psum_scatter(partial_value, 'fsdp', scatter_dimension=0, tiled=True)  44.3 us
    pallas_call x1, Pallas kernels, pool_rows(): pl.pallas_call(functools.partial(pool_kernel, blk=blk, slots=slots), grid...  42.4 us
    pallas_call x1, Pallas kernels, scatter_rows(): pl.pallas_call(functools.partial(scatter_kernel, slots=slots), grid_spec=...  41.7 us
    dot_general x1, matrix products, on_device(): lax.dot_general(grad_low_other, down_other, contract, preferred_element_t...  12.5 us
    dot_general x1, matrix products, on_device(): lax.dot_general(grad_low_mine, down_mine, contract, preferred_element_typ...  10.7 us
    all_to_all x1, starting transfers between devices, on_device(): lax.all_to_all(send_ids, 'dp', split_axis=1, concat_axis=0, tiled=True)  10.3 us
  transfers between devices with their start and end apart: 7, of which 3 were waited for; matrix products, arithmetic and copies ran while one was open for 9% of the time, Pallas kernels for 11%

profile of v2, /device:TPU:1, one launch (start us, length us, event | category | flops | bytes accessed | tf_op | source)
XLA Modules:
  0.0 372.3 jit_solution(853828780579049500)
XLA Ops:
  6.5 0.0 copy-start.3
  6.5 0.0 copy-start.1
  6.5 0.0 copy-start
  6.5 0.0 all-gather.5.cloned.1.call-start
  6.5 2.5 constant_dynamic-slice_fusion
  9.0 0.0 all-gather.5.cloned.1.call-update
  9.0 0.0 all-gather.3.cloned.1.call-start
  9.1 2.3 constant_dynamic-slice_fusion.1
  11.4 0.0 all-gather.3.cloned.1.call-update
  11.4 0.0 copy-done.3
  11.4 0.0 copy-done.1
  11.5 0.7 fusion.29
  12.2 10.3 %all-to-all-start = ((s32[128,64,4]{0,2,1:T(4,128)}), s32[128,64,4]{0,2,1:T(4,128)S(1)}, u32[]{:S(2)}, u32[]{:S(2)}) async-start(s32[128,64,4]{0,2,1:T(4,128)} %fusion.29), calls=%async_computation | async-start | bytes 262144 | tf_op jit(solution)/shard_map/all_to_all | solution.py:108
  22.5 0.0 copy-done
  22.5 2.2 pad_convert_fusion.tab_ref
  24.7 6.3 %all-to-all-done = s32[128,64,4]{0,2,1:T(4,128)S(1)} async-done(((s32[128,64,4]{0,2,1:T(4,128)}), s32[128,64,4]{0,2,1:T(4,128)S(1)}, u32[]{:S(2)}, u32[]{:S(2)}) %all-to-all-start) | async-done | bytes 131104 | tf_op jit(solution)/shard_map/all_to_all | solution.py:108
  31.0 2.7 copy.10
  33.7 5.5 %reshape.19.ids_ref = s32[32768]{0:T(1024)} reshape(s32[64,128,4]{2,1,0:T(8,128)} %copy.10) | data formatting | bytes 262144 | tf_op jit(solution)/shard_map/reshape | solution.py:110
  39.2 42.4 %shard_map.73 = bf16[8192,128]{1,0:T(8,128)(2,1)} custom-call(s32[32768]{0:T(1024)} %reshape.19.ids_ref, f32[8200,128]{1,0:T(8,128)} %pad_convert_fusion.tab_ref), custom_call_target="tpu_custom_call" | custom-call | tf_op jit(solution)/shard_map/pallas_call | solution.py:32
  81.5 4.5 %all-to-all-start.1 = ((bf16[64,128,128]{2,1,0:T(8,128)(2,1)}), bf16[64,128,128]{2,1,0:T(8,128)(2,1)S(1)}, u32[]{:S(2)}, u32[]{:S(2)}) async-start(bf16[64,128,128]{2,1,0:T(8,128)(2,1)} %bitcast.56), calls=%async_computation.1 | async-start | bytes 4194304 | tf_op jit(solution)/shard_map/all_to_all | solution.py:116
  86.1 0.0 reduce-scatter.2.cloned.1.call-start
  86.1 0.0 all-gather.5.cloned.1.call-done
  86.1 0.7 collective-permute-start.1
  86.8 98.4 %all-gather.3.cloned.1.call-done = bf16[8192,256]{1,0:T(8,128)(2,1)} async-done(((bf16[2048,256]{1,0:T(8,128)(2,1)}), bf16[8192,256]{1,0:T(8,128)(2,1)}) %all-gather.3.cloned.1.call-update) | async-done | bytes 4194320 | tf_op jit(solution)/shard_map/all_gather | solution.py:99
  185.2 0.7 collective-permute-start
  185.9 0.0 all-to-all-done.1
  185.9 7.8 %fusion.21 = f32[128,8192]{1,0:T(8,128)} fusion(bf16[256,8192]{1,0:T(8,128)(2,1)} %all-gather.5.cloned.1.call-done, bf16[8192,256]{1,0:T(8,128)(2,1)} %all-gather.3.cloned.1.call-done, bf16[64,128,128]{2,1,0:T(8,128)(2,1)S(1)} %all-to-all-done.1), kind=kOutput, calls=%fused_computation.23 | convolution fusion | flops 1073774592 | bytes 14680064 | tf_op jit(solution)/shard_map/dot_general | solution.py:123
  193.7 0.0 copy-start.2
  193.7 10.7 %fusion.19 = f32[128,8192]{1,0:T(8,128)} fusion(bf16[8192,256]{1,0:T(8,128)(2,1)} %all-gather.3.cloned.1.call-done, bf16[256,8192]{1,0:T(8,128)(2,1)} %all-gather.5.cloned.1.call-done, bf16[128,8192]{1,0:T(8,128)(2,1)} %param.13, bf16[64,128,128]{2,1,0:T(8,128)(2,1)S(1)} %all-to-all-done.1), kind=kOutput, calls=%fused_computation.22 | convolution fusion | flops 1077968896 | bytes 16777216 | tf_op jit(solution)/shard_map/dot_general | solution.py:134
  204.5 0.0 collective-permute-done.1
  204.5 0.0 collective-permute-done
  204.5 0.0 copy-done.2
  204.5 9.6 %fusion.3 = f32[128,8192]{1,0:T(8,128)} fusion(f32[128,8192]{1,0:T(8,128)} %fusion.21, bf16[256,8192]{1,0:T(8,128)(2,1)} %collective-permute-done.1, bf16[128,8192]{1,0:T(8,128)(2,1)} %param.13, f32[8192]{0:T(1024)S(1)} %copy-done.2, bf16[8192,256]{1,0:T(8,128)(2,1)} %collective-permute-done, bf16[64,128,128]{2,1,0:T(8,128)(2,1)S(1)} %all-to-all-done.1), kind=kOutput, calls=%fused_computation.5 | convolution fusion | flops 1079017472 | bytes 21004288 | tf_op jit(solution)/shard_map/dot_general | solution.py:124
  214.1 12.5 %fusion.10 = bf16[16,64,8,128]{3,2,1,0:T(8,128)(2,1)} fusion(f32[128,8192]{1,0:T(8,128)} %fusion.3, f32[128,8192]{1,0:T(8,128)} %fusion.19, bf16[8192,256]{1,0:T(8,128)(2,1)} %collective-permute-done, bf16[256,8192]{1,0:T(8,128)(2,1)} %collective-permute-done.1, bf16[128,8192]{1,0:T(8,128)(2,1)} %param.13, bf16[64,128,128]{2,1,0:T(8,128)(2,1)S(1)} %all-to-all-done.1), kind=kOutput, calls=%fused_computation.15 | convolution fusion | flops 1081114624 | bytes 23068672 | tf_op jit(solution)/shard_map/dot_general | solution.py:136
  226.6 2.2 copy.37
  228.7 46.4 %all_to_all.45 = bf16[128,64,128]{2,0,1:T(8,128)(2,1)S(1)} all-to-all(bf16[128,64,128]{2,0,1:T(8,128)(2,1)S(1)} %bitcast.55), channel_id=1, replica_groups=mesh['dp'=64,'fsdp'=4] {'dp'}, dimensions={1} | all-to-all | bytes 4194304 | tf_op jit(solution)/shard_map/all_to_all | solution.py:138
  275.1 2.6 convert_element_type.48
  277.7 41.7 %shard_map.74 = bf16[8192,128]{1,0:T(8,128)(2,1)} custom-call(s32[32768]{0:T(1024)} %reshape.19.ids_ref, f32[8192,128]{1,0:T(8,128)} %bitcast.54), custom_call_target="tpu_custom_call" | custom-call | tf_op jit(solution)/shard_map/pallas_call | solution.py:71
  319.4 0.0 reduce-scatter.2.cloned.1.call-update
  319.4 44.3 %reduce-scatter.2.cloned.1.call-done = bf16[2048,128]{1,0:T(8,128)(2,1)} async-done(((bf16[8192,128]{1,0:T(8,128)(2,1)}), bf16[2048,128]{1,0:T(8,128)(2,1)}) %reduce-scatter.2.cloned.1.call-update) | async-done | bytes 524304 | tf_op jit(solution)/shard_map/reduce_scatter | solution.py:142
  363.7 2.1 convert_element_type.46
Async XLA Ops:
  6.5 4.9 %copy-start.3 = (s32[128,64]{0,1:T(8,128)S(1)}, s32[128,64]{0,1:T(8,128)}, u32[]{:S(2)}) copy-start(s32[128,64]{0,1:T(8,128)} %param.8) | copy-start | bytes 98308
  6.5 4.9 %copy-start.1 = (s32[128,64,4]{0,2,1:T(4,128)S(1)}, s32[128,64,4]{0,2,1:T(4,128)}, u32[]{:S(2)}) copy-start(s32[128,64,4]{0,2,1:T(4,128)} %param.7) | copy-start | bytes 393220
  6.5 16.0 %copy-start = (bf16[8192,128]{1,0:T(8,128)(2,1)S(1)}, bf16[8192,128]{1,0:T(8,128)(2,1)}, u32[]{:S(2)}) copy-start(bf16[8192,128]{1,0:T(8,128)(2,1)} %param.9) | copy-start | bytes 6291460
  6.5 79.6 %all-gather.5.cloned.1.call-start = ((), (), s32[]{:S(2)}) async-start(), calls=%async_computation.5 | async-start | bytes 5242880 | tf_op jit(solution)/shard_map/all_gather | solution.py:100
  9.0 176.2 %all-gather.3.cloned.1.call-start = ((), (), s32[]{:S(2)}) async-start(), calls=%async_computation.4 | async-start | bytes 5242880 | tf_op jit(solution)/shard_map/all_gather | solution.py:99
  12.2 18.9 %all-to-all-start = ((s32[128,64,4]{0,2,1:T(4,128)}), s32[128,64,4]{0,2,1:T(4,128)S(1)}, u32[]{:S(2)}, u32[]{:S(2)}) async-start(s32[128,64,4]{0,2,1:T(4,128)} %fusion.29), calls=%async_computation | async-start | bytes 262144 | tf_op jit(solution)/shard_map/all_to_all | solution.py:108
  81.5 104.4 %all-to-all-start.1 = ((bf16[64,128,128]{2,1,0:T(8,128)(2,1)}), bf16[64,128,128]{2,1,0:T(8,128)(2,1)S(1)}, u32[]{:S(2)}, u32[]{:S(2)}) async-start(bf16[64,128,128]{2,1,0:T(8,128)(2,1)} %bitcast.56), calls=%async_computation.1 | async-start | bytes 4194304 | tf_op jit(solution)/shard_map/all_to_all | solution.py:116
  86.1 277.7 %reduce-scatter.2.cloned.1.call-start = ((), (), s32[]{:S(2)}) async-start(), calls=%async_computation.6 | async-start | bytes 2621440 | tf_op jit(solution)/shard_map/reduce_scatter | solution.py:142
  86.1 118.3 %collective-permute-start.1 = (bf16[256,8192]{1,0:T(8,128)(2,1)}, bf16[256,8192]{1,0:T(8,128)(2,1)}, u32[]{:S(2)}, u32[]{:S(2)}) collective-permute-start(bf16[256,8192]{1,0:T(8,128)(2,1)} %all-gather.5.cloned.1.call-done), channel_id=1, source_target_pairs={{0,4},{4,0},{8,12},{12,8},{16,20},{20,16},{24,28},{28,24},{32,36},... | collective-permute-start | bytes 12582920 | tf_op jit(solution)/shard_map/ppermute | solution.py:103
  185.2 19.2 %collective-permute-start = (bf16[8192,256]{1,0:T(8,128)(2,1)}, bf16[8192,256]{1,0:T(8,128)(2,1)}, u32[]{:S(2)}, u32[]{:S(2)}) collective-permute-start(bf16[8192,256]{1,0:T(8,128)(2,1)} %all-gather.3.cloned.1.call-done), channel_id=1, source_target_pairs={{0,4},{4,0},{8,12},{12,8},{16,20},{20,16},{24,28},{28,24},{32,36},... | collective-permute-start | bytes 12582920 | tf_op jit(solution)/shard_map/ppermute | solution.py:102
  193.7 10.8 %copy-start.2 = (f32[8192]{0:T(1024)S(1)}, f32[8192]{0:T(1024)}, u32[]{:S(2)}) copy-start(f32[8192]{0:T(1024)} %param.12) | copy-start | bytes 98308
Sparse Core Ops, SparseCore 0:
  9.2 76.0 all-gather.4
  87.1 98.1 all-gather.2
  319.6 44.0 reduce-scatter.1

commit v3 on v2

--- a/solution.py
+++ b/solution.py
@@ -119,6 +119,7 @@
     grad_gate = (upstream * pooled.astype(jnp.float32)).astype(jnp.bfloat16)
     low_mine = jnp.dot(pooled, down_mine, preferred_element_type=jnp.float32).astype(jnp.bfloat16)
     low_other = jnp.dot(pooled, down_other, preferred_element_type=jnp.float32).astype(jnp.bfloat16)
+    low_mine, low_other = lax.optimization_barrier((low_mine, low_other))
     gate_value = (
         jnp.dot(low_mine, up_mine, preferred_element_type=jnp.float32)
         + jnp.dot(low_other, up_other, preferred_element_type=jnp.float32)
@@ -131,6 +132,7 @@
     grad_low_other = lax.dot_general(
         grad_gate, up_other, contract, preferred_element_type=jnp.float32
     ).astype(jnp.bfloat16)
+    grad_low_mine, grad_low_other = lax.optimization_barrier((grad_low_mine, grad_low_other))
     back_term = lax.dot_general(
         grad_low_mine, down_mine, contract, preferred_element_type=jnp.float32
     ) + lax.dot_general(grad_low_other, down_other, contract, preferred_element_type=jnp.float32)

time: 373 us -> 356 us (0.954)
  matrix products: 40.6 us -> 24.5 us
    all_gather x1, waiting for transfers between devices: 98.4 us -> 3.65 us  [on_device(): down_mine = lax.all_gather(down_mine, 'fsdp', axis=0, tiled=True)]
    all_gather x1, waiting for transfers between devices: 0.02 us -> 93.3 us  [on_device(): up_mine = lax.all_gather(up_mine, 'fsdp', axis=1, tiled=True)]
    dot_general x0 -> x4, matrix products: none -> 14.8 us  [the longest x1 4.36 us: on_device(): lax.dot_general(grad_gate, up_other, contract, preferred_element_type=jnp...]
    dot_general x1, matrix products: 10.7 us -> 1.48 us  [on_device(): lax.dot_general(grad_low_mine, down_mine, contract, preferred_element_typ...]
    dot_general x1, matrix products: 12.5 us -> 3.79 us  [on_device(): lax.dot_general(grad_low_other, down_other, contract, preferred_element_t...]
    dot_general x1, matrix products: 7.82 us -> 0.73 us  [on_device(): jnp.dot(low_mine, up_mine, preferred_element_type=jnp.float32)]
    dot_general x1, matrix products: 9.61 us -> 3.67 us  [on_device(): jnp.dot(low_other, up_other, preferred_element_type=jnp.float32)]
  transfers between devices with their start and end apart: 7 -> 7, of which waited for: 3 -> 4; matrix products, arithmetic and copies ran while one was open for 9% -> 7% of each run, Pallas kernels for 11% -> 12%
where the time goes in v3:
time: 356 us
  waiting for transfers between devices  148 us (42%)
  Pallas kernels  84.1 us (24%)
  blocking collectives  46.4 us (13%)
  matrix products  24.5 us (7%)
  starting transfers between devices  17.2 us (5%)
  local copies, waits for them, and re-layouts  15.3 us (4%)
  between operations  13.3 us (4%)
  other arithmetic  7.61 us (2%)
    all_gather x1, waiting for transfers between devices, on_device(): up_mine = lax.all_gather(up_mine, 'fsdp', axis=1, tiled=True)  93.3 us
    all_to_all x1, blocking collectives, on_device(): lax.all_to_all(grad_pooled, 'dp', split_axis=1, concat_axis=0, tiled=True)  46.4 us
    reduce_scatter x1, waiting for transfers between devices, on_device(): lax.psum_scatter(partial_value, 'fsdp', scatter_dimension=0, tiled=True)  44.3 us
    pallas_call x1, Pallas kernels, pool_rows(): pl.pallas_call(functools.partial(pool_kernel, blk=blk, slots=slots), grid...  42.4 us
    pallas_call x1, Pallas kernels, scatter_rows(): pl.pallas_call(functools.partial(scatter_kernel, slots=slots), grid_spec=...  41.7 us
    all_to_all x1, starting transfers between devices, on_device(): lax.all_to_all(send_ids, 'dp', split_axis=1, concat_axis=0, tiled=True)  10.3 us
  transfers between devices with their start and end apart: 7, of which 4 were waited for; matrix products, arithmetic and copies ran while one was open for 7% of the time, Pallas kernels for 12%

profile of v3, /device:TPU:1, one launch (start us, length us, event | category | flops | bytes accessed | tf_op | source)
XLA Modules:
  0.0 355.8 jit_solution(6541972431318574123)
XLA Ops:
  6.5 0.0 copy-start.4
  6.5 0.0 copy-start.6
  6.5 0.0 all-gather.3.cloned.1.call-start
  6.5 2.4 constant_dynamic-slice_fusion.1
  9.0 0.0 all-gather.3.cloned.1.call-update
  9.0 0.0 all-gather.5.cloned.1.call-start
  9.0 2.4 constant_dynamic-slice_fusion
  11.4 0.0 all-gather.5.cloned.1.call-update
  11.5 0.0 copy-done.4
  11.5 0.0 copy-done.6
  11.5 0.7 fusion.21
  12.2 10.3 %all-to-all-start = ((s32[128,64,4]{0,2,1:T(4,128)}), s32[128,64,4]{0,2,1:T(4,128)S(1)}, u32[]{:S(2)}, u32[]{:S(2)}) async-start(s32[128,64,4]{0,2,1:T(4,128)} %fusion.21), calls=%async_computation | async-start | bytes 262144 | tf_op jit(solution)/shard_map/all_to_all | solution.py:108
  22.5 0.0 copy-done.3
  22.5 2.3 pad_convert_fusion.tab_ref
  24.8 6.2 %all-to-all-done = s32[128,64,4]{0,2,1:T(4,128)S(1)} async-done(((s32[128,64,4]{0,2,1:T(4,128)}), s32[128,64,4]{0,2,1:T(4,128)S(1)}, u32[]{:S(2)}, u32[]{:S(2)}) %all-to-all-start) | async-done | bytes 131104 | tf_op jit(solution)/shard_map/all_to_all | solution.py:108
  31.1 2.6 copy.10
  33.7 5.5 %reshape.19.ids_ref = s32[32768]{0:T(1024)} reshape(s32[64,128,4]{2,1,0:T(8,128)} %copy.10) | data formatting | bytes 262144 | tf_op jit(solution)/shard_map/reshape | solution.py:110
  39.2 42.4 %shard_map.73 = bf16[8192,128]{1,0:T(8,128)(2,1)} custom-call(s32[32768]{0:T(1024)} %reshape.19.ids_ref, f32[8200,128]{1,0:T(8,128)} %pad_convert_fusion.tab_ref), custom_call_target="tpu_custom_call" | custom-call | tf_op jit(solution)/shard_map/pallas_call | solution.py:32
  81.5 5.3 %all-to-all-start.1 = ((bf16[64,128,128]{2,1,0:T(8,128)(2,1)}), bf16[64,128,128]{2,1,0:T(8,128)(2,1)}, u32[]{:S(2)}, u32[]{:S(2)}) async-start(bf16[64,128,128]{2,1,0:T(8,128)(2,1)} %bitcast.50), calls=%async_computation.1 | async-start | bytes 4194304 | tf_op jit(solution)/shard_map/all_to_all | solution.py:116
  86.9 0.0 copy-start
  86.9 0.0 reduce-scatter.2.cloned.1.call-start
  86.9 3.6 %all-gather.3.cloned.1.call-done = bf16[8192,256]{1,0:T(8,128)(2,1)} async-done(((bf16[2048,256]{1,0:T(8,128)(2,1)}), bf16[8192,256]{1,0:T(8,128)(2,1)}) %all-gather.3.cloned.1.call-update) | async-done | bytes 4194320 | tf_op jit(solution)/shard_map/all_gather | solution.py:99
  90.6 0.7 collective-permute-start
  91.3 93.3 %all-gather.5.cloned.1.call-done = bf16[256,8192]{1,0:T(8,128)(2,1)} async-done(((bf16[256,2048]{1,0:T(8,128)(2,1)}), bf16[256,8192]{1,0:T(8,128)(2,1)}) %all-gather.5.cloned.1.call-update) | async-done | bytes 4194320 | tf_op jit(solution)/shard_map/all_gather | solution.py:100
  184.6 0.7 collective-permute-start.1
  185.3 0.0 all-to-all-done.1
  185.3 3.7 %fusion.13 = bf16[128,256]{1,0:T(8,128)(2,1)S(1)} fusion(bf16[8192,256]{1,0:T(8,128)(2,1)} %all-gather.3.cloned.1.call-done, bf16[64,128,128]{2,1,0:T(8,128)(2,1)} %all-to-all-done.1), kind=kOutput, calls=%fused_computation.18 | convolution fusion | flops 536903680 | bytes 6356992 | tf_op jit(solution)/shard_map/dot_general | solution.py:120
  189.0 0.0 copy-done
  189.0 0.3 copy-done.1
  189.3 3.2 convolution_convert_fusion.1
  192.6 0.0 collective-permute-done
  192.6 3.5 fusion.16
  196.1 0.0 collective-permute-done.1
  196.1 4.4 %convolution_convert_fusion = bf16[128,256]{1,0:T(8,128)(2,1)S(1)} fusion(bf16[256,8192]{1,0:T(8,128)(2,1)} %collective-permute-done.1, bf16[128,8192]{1,0:T(8,128)(2,1)S(1)} %copy-done, bf16[64,128,128]{2,1,0:T(8,128)(2,1)} %all-to-all-done.1), kind=kOutput, calls=%fused_computation.20 | convolution fusion | flops 541097984 | bytes 8454144 | tf_op jit(solution)/shard_map/dot_general | solution.py:132
  200.5 0.0 copy-start.2
  200.5 0.7 fusion.22
  201.2 1.4 copy-done.2
  202.7 1.5 fusion.23
  204.2 0.0 copy-done.5
  204.2 3.7 %fusion.3 = f32[128,8192]{1,0:T(8,128)S(1)} fusion(f32[128,8192]{1,0:T(8,128)S(1)} %fusion.22, bf16[128,256]{1,0:T(8,128)(2,1)S(1)} %fusion.16, bf16[256,8192]{1,0:T(8,128)(2,1)} %collective-permute-done.1, bf16[128,8192]{1,0:T(8,128)(2,1)S(1)} %copy-done, f32[8192]{0:T(1024)S(1)} %copy-done.5), kind=kOutput, calls=%fused_computation.5 | convolution fusion | flops 542113792 | bytes 14778368 | tf_op jit(solution)/shard_map/dot_general | solution.py:125
  207.9 3.8 %fusion.10 = bf16[16,64,8,128]{3,2,1,0:T(8,128)(2,1)S(1)} fusion(f32[128,8192]{1,0:T(8,128)S(1)} %fusion.3, f32[128,8192]{1,0:T(8,128)S(1)} %fusion.23, bf16[128,256]{1,0:T(8,128)(2,1)S(1)} %convolution_convert_fusion, bf16[8192,256]{1,0:T(8,128)(2,1)} %collective-permute-done), kind=kOutput, calls=%fused_computation.15 | convolution fusion | flops 540016640 | bytes 14745600 | tf_op jit(solution)/shard_map/dot_general | solution.py:138
  211.7 0.6 copy.31
  212.3 46.4 %all_to_all.45 = bf16[128,64,128]{2,0,1:T(8,128)(2,1)S(1)} all-to-all(bf16[128,64,128]{2,0,1:T(8,128)(2,1)S(1)} %bitcast.49), channel_id=1, replica_groups=mesh['dp'=64,'fsdp'=4] {'dp'}, dimensions={1} | all-to-all | bytes 4194304 | tf_op jit(solution)/shard_map/all_to_all | solution.py:140
  258.6 2.5 convert_element_type.48
  261.2 41.7 %shard_map.74 = bf16[8192,128]{1,0:T(8,128)(2,1)} custom-call(s32[32768]{0:T(1024)} %reshape.19.ids_ref, f32[8192,128]{1,0:T(8,128)} %bitcast.48), custom_call_target="tpu_custom_call" | custom-call | tf_op jit(solution)/shard_map/pallas_call | solution.py:71
  302.9 0.0 reduce-scatter.2.cloned.1.call-update
  303.0 44.3 %reduce-scatter.2.cloned.1.call-done = bf16[2048,128]{1,0:T(8,128)(2,1)} async-done(((bf16[8192,128]{1,0:T(8,128)(2,1)}), bf16[2048,128]{1,0:T(8,128)(2,1)}) %reduce-scatter.2.cloned.1.call-update) | async-done | bytes 524304 | tf_op jit(solution)/shard_map/reduce_scatter | solution.py:144
  347.2 2.1 convert_element_type.46
  (3 shorter events, 0.0 us)
Async XLA Ops:
  6.5 4.9 %copy-start.4 = (s32[128,64,4]{0,2,1:T(4,128)S(1)}, s32[128,64,4]{0,2,1:T(4,128)}, u32[]{:S(2)}) copy-start(s32[128,64,4]{0,2,1:T(4,128)} %param.7) | copy-start | bytes 393220
  6.5 4.9 %copy-start.6 = (s32[128,64]{0,1:T(8,128)S(1)}, s32[128,64]{0,1:T(8,128)}, u32[]{:S(2)}) copy-start(s32[128,64]{0,1:T(8,128)} %param.8) | copy-start | bytes 98308
  6.5 16.0 %copy-start.3 = (bf16[8192,128]{1,0:T(8,128)(2,1)S(1)}, bf16[8192,128]{1,0:T(8,128)(2,1)}, u32[]{:S(2)}) copy-start(bf16[8192,128]{1,0:T(8,128)(2,1)} %param.9) | copy-start | bytes 6291460
  6.5 84.0 %all-gather.3.cloned.1.call-start = ((), (), s32[]{:S(2)}) async-start(), calls=%async_computation.4 | async-start | bytes 5242880 | tf_op jit(solution)/shard_map/all_gather | solution.py:99
  9.0 175.6 %all-gather.5.cloned.1.call-start = ((), (), s32[]{:S(2)}) async-start(), calls=%async_computation.5 | async-start | bytes 5242880 | tf_op jit(solution)/shard_map/all_gather | solution.py:100
  12.2 18.9 %all-to-all-start = ((s32[128,64,4]{0,2,1:T(4,128)}), s32[128,64,4]{0,2,1:T(4,128)S(1)}, u32[]{:S(2)}, u32[]{:S(2)}) async-start(s32[128,64,4]{0,2,1:T(4,128)} %fusion.21), calls=%async_computation | async-start | bytes 262144 | tf_op jit(solution)/shard_map/all_to_all | solution.py:108
  81.5 103.8 %all-to-all-start.1 = ((bf16[64,128,128]{2,1,0:T(8,128)(2,1)}), bf16[64,128,128]{2,1,0:T(8,128)(2,1)}, u32[]{:S(2)}, u32[]{:S(2)}) async-start(bf16[64,128,128]{2,1,0:T(8,128)(2,1)} %bitcast.50), calls=%async_computation.1 | async-start | bytes 4194304 | tf_op jit(solution)/shard_map/all_to_all | solution.py:116
  86.9 102.1 %copy-start = (bf16[128,8192]{1,0:T(8,128)(2,1)S(1)}, bf16[128,8192]{1,0:T(8,128)(2,1)}, u32[]{:S(2)}) copy-start(bf16[128,8192]{1,0:T(8,128)(2,1)} %param.13) | copy-start | bytes 6291460
  86.9 260.3 %reduce-scatter.2.cloned.1.call-start = ((), (), s32[]{:S(2)}) async-start(), calls=%async_computation.6 | async-start | bytes 2621440 | tf_op jit(solution)/shard_map/reduce_scatter | solution.py:144
  90.6 102.0 %collective-permute-start = (bf16[8192,256]{1,0:T(8,128)(2,1)}, bf16[8192,256]{1,0:T(8,128)(2,1)}, u32[]{:S(2)}, u32[]{:S(2)}) collective-permute-start(bf16[8192,256]{1,0:T(8,128)(2,1)} %all-gather.3.cloned.1.call-done), channel_id=1, source_target_pairs={{0,4},{4,0},{8,12},{12,8},{16,20},{20,16},{24,28},{28,24},{32,36},... | collective-permute-start | bytes 12582920 | tf_op jit(solution)/shard_map/ppermute | solution.py:102
  184.6 11.6 %collective-permute-start.1 = (bf16[256,8192]{1,0:T(8,128)(2,1)}, bf16[256,8192]{1,0:T(8,128)(2,1)}, u32[]{:S(2)}, u32[]{:S(2)}) collective-permute-start(bf16[256,8192]{1,0:T(8,128)(2,1)} %all-gather.5.cloned.1.call-done), channel_id=1, source_target_pairs={{0,4},{4,0},{8,12},{12,8},{16,20},{20,16},{24,28},{28,24},{32,36},... | collective-permute-start | bytes 12582920 | tf_op jit(solution)/shard_map/ppermute | solution.py:103
  185.3 4.0 %copy-start.1 = (bf16[256,8192]{1,0:T(8,128)(2,1)S(1)}, bf16[256,8192]{1,0:T(8,128)(2,1)}, u32[]{:S(2)}) copy-start(bf16[256,8192]{1,0:T(8,128)(2,1)} %all-gather.5.cloned.1.call-done) | copy-start | bytes 12582916
  200.5 2.2 copy-start.2
  202.7 1.5 copy-start.5
Sparse Core Ops, SparseCore 0:
  9.2 81.3 all-gather.2
  92.4 92.1 all-gather.4
  303.1 44.0 reduce-scatter.1

commit v4 on v2

--- a/solution.py
+++ b/solution.py
@@ -42,12 +42,18 @@
     )(ids_flat, table_f32)
 
 
-def scatter_kernel(ids_ref, g_ref, out_ref, *accs, slots):
+def scatter_kernel(ids_ref, g_ref, *rest, slots, has_init):
+    if has_init:
+        init_ref, out_ref, *accs = rest
+    else:
+        out_ref, *accs = rest
     nacc = len(accs)
     count = g_ref.shape[0]
     rows = out_ref.shape[0]
     for a in accs:
         a[...] = jnp.zeros(a.shape, jnp.float32)
+    if has_init:
+        accs[0][pl.ds(0, rows), :] = init_ref[...]
 
     def body(s2, carry):
         for k in range(2):
@@ -66,23 +72,29 @@
     out_ref[...] = total.astype(out_ref.dtype)
 
 
-def scatter_rows(ids_flat, g_f32, rows, slots):
+def scatter_rows(ids_flat, g_f32, rows, slots, init=None, out_dtype=jnp.bfloat16):
     count, width = g_f32.shape
+    whole = lambda i, ids: (0, 0)
+    in_specs = [pl.BlockSpec((count, width), whole)]
+    operands = [ids_flat, g_f32]
+    if init is not None:
+        in_specs.append(pl.BlockSpec((rows, width), whole))
+        operands.append(init)
     return pl.pallas_call(
-        functools.partial(scatter_kernel, slots=slots),
+        functools.partial(scatter_kernel, slots=slots, has_init=init is not None),
         grid_spec=pltpu.PrefetchScalarGridSpec(
             num_scalar_prefetch=1,
             grid=(1,),
-            in_specs=[pl.BlockSpec((count, width), lambda i, ids: (0, 0))],
+            in_specs=in_specs,
             out_specs=pl.BlockSpec((rows, width), lambda i, ids: (0, 0)),
             scratch_shapes=[
                 pltpu.VMEM((rows + ZERO_ROWS, width), jnp.float32)
                 for _ in range(SCATTER_ACCS)
             ],
         ),
-        out_shape=jax.ShapeDtypeStruct((rows, width), jnp.bfloat16),
+        out_shape=jax.ShapeDtypeStruct((rows, width), out_dtype),
         compiler_params=pltpu.CompilerParams(vmem_limit_bytes=62 * 1024 * 1024),
-    )(ids_flat, g_f32)
+    )(*operands)
 
 
 def on_device(bag_ids, bag_counts, emb_table, cross_down, cross_up, cross_bias, cotangent):
@@ -115,30 +127,44 @@
     pooled_local = pool_rows(ids_flat, table_f32, slot_count)
     pooled = lax.all_to_all(pooled_local, "dp", split_axis=0, concat_axis=1, tiled=True)
 
-    upstream = cotangent.astype(jnp.float32)
-    grad_gate = (upstream * pooled.astype(jnp.float32)).astype(jnp.bfloat16)
-    low_mine = jnp.dot(pooled, down_mine, preferred_element_type=jnp.float32).astype(jnp.bfloat16)
-    low_other = jnp.dot(pooled, down_other, preferred_element_type=jnp.float32).astype(jnp.bfloat16)
-    gate_value = (
-        jnp.dot(low_mine, up_mine, preferred_element_type=jnp.float32)
-        + jnp.dot(low_other, up_other, preferred_element_type=jnp.float32)
-        + cross_bias
-    )
-    contract = (((1,), (1,)), ((), ()))
-    grad_low_mine = lax.dot_general(
-        grad_gate, up_mine, contract, preferred_element_type=jnp.float32
-    ).astype(jnp.bfloat16)
-    grad_low_other = lax.dot_general(
-        grad_gate, up_other, contract, preferred_element_type=jnp.float32
-    ).astype(jnp.bfloat16)
-    back_term = lax.dot_general(
-        grad_low_mine, down_mine, contract, preferred_element_type=jnp.float32
-    ) + lax.dot_general(grad_low_other, down_other, contract, preferred_element_type=jnp.float32)
-    grad_pooled = (upstream * (gate_value + 1.0) + back_term).astype(jnp.bfloat16)
-    grad_local = lax.all_to_all(grad_pooled, "dp", split_axis=1, concat_axis=0, tiled=True)
-    partial_value = scatter_rows(
-        ids_flat, grad_local.astype(jnp.float32), vocab_rows, slot_count
-    )
+    def backward_rows(pooled_part, cot_part):
+        upstream = cot_part.astype(jnp.float32)
+        grad_gate = (upstream * pooled_part.astype(jnp.float32)).astype(jnp.bfloat16)
+        low_mine = jnp.dot(pooled_part, down_mine, preferred_element_type=jnp.float32)
+        low_other = jnp.dot(pooled_part, down_other, preferred_element_type=jnp.float32)
+        low_mine, low_other = lax.optimization_barrier(
+            (low_mine.astype(jnp.bfloat16), low_other.astype(jnp.bfloat16))
+        )
+        gate_value = (
+            jnp.dot(low_mine, up_mine, preferred_element_type=jnp.float32)
+            + jnp.dot(low_other, up_other, preferred_element_type=jnp.float32)
+            + cross_bias
+        )
+        contract = (((1,), (1,)), ((), ()))
+        grad_low_mine = lax.dot_general(
+            grad_gate, up_mine, contract, preferred_element_type=jnp.float32
+        ).astype(jnp.bfloat16)
+        grad_low_other = lax.dot_general(
+            grad_gate, up_other, contract, preferred_element_type=jnp.float32
+        ).astype(jnp.bfloat16)
+        grad_low_mine, grad_low_other = lax.optimization_barrier((grad_low_mine, grad_low_other))
+        back_term = lax.dot_general(
+            grad_low_mine, down_mine, contract, preferred_element_type=jnp.float32
+        ) + lax.dot_general(grad_low_other, down_other, contract, preferred_element_type=jnp.float32)
+        grad_pooled = (upstream * (gate_value + 1.0) + back_term).astype(jnp.bfloat16)
+        return lax.all_to_all(grad_pooled, "dp", split_axis=1, concat_axis=0, tiled=True)
+
+    split = row_count // 2
+    ids_by_source = got_ids.reshape(dp_size, row_count, slot_count)
+    partial_value = None
+    for lo in (0, split):
+        grad_local = backward_rows(pooled[lo:lo + split], cotangent[lo:lo + split])
+        ids_part = ids_by_source[:, lo:lo + split].reshape(-1)
+        last = lo == split
+        partial_value = scatter_rows(
+            ids_part, grad_local.astype(jnp.float32), vocab_rows, slot_count,
+            init=partial_value, out_dtype=jnp.bfloat16 if last else jnp.float32,
+        )
     summed = lax.psum_scatter(
         partial_value, "fsdp", scatter_dimension=0, tiled=True
     )

time: 373 us -> 376 us (level)
  blocking collectives: 46.4 us -> 0 us
  starting transfers between devices: 16.3 us -> 40.8 us
  local copies, waits for them, and re-layouts: 15.1 us -> 26.5 us
  Pallas kernels: 84.1 us -> 92.9 us
  waiting for transfers between devices: 149 us -> 155 us
  matrix products: 40.6 us -> 36.2 us
    all_gather x1, waiting for transfers between devices: 98.4 us -> 0.02 us  [on_device(): down_mine = lax.all_gather(down_mine, 'fsdp', axis=0, tiled=True)]
    all_gather x1, waiting for transfers between devices: 0.02 us -> 98.4 us  [on_device(): up_mine = lax.all_gather(up_mine, 'fsdp', axis=1, tiled=True)]
    all_to_all x1 -> x0, blocking collectives: 46.4 us -> none  [on_device(): lax.all_to_all(grad_pooled, 'dp', split_axis=1, concat_axis=0, tiled=True)]
    all_to_all x0 -> x2, starting transfers between devices: none -> 24.2 us  [backward_rows(): lax.all_to_all(grad_pooled, 'dp', split_axis=1, concat_axis=0, tiled=True)]
    pallas_call x1 -> x2, Pallas kernels: 41.7 us -> 50.5 us  [scatter_rows(): pl.pallas_call(functools.partial(scatter_kernel, slots=slots, has_init=in...]
    unnamed x8 -> x19, local copies, waits for them, and re-layouts: 0.01 us -> 5.02 us
    reshape x0 -> x2, local copies, waits for them, and re-layouts: none -> 4.54 us  [on_device(): ids_part = ids_by_source[:, lo:lo + split].reshape(-1)]
    dot_general x4 -> x16, matrix products: 40.6 us -> 36.2 us  [the longest x2 7.33 us: backward_rows(): lax.dot_general(grad_gate, up_other, contract, preferred_element_type=jnp...]
  transfers between devices with their start and end apart: 7 -> 9, of which waited for: 3 -> 4; matrix products, arithmetic and copies ran while one was open for 9% -> 13% of each run, Pallas kernels for 11% -> 18%
where the time goes in v4:
time: 376 us; the launch traced here: 375 us
  waiting for transfers between devices  155 us (41%)
  Pallas kernels  92.9 us (25%)
  starting transfers between devices  40.8 us (11%)
  matrix products  36.2 us (10%)
  local copies, waits for them, and re-layouts  26.5 us (7%)
  between operations  13.3 us (4%)
  other arithmetic  9.54 us (3%)
    all_gather x1, waiting for transfers between devices, on_device(): up_mine = lax.all_gather(up_mine, 'fsdp', axis=1, tiled=True)  98.4 us
    pallas_call x2, Pallas kernels, scatter_rows(): pl.pallas_call(functools.partial(scatter_kernel, slots=slots, has_init=in...  50.5 us
    reduce_scatter x1, waiting for transfers between devices, on_device(): lax.psum_scatter(partial_value, 'fsdp', scatter_dimension=0, tiled=True)  48.3 us
    pallas_call x1, Pallas kernels, pool_rows(): pl.pallas_call(functools.partial(pool_kernel, blk=blk, slots=slots), grid...  42.4 us
    all_to_all x2, starting transfers between devices, backward_rows(): lax.all_to_all(grad_pooled, 'dp', split_axis=1, concat_axis=0, tiled=True)  24.2 us
    all_to_all x1, starting transfers between devices, on_device(): lax.all_to_all(send_ids, 'dp', split_axis=1, concat_axis=0, tiled=True)  10.3 us
  transfers between devices with their start and end apart: 9, of which 4 were waited for; matrix products, arithmetic and copies ran while one was open for 13% of the time, Pallas kernels for 18%

profile of v4, /device:TPU:1, one launch (start us, length us, event | category | flops | bytes accessed | tf_op | source)
XLA Modules:
  0.0 374.6 jit_solution(16093907485057999858)
XLA Ops:
  6.5 2.3 constant_dynamic-slice_fusion.1
  8.9 2.6 constant_dynamic-slice_fusion
  11.5 0.7 fusion.26
  12.2 10.3 %all-to-all-start = ((s32[128,64,4]{0,2,1:T(4,128)}), s32[128,64,4]{0,2,1:T(4,128)S(1)}, u32[]{:S(2)}, u32[]{:S(2)}) async-start(s32[128,64,4]{0,2,1:T(4,128)} %fusion.26), calls=%async_computation | async-start | bytes 262144 | tf_op jit(solution)/shard_map/all_to_all | solution.py:120
  22.5 2.3 pad_convert_fusion.tab_ref
  24.8 6.2 %all-to-all-done = s32[128,64,4]{0,2,1:T(4,128)S(1)} async-done(((s32[128,64,4]{0,2,1:T(4,128)}), s32[128,64,4]{0,2,1:T(4,128)S(1)}, u32[]{:S(2)}, u32[]{:S(2)}) %all-to-all-start) | async-done | bytes 131104 | tf_op jit(solution)/shard_map/all_to_all | solution.py:120
  31.1 2.6 copy.13
  33.7 5.5 %reshape.35.ids_ref = s32[32768]{0:T(1024)} reshape(s32[64,128,4]{2,1,0:T(8,128)} %copy.13) | data formatting | bytes 262144 | tf_op jit(solution)/shard_map/reshape | solution.py:122
  39.2 42.4 %shard_map.73 = bf16[8192,128]{1,0:T(8,128)(2,1)} custom-call(s32[32768]{0:T(1024)} %reshape.35.ids_ref, f32[8200,128]{1,0:T(8,128)} %pad_convert_fusion.tab_ref), custom_call_target="tpu_custom_call" | custom-call | tf_op jit(solution)/shard_map/pallas_call | solution.py:32
  81.5 4.5 %all-to-all-start.1 = ((bf16[64,128,128]{2,1,0:T(8,128)(2,1)}), bf16[64,128,128]{2,1,0:T(8,128)(2,1)S(1)}, u32[]{:S(2)}, u32[]{:S(2)}) async-start(bf16[64,128,128]{2,1,0:T(8,128)(2,1)} %bitcast.65), calls=%async_computation.1 | async-start | bytes 4194304 | tf_op jit(solution)/shard_map/all_to_all | solution.py:128
  86.1 0.7 collective-permute-start
  86.8 98.4 %all-gather.5.cloned.1.call-done = bf16[256,8192]{1,0:T(8,128)(2,1)} async-done(((bf16[256,2048]{1,0:T(8,128)(2,1)}), bf16[256,8192]{1,0:T(8,128)(2,1)}) %all-gather.5.cloned.1.call-update) | async-done | bytes 4194320 | tf_op jit(solution)/shard_map/all_gather | solution.py:112
  185.2 0.7 collective-permute-start.1
  186.1 2.0 copy-done
  188.1 0.9 convolution_convert_fusion.7
  188.9 0.8 convolution_convert_fusion.3
  189.8 1.5 copy-done.2
  191.3 1.4 convolution_convert_fusion.5
  192.7 1.4 convolution_convert_fusion.1
  194.1 3.0 convolution_convert_fusion.6
  197.1 3.0 convolution_convert_fusion.2
  200.2 3.6 convolution_convert_fusion
  203.8 0.8 fusion.30
  204.6 1.4 fusion.31
  206.0 3.3 fusion.3
  209.3 3.6 fusion.12
  213.0 1.3 copy.47
  214.2 17.7 %all-to-all-start.3 = ((bf16[64,64,128]{2,0,1:T(8,128)(2,1)}), bf16[64,64,128]{2,0,1:T(8,128)(2,1)}, u32[]{:S(2)}, u32[]{:S(2)}) async-start(bf16[64,64,128]{2,0,1:T(8,128)(2,1)} %bitcast.67), calls=%async_computation.3 | async-start | bytes 2097152 | tf_op jit(solution)/shard_map/all_to_all | solution.py:155
  232.0 3.7 convolution_convert_fusion.4
  235.7 0.8 fusion.28
  236.6 1.3 copy-done.1
  237.9 1.4 fusion.29
  239.3 3.3 fusion.7
  242.6 3.6 fusion.13
  246.2 1.3 copy.48
  247.5 2.3 all-to-all-done.3
  249.8 6.5 %all-to-all-start.2 = ((bf16[64,64,128]{2,0,1:T(8,128)(2,1)}), bf16[64,64,128]{2,0,1:T(8,128)(2,1)S(1)}, u32[]{:S(2)}, u32[]{:S(2)}) async-start(bf16[64,64,128]{2,0,1:T(8,128)(2,1)} %bitcast.62), calls=%async_computation.2 | async-start | bytes 2097152 | tf_op jit(solution)/shard_map/all_to_all | solution.py:155
  256.3 0.3 reduce-scatter.2.cloned.1.call-start
  256.8 0.7 copy.12
  257.5 2.3 reshape.34.ids_ref
  259.7 0.7 copy.16
  260.4 2.3 reshape.36.ids_ref
  262.7 2.8 convert_element_type.92
  265.5 25.1 %shard_map.74.rest_0_ = f32[8192,128]{1,0:T(8,128)} custom-call(s32[16384]{0:T(1024)} %reshape.36.ids_ref, f32[4096,128]{1,0:T(8,128)} %bitcast.63), custom_call_target="tpu_custom_call" | custom-call | tf_op jit(solution)/shard_map/pallas_call | solution.py:83
  290.6 1.6 convert_element_type.91
  292.3 25.4 %shard_map.75 = bf16[8192,128]{1,0:T(8,128)(2,1)} custom-call(s32[16384]{0:T(1024)} %reshape.34.ids_ref, f32[4096,128]{1,0:T(8,128)} %bitcast.66, f32[8192,128]{1,0:T(8,128)} %shard_map.74.rest_0_), custom_call_target="tpu_custom_call" | custom-call | tf_op jit(solution)/shard_map/pallas_call | solution.py:83
  317.7 48.3 %reduce-scatter.2.cloned.1.call-done = bf16[2048,128]{1,0:T(8,128)(2,1)} async-done(((bf16[8192,128]{1,0:T(8,128)(2,1)}), bf16[2048,128]{1,0:T(8,128)(2,1)}) %reduce-scatter.2.cloned.1.call-update) | async-done | bytes 524304 | tf_op jit(solution)/shard_map/reduce_scatter | solution.py:168
  366.0 2.1 convert_element_type.88
  (27 shorter events, 0.5 us)
Async XLA Ops:
  6.5 79.6 %all-gather.3.cloned.1.call-start = ((), (), s32[]{:S(2)}) async-start(), calls=%async_computation.5 | async-start | bytes 5242880 | tf_op jit(solution)/shard_map/all_gather | solution.py:111
  8.8 2.7 copy-start.7
  8.8 2.7 copy-start.8
  8.8 13.7 %copy-start.5 = (bf16[8192,128]{1,0:T(8,128)(2,1)S(1)}, bf16[8192,128]{1,0:T(8,128)(2,1)}, u32[]{:S(2)}) copy-start(bf16[8192,128]{1,0:T(8,128)(2,1)} %param.9) | copy-start | bytes 6291460
  8.8 176.3 %all-gather.5.cloned.1.call-start = ((), (), s32[]{:S(2)}) async-start(), calls=%async_computation.6 | async-start | bytes 5242880 | tf_op jit(solution)/shard_map/all_gather | solution.py:112
  12.2 18.9 %all-to-all-start = ((s32[128,64,4]{0,2,1:T(4,128)}), s32[128,64,4]{0,2,1:T(4,128)S(1)}, u32[]{:S(2)}, u32[]{:S(2)}) async-start(s32[128,64,4]{0,2,1:T(4,128)} %fusion.26), calls=%async_computation | async-start | bytes 262144 | tf_op jit(solution)/shard_map/all_to_all | solution.py:120
  81.5 104.3 %all-to-all-start.1 = ((bf16[64,128,128]{2,1,0:T(8,128)(2,1)}), bf16[64,128,128]{2,1,0:T(8,128)(2,1)S(1)}, u32[]{:S(2)}, u32[]{:S(2)}) async-start(bf16[64,128,128]{2,1,0:T(8,128)(2,1)} %bitcast.65), calls=%async_computation.1 | async-start | bytes 4194304 | tf_op jit(solution)/shard_map/all_to_all | solution.py:128
  86.1 108.0 %collective-permute-start = (bf16[8192,256]{1,0:T(8,128)(2,1)}, bf16[8192,256]{1,0:T(8,128)(2,1)}, u32[]{:S(2)}, u32[]{:S(2)}) collective-permute-start(bf16[8192,256]{1,0:T(8,128)(2,1)} %all-gather.3.cloned.1.call-done), channel_id=1, source_target_pairs={{0,4},{4,0},{8,12},{12,8},{16,20},{20,16},{24,28},{28,24},{32,36},... | collective-permute-start | bytes 12582920 | tf_op jit(solution)/shard_map/ppermute | solution.py:114
  185.2 15.0 %collective-permute-start.1 = (bf16[256,8192]{1,0:T(8,128)(2,1)}, bf16[256,8192]{1,0:T(8,128)(2,1)}, u32[]{:S(2)}, u32[]{:S(2)}) collective-permute-start(bf16[256,8192]{1,0:T(8,128)(2,1)} %all-gather.5.cloned.1.call-done), channel_id=1, source_target_pairs={{0,4},{4,0},{8,12},{12,8},{16,20},{20,16},{24,28},{28,24},{32,36},... | collective-permute-start | bytes 12582920 | tf_op jit(solution)/shard_map/ppermute | solution.py:115
  185.9 2.2 copy-start
  188.1 1.7 copy-start.4
  188.9 2.3 copy-start.2
  204.6 1.4 copy-start.6
  214.2 35.6 %all-to-all-start.3 = ((bf16[64,64,128]{2,0,1:T(8,128)(2,1)}), bf16[64,64,128]{2,0,1:T(8,128)(2,1)}, u32[]{:S(2)}, u32[]{:S(2)}) async-start(bf16[64,64,128]{2,0,1:T(8,128)(2,1)} %bitcast.67), calls=%async_computation.3 | async-start | bytes 2097152 | tf_op jit(solution)/shard_map/all_to_all | solution.py:155
  232.0 3.7 copy-start.3
  235.7 2.2 copy-start.1
  249.8 40.8 %all-to-all-start.2 = ((bf16[64,64,128]{2,0,1:T(8,128)(2,1)}), bf16[64,64,128]{2,0,1:T(8,128)(2,1)S(1)}, u32[]{:S(2)}, u32[]{:S(2)}) async-start(bf16[64,64,128]{2,0,1:T(8,128)(2,1)} %bitcast.62), calls=%async_computation.2 | async-start | bytes 2097152 | tf_op jit(solution)/shard_map/all_to_all | solution.py:155
  256.3 109.6 %reduce-scatter.2.cloned.1.call-start = ((), (), s32[]{:S(2)}) async-start(), calls=%async_computation.7 | async-start | bytes 2621440 | tf_op jit(solution)/shard_map/reduce_scatter | solution.py:168
Sparse Core Ops, SparseCore 0:
  9.2 76.0 all-gather.2
  87.1 98.0 all-gather.4
  317.8 48.0 reduce-scatter.1

commit v5 on v3

--- a/solution.py
+++ b/solution.py
@@ -92,15 +92,51 @@
     rank = cross_down.shape[1]
     half = rank // 2
 
+    fsdp_size = lax.axis_size("fsdp")
     dp_idx = lax.axis_index("dp")
+    f_idx = lax.axis_index("fsdp")
     core = dp_idx % 2
-    down_mine = lax.dynamic_slice_in_dim(cross_down, core * half, half, 1)
-    up_mine = lax.dynamic_slice_in_dim(cross_up, core * half, half, 0)
-    down_mine = lax.all_gather(down_mine, "fsdp", axis=0, tiled=True)
-    up_mine = lax.all_gather(up_mine, "fsdp", axis=1, tiled=True)
-    partner = [(i, i ^ 1) for i in range(dp_size)]
-    down_other = lax.ppermute(down_mine, "dp", partner)
-    up_other = lax.ppermute(up_mine, "dp", partner)
+    z_lo = (dp_idx // 8) % 2
+    shard_rows = cross_down.shape[0]
+    down_piece = lax.dynamic_slice_in_dim(cross_down, core * half, half, 1)
+    up_piece = lax.dynamic_slice_in_dim(cross_up, core * half, half, 0)
+    piece = jnp.concatenate([down_piece, up_piece.T], axis=1)
+
+    def device_of(dp, f):
+        return dp * fsdp_size + f
+
+    def z_step(dp, f, step):
+        lo = (dp // 8) % 2
+        z = (2 * f + lo + step) % (2 * fsdp_size)
+        return dp + (z % 2 - lo) * 8, z // 2
+
+    ring_perm, pair_perm = [], []
+    for dp in range(dp_size):
+        for f in range(fsdp_size):
+            lo = (dp // 8) % 2
+            ring_perm.append((device_of(dp, f), device_of(*z_step(dp, f, 1 if lo else -1))))
+            pair_perm.append((device_of(dp, f), device_of(dp ^ 8, f)))
+    core_perm = [(device_of(dp, f), device_of(dp ^ 1, f))
+                 for dp in range(dp_size) for f in range(fsdp_size)]
+    both = ("dp", "fsdp")
+    got_a = lax.ppermute(piece, both, ring_perm)
+    got_b = lax.ppermute(got_a, both, pair_perm)
+    got_c = lax.ppermute(got_b, both, ring_perm)
+    step_a = jnp.where(z_lo == 0, -1, 1)
+    shards = [
+        (piece, f_idx),
+        (got_a, (f_idx + step_a) % fsdp_size),
+        (got_b, (f_idx - step_a) % fsdp_size),
+        (got_c, (f_idx + 2) % fsdp_size),
+    ]
+    mine = jnp.zeros((shard_rows * fsdp_size, 2 * half), piece.dtype)
+    other = jnp.zeros((shard_rows * fsdp_size, 2 * half), piece.dtype)
+    for part, where in shards:
+        mine = lax.dynamic_update_slice_in_dim(mine, part, where * shard_rows, 0)
+        swapped = lax.ppermute(part, both, core_perm)
+        other = lax.dynamic_update_slice_in_dim(other, swapped, where * shard_rows, 0)
+    down_mine, up_t_mine = mine[:, :half], mine[:, half:]
+    down_other, up_t_other = other[:, :half], other[:, half:]
 
     slot_iota = lax.broadcasted_iota(jnp.int32, bag_ids.shape, 2)
     live_ids = jnp.where(slot_iota < bag_counts[:, :, None], bag_ids, vocab_rows)
@@ -120,18 +156,18 @@
     low_mine = jnp.dot(pooled, down_mine, preferred_element_type=jnp.float32).astype(jnp.bfloat16)
     low_other = jnp.dot(pooled, down_other, preferred_element_type=jnp.float32).astype(jnp.bfloat16)
     low_mine, low_other = lax.optimization_barrier((low_mine, low_other))
+    contract = (((1,), (1,)), ((), ()))
     gate_value = (
-        jnp.dot(low_mine, up_mine, preferred_element_type=jnp.float32)
-        + jnp.dot(low_other, up_other, preferred_element_type=jnp.float32)
+        lax.dot_general(low_mine, up_t_mine, contract, preferred_element_type=jnp.float32)
+        + lax.dot_general(low_other, up_t_other, contract, preferred_element_type=jnp.float32)
         + cross_bias
     )
-    contract = (((1,), (1,)), ((), ()))
-    grad_low_mine = lax.dot_general(
-        grad_gate, up_mine, contract, preferred_element_type=jnp.float32
-    ).astype(jnp.bfloat16)
-    grad_low_other = lax.dot_general(
-        grad_gate, up_other, contract, preferred_element_type=jnp.float32
-    ).astype(jnp.bfloat16)
+    grad_low_mine = jnp.dot(grad_gate, up_t_mine, preferred_element_type=jnp.float32).astype(
+        jnp.bfloat16
+    )
+    grad_low_other = jnp.dot(grad_gate, up_t_other, preferred_element_type=jnp.float32).astype(
+        jnp.bfloat16
+    )
     grad_low_mine, grad_low_other = lax.optimization_barrier((grad_low_mine, grad_low_other))
     back_term = lax.dot_general(
         grad_low_mine, down_mine, contract, preferred_element_type=jnp.float32

time: 356 us -> 414 us (1.16)
  local copies, waits for them, and re-layouts: 15.3 us -> 44.3 us
  waiting for transfers between devices: 148 us -> 168 us
  blocking collectives: 46.4 us -> 36.3 us
  starting transfers between devices: 17.2 us -> 26.4 us
  matrix products: 24.5 us -> 30.4 us
    all_gather x2 -> x0, waiting for transfers between devices: 97 us -> none  [the longest x1 93.3 us: on_device(): up_mine = lax.all_gather(up_mine, 'fsdp', axis=1, tiled=True)]
    ppermute x2 -> x7, waiting for transfers between devices: 0.01 us -> 80.8 us  [the longest x1 45.5 us: on_device(): got_a = lax.ppermute(piece, both, ring_perm)]
    all_to_all x1, waiting for transfers between devices: 6.23 us -> 39.9 us  [on_device(): lax.all_to_all(send_ids, 'dp', split_axis=1, concat_axis=0, tiled=True)]
    dynamic_update_slice x0 -> x7, local copies, waits for them, and re-layouts: none -> 22.5 us  [the longest x4 12.9 us: on_device(): lax.dynamic_update_slice_in_dim(other, swapped, where * shard_rows, 0)]
    all_to_all x1, blocking collectives: 46.4 us -> 36.3 us  [on_device(): lax.all_to_all(grad_pooled, 'dp', split_axis=1, concat_axis=0, tiled=True)]
    ppermute x2 -> x7, starting transfers between devices: 1.4 us -> 10.8 us  [the longest x1 6.43 us: on_device(): got_a = lax.ppermute(piece, both, ring_perm)]
    another operation x0 -> x2, local copies, waits for them, and re-layouts: none -> 8.51 us
  transfers between devices with their start and end apart: 7 -> 10, of which waited for: 4 -> 5; matrix products, arithmetic and copies ran while one was open for 7% -> 11% of each run, Pallas kernels for 12% -> 10%
where the time goes in v5:
time: 414 us; the launch traced here: 413 us
  waiting for transfers between devices  168 us (41%)
  Pallas kernels  84.2 us (20%)
  local copies, waits for them, and re-layouts  44.3 us (11%)
  blocking collectives  36.3 us (9%)
  matrix products  30.4 us (7%)
  starting transfers between devices  26.4 us (6%)
  between operations  13.5 us (3%)
  other arithmetic  10.5 us (3%)
    reduce_scatter x1, waiting for transfers between devices, on_device(): lax.psum_scatter(partial_value, 'fsdp', scatter_dimension=0, tiled=True)  46.9 us
    ppermute x1, waiting for transfers between devices, on_device(): got_a = lax.ppermute(piece, both, ring_perm)  45.5 us
    pallas_call x1, Pallas kernels, pool_rows(): pl.pallas_call(functools.partial(pool_kernel, blk=blk, slots=slots), grid...  42.5 us
    pallas_call x1, Pallas kernels, scatter_rows(): pl.pallas_call(functools.partial(scatter_kernel, slots=slots), grid_spec=...  41.8 us
    all_to_all x1, waiting for transfers between devices, on_device(): lax.all_to_all(send_ids, 'dp', split_axis=1, concat_axis=0, tiled=True)  39.9 us
    all_to_all x1, blocking collectives, on_device(): lax.all_to_all(grad_pooled, 'dp', split_axis=1, concat_axis=0, tiled=True)  36.3 us
    ppermute x1, waiting for transfers between devices, on_device(): got_c = lax.ppermute(got_b, both, ring_perm)  34.2 us
    dynamic_update_slice x4, local copies, waits for them, and re-layouts, on_device(): lax.dynamic_update_slice_in_dim(other, swapped, where * shard_rows, 0)  12.9 us
  transfers between devices with their start and end apart: 10, of which 5 were waited for; matrix products, arithmetic and copies ran while one was open for 11% of the time, Pallas kernels for 10%

profile of v5, /device:TPU:1, one launch (start us, length us, event | category | flops | bytes accessed | tf_op | source)
XLA Modules:
  0.0 413.2 jit_solution(20641448149966315)
XLA Ops:
  6.5 1.3 constant_dynamic-slice_fusion
  7.8 0.6 copy.15
  8.5 1.3 dynamic-slice_bitcast_fusion
  9.8 4.3 %broadcast.13.clone = bf16[8192,512]{0,1:T(8,128)(2,1)} broadcast(bf16[]{:T(256)} %constant.59.clone.1), dimensions={} | broadcast | bytes 8388610 | tf_op jit(solution)/shard_map/broadcast.1
  14.1 1.9 pad_maximum_fusion
  15.9 1.4 copy-done.1
  17.3 6.4 %collective-permute-start = (bf16[2048,512]{0,1:T(8,128)(2,1)S(1)}, bf16[2048,512]{0,1:T(8,128)(2,1)}, u32[]{:S(2)}, u32[]{:S(2)}) collective-permute-start(bf16[2048,512]{0,1:T(8,128)(2,1)S(1)} %get-tuple-element.13), channel_id=1, source_target_pairs={{0,35},{1,32},{2,33},{3,34},{4,39},{5,36},{6,37},{7,38},{8,43},{9,... | collective-permute-start | bytes 6291464 | tf_op jit(solution)/shard_map/ppermute | solution.py:122
  23.7 45.5 %collective-permute-done = bf16[2048,512]{0,1:T(8,128)(2,1)} collective-permute-done((bf16[2048,512]{0,1:T(8,128)(2,1)S(1)}, bf16[2048,512]{0,1:T(8,128)(2,1)}, u32[]{:S(2)}, u32[]{:S(2)}) %collective-permute-start) | collective-permute-done | bytes 2097184 | tf_op jit(solution)/shard_map/ppermute | solution.py:122
  69.2 0.7 fusion.45
  69.9 10.2 %all-to-all-start = ((s32[128,64,4]{0,2,1:T(4,128)}), s32[128,64,4]{0,2,1:T(4,128)S(1)}, u32[]{:S(2)}, u32[]{:S(2)}) async-start(s32[128,64,4]{0,2,1:T(4,128)} %fusion.45), calls=%async_computation | async-start | bytes 262144 | tf_op jit(solution)/shard_map/all_to_all | solution.py:144
  80.1 3.3 pad_convert_fusion.tab_ref
  83.4 39.9 %all-to-all-done = s32[128,64,4]{0,2,1:T(4,128)S(1)} async-done(((s32[128,64,4]{0,2,1:T(4,128)}), s32[128,64,4]{0,2,1:T(4,128)S(1)}, u32[]{:S(2)}, u32[]{:S(2)}) %all-to-all-start) | async-done | bytes 131104 | tf_op jit(solution)/shard_map/all_to_all | solution.py:144
  123.3 2.6 copy.11
  125.9 5.5 %reshape.19.ids_ref = s32[32768]{0:T(1024)} reshape(s32[64,128,4]{2,1,0:T(8,128)} %copy.11) | data formatting | bytes 262144 | tf_op jit(solution)/shard_map/reshape | solution.py:146
  131.4 42.5 %shard_map.73 = bf16[8192,128]{1,0:T(8,128)(2,1)} custom-call(s32[32768]{0:T(1024)} %reshape.19.ids_ref, f32[8200,128]{1,0:T(8,128)} %pad_convert_fusion.tab_ref), custom_call_target="tpu_custom_call" | custom-call | tf_op jit(solution)/shard_map/pallas_call | solution.py:32
  173.9 5.3 %all-to-all-start.1 = ((bf16[64,128,128]{2,1,0:T(8,128)(2,1)}), bf16[64,128,128]{2,1,0:T(8,128)(2,1)}, u32[]{:S(2)}, u32[]{:S(2)}) async-start(bf16[64,128,128]{2,1,0:T(8,128)(2,1)} %bitcast.44), calls=%async_computation.1 | async-start | bytes 4194304 | tf_op jit(solution)/shard_map/all_to_all | solution.py:152
  179.2 0.0 reduce-scatter.2.cloned.1.call-start
  179.2 0.7 collective-permute-start.3
  180.0 2.3 collective-permute-start.2
  182.3 0.4 collective-permute-start.4
  182.7 0.1 collective-permute-start.5
  182.8 1.1 collective-permute-done.3
  183.9 4.3 %broadcast.13 = bf16[8192,512]{0,1:T(8,128)(2,1)} broadcast(bf16[]{:T(256)} %constant.59.clone.1), dimensions={} | broadcast | bytes 8388610 | tf_op jit(solution)/shard_map/broadcast.1
  188.1 3.2 constant_dynamic-update-slice_fusion.3
  191.3 3.2 constant_dynamic-update-slice_fusion.6
  194.5 34.2 %collective-permute-done.2 = bf16[2048,512]{0,1:T(8,128)(2,1)} collective-permute-done((bf16[2048,512]{0,1:T(8,128)(2,1)}, bf16[2048,512]{0,1:T(8,128)(2,1)}, u32[]{:S(2)}, u32[]{:S(2)}) %collective-permute-start.2) | collective-permute-done | bytes 2097184 | tf_op jit(solution)/shard_map/ppermute | solution.py:124
  228.7 0.9 collective-permute-start.6
  229.6 3.2 constant_dynamic-update-slice_fusion.2
  232.8 3.2 constant_dynamic-update-slice_fusion.5
  236.0 3.2 constant_dynamic-update-slice_fusion.1
  239.2 3.3 constant_dynamic-update-slice_fusion.4
  242.5 4.5 %fusion.27 = bf16[128,256]{1,0:T(8,128)(2,1)S(1)} fusion(bf16[8192,512]{0,1:T(8,128)(2,1)} %constant_dynamic-update-slice_fusion.4, bf16[64,128,128]{2,1,0:T(8,128)(2,1)} %all-to-all-done.1), kind=kOutput, calls=%fused_computation.31 | convolution fusion | flops 536903680 | bytes 6356992 | tf_op jit(solution)/shard_map/dot_general | solution.py:156
  246.9 4.4 %fusion.37 = bf16[128,256]{1,0:T(8,128)(2,1)S(1)} fusion(bf16[8192,512]{0,1:T(8,128)(2,1)} %constant_dynamic-update-slice_fusion.4, bf16[128,8192]{1,0:T(8,128)(2,1)S(1)} %copy-done, bf16[64,128,128]{2,1,0:T(8,128)(2,1)} %all-to-all-done.1), kind=kOutput, calls=%fused_computation.33 | convolution fusion | flops 541097984 | bytes 8454144 | tf_op jit(solution)/shard_map/dot_general | solution.py:165
  251.3 3.2 constant_dynamic-update-slice_fusion
  254.6 4.4 %fusion.40 = bf16[128,256]{1,0:T(8,128)(2,1)S(1)} fusion(bf16[8192,512]{0,1:T(8,128)(2,1)} %constant_dynamic-update-slice_fusion, bf16[128,8192]{1,0:T(8,128)(2,1)S(1)} %copy-done, bf16[64,128,128]{2,1,0:T(8,128)(2,1)} %all-to-all-done.1), kind=kOutput, calls=%fused_computation.34 | convolution fusion | flops 541097984 | bytes 8454144 | tf_op jit(solution)/shard_map/dot_general | solution.py:168
  258.9 2.9 fusion.16
  261.8 4.3 %fusion.32 = bf16[128,256]{1,0:T(8,128)(2,1)S(1)} fusion(bf16[8192,512]{0,1:T(8,128)(2,1)} %constant_dynamic-update-slice_fusion, bf16[64,128,128]{2,1,0:T(8,128)(2,1)} %all-to-all-done.1), kind=kOutput, calls=%fused_computation.32 | convolution fusion | flops 536903680 | bytes 6356992 | tf_op jit(solution)/shard_map/dot_general | solution.py:157
  266.2 0.0 copy-start.4
  266.2 2.9 fusion.11
  269.1 3.7 fusion.3
  272.8 3.4 fusion.22
  276.2 0.6 copy.34
  276.8 36.3 %all_to_all.45 = bf16[128,64,128]{2,0,1:T(8,128)(2,1)S(1)} all-to-all(bf16[128,64,128]{2,0,1:T(8,128)(2,1)S(1)} %bitcast.43), channel_id=1, replica_groups=mesh['dp'=64,'fsdp'=4] {'dp'}, dimensions={1} | all-to-all | bytes 4194304 | tf_op jit(solution)/shard_map/all_to_all | solution.py:176
  313.1 2.5 convert_element_type.48
  315.6 41.8 %shard_map.74 = bf16[8192,128]{1,0:T(8,128)(2,1)} custom-call(s32[32768]{0:T(1024)} %reshape.19.ids_ref, f32[8192,128]{1,0:T(8,128)} %bitcast.42), custom_call_target="tpu_custom_call" | custom-call | tf_op jit(solution)/shard_map/pallas_call | solution.py:71
  357.3 0.0 reduce-scatter.2.cloned.1.call-update
  357.4 46.9 %reduce-scatter.2.cloned.1.call-done = bf16[2048,128]{1,0:T(8,128)(2,1)} async-done(((bf16[8192,128]{1,0:T(8,128)(2,1)}), bf16[2048,128]{1,0:T(8,128)(2,1)}) %reduce-scatter.2.cloned.1.call-update) | async-done | bytes 524304 | tf_op jit(solution)/shard_map/reduce_scatter | solution.py:180
  404.2 2.1 convert_element_type.46
  (16 shorter events, 0.0 us)
Async XLA Ops:
  14.0 55.1 %copy-start.3 = (s32[128,64,4]{0,2,1:T(4,128)S(1)}, s32[128,64,4]{0,2,1:T(4,128)}, u32[]{:S(2)}) copy-start(s32[128,64,4]{0,2,1:T(4,128)} %param.7) | copy-start | bytes 393220
  14.0 55.1 %copy-start.5 = (s32[128,64]{0,1:T(8,128)S(1)}, s32[128,64]{0,1:T(8,128)}, u32[]{:S(2)}) copy-start(s32[128,64]{0,1:T(8,128)} %param.8) | copy-start | bytes 98308
  15.9 1.4 copy-start.1
  17.3 51.9 %collective-permute-start = (bf16[2048,512]{0,1:T(8,128)(2,1)S(1)}, bf16[2048,512]{0,1:T(8,128)(2,1)}, u32[]{:S(2)}, u32[]{:S(2)}) collective-permute-start(bf16[2048,512]{0,1:T(8,128)(2,1)S(1)} %get-tuple-element.13), channel_id=1, source_target_pairs={{0,35},{1,32},{2,33},{3,34},{4,39},{5,36},{6,37},{7,38},{8,43},{9,... | collective-permute-start | bytes 6291464 | tf_op jit(solution)/shard_map/ppermute | solution.py:122
  69.2 110.8 %collective-permute-start.1 = (bf16[2048,512]{0,1:T(8,128)(2,1)}, bf16[2048,512]{0,1:T(8,128)(2,1)}, u32[]{:S(2)}, u32[]{:S(2)}) collective-permute-start(bf16[2048,512]{0,1:T(8,128)(2,1)} %collective-permute-done), channel_id=1, source_target_pairs={{0,32},{1,33},{2,34},{3,35},{4,36},{5,37},{6,38},{7,39},{8,40},{9,... | collective-permute-start | bytes 6291464 | tf_op jit(solution)/shard_map/ppermute | solution.py:123
  69.9 53.4 %all-to-all-start = ((s32[128,64,4]{0,2,1:T(4,128)}), s32[128,64,4]{0,2,1:T(4,128)S(1)}, u32[]{:S(2)}, u32[]{:S(2)}) async-start(s32[128,64,4]{0,2,1:T(4,128)} %fusion.45), calls=%async_computation | async-start | bytes 262144 | tf_op jit(solution)/shard_map/all_to_all | solution.py:144
  131.4 47.9 %copy-start.2 = (bf16[2048,512]{0,1:T(8,128)(2,1)S(1)}, bf16[2048,512]{0,1:T(8,128)(2,1)}, u32[]{:S(2)}) copy-start(bf16[2048,512]{0,1:T(8,128)(2,1)} %copy-done.1) | copy-start | bytes 6291460
  173.9 68.6 %all-to-all-start.1 = ((bf16[64,128,128]{2,1,0:T(8,128)(2,1)}), bf16[64,128,128]{2,1,0:T(8,128)(2,1)}, u32[]{:S(2)}, u32[]{:S(2)}) async-start(bf16[64,128,128]{2,1,0:T(8,128)(2,1)} %bitcast.44), calls=%async_computation.1 | async-start | bytes 4194304 | tf_op jit(solution)/shard_map/all_to_all | solution.py:152
  179.2 225.0 %reduce-scatter.2.cloned.1.call-start = ((), (), s32[]{:S(2)}) async-start(), calls=%async_computation.4 | async-start | bytes 2621440 | tf_op jit(solution)/shard_map/reduce_scatter | solution.py:180
  179.2 4.6 %collective-permute-start.3 = (bf16[2048,512]{0,1:T(8,128)(2,1)S(1)}, bf16[2048,512]{0,1:T(8,128)(2,1)}, u32[]{:S(2)}, u32[]{:S(2)}) collective-permute-start(bf16[2048,512]{0,1:T(8,128)(2,1)S(1)} %copy-done.2), channel_id=1, source_target_pairs={{0,4},{1,5},{2,6},{3,7},{4,0},{5,1},{6,2},{7,3},{8,12},{9,13},{10,... | collective-permute-start | bytes 6291464 | tf_op jit(solution)/shard_map/ppermute | solution.py:136
  180.0 48.7 %collective-permute-start.2 = (bf16[2048,512]{0,1:T(8,128)(2,1)}, bf16[2048,512]{0,1:T(8,128)(2,1)}, u32[]{:S(2)}, u32[]{:S(2)}) collective-permute-start(bf16[2048,512]{0,1:T(8,128)(2,1)} %collective-permute-done.1), channel_id=1, source_target_pairs={{0,35},{1,32},{2,33},{3,34},{4,39},{5,36},{6,37},{7,38},{8,43},{9,... | collective-permute-start | bytes 6291464 | tf_op jit(solution)/shard_map/ppermute | solution.py:124
  182.3 47.3 %collective-permute-start.4 = (bf16[2048,512]{0,1:T(8,128)(2,1)}, bf16[2048,512]{0,1:T(8,128)(2,1)}, u32[]{:S(2)}, u32[]{:S(2)}) collective-permute-start(bf16[2048,512]{0,1:T(8,128)(2,1)} %collective-permute-done), channel_id=1, source_target_pairs={{0,4},{1,5},{2,6},{3,7},{4,0},{5,1},{6,2},{7,3},{8,12},{9,13},{10,... | collective-permute-start | bytes 6291464 | tf_op jit(solution)/shard_map/ppermute | solution.py:136
  182.7 53.3 %collective-permute-start.5 = (bf16[2048,512]{0,1:T(8,128)(2,1)}, bf16[2048,512]{0,1:T(8,128)(2,1)}, u32[]{:S(2)}, u32[]{:S(2)}) collective-permute-start(bf16[2048,512]{0,1:T(8,128)(2,1)} %collective-permute-done.1), channel_id=1, source_target_pairs={{0,4},{1,5},{2,6},{3,7},{4,0},{5,1},{6,2},{7,3},{8,12},{9,13},{10,... | collective-permute-start | bytes 6291464 | tf_op jit(solution)/shard_map/ppermute | solution.py:136
  228.7 22.6 %collective-permute-start.6 = (bf16[2048,512]{0,1:T(8,128)(2,1)}, bf16[2048,512]{0,1:T(8,128)(2,1)}, u32[]{:S(2)}, u32[]{:S(2)}) collective-permute-start(bf16[2048,512]{0,1:T(8,128)(2,1)} %collective-permute-done.2), channel_id=1, source_target_pairs={{0,4},{1,5},{2,6},{3,7},{4,0},{5,1},{6,2},{7,3},{8,12},{9,13},{10,... | collective-permute-start | bytes 6291464 | tf_op jit(solution)/shard_map/ppermute | solution.py:136
  242.5 4.5 %copy-start = (bf16[128,8192]{1,0:T(8,128)(2,1)S(1)}, bf16[128,8192]{1,0:T(8,128)(2,1)}, u32[]{:S(2)}) copy-start(bf16[128,8192]{1,0:T(8,128)(2,1)} %param.13) | copy-start | bytes 6291460
  266.2 2.9 copy-start.4
Sparse Core Ops, SparseCore 0:
  357.5 46.6 reduce-scatter.1

commit v6 on v3

--- a/solution.py
+++ b/solution.py
@@ -95,12 +95,12 @@
     dp_idx = lax.axis_index("dp")
     core = dp_idx % 2
     down_mine = lax.dynamic_slice_in_dim(cross_down, core * half, half, 1)
-    up_mine = lax.dynamic_slice_in_dim(cross_up, core * half, half, 0)
+    up_t_mine = lax.dynamic_slice_in_dim(cross_up, core * half, half, 0).T
     down_mine = lax.all_gather(down_mine, "fsdp", axis=0, tiled=True)
-    up_mine = lax.all_gather(up_mine, "fsdp", axis=1, tiled=True)
+    up_t_mine = lax.all_gather(up_t_mine, "fsdp", axis=0, tiled=True)
     partner = [(i, i ^ 1) for i in range(dp_size)]
     down_other = lax.ppermute(down_mine, "dp", partner)
-    up_other = lax.ppermute(up_mine, "dp", partner)
+    up_t_other = lax.ppermute(up_t_mine, "dp", partner)
 
     slot_iota = lax.broadcasted_iota(jnp.int32, bag_ids.shape, 2)
     live_ids = jnp.where(slot_iota < bag_counts[:, :, None], bag_ids, vocab_rows)
@@ -120,18 +120,18 @@
     low_mine = jnp.dot(pooled, down_mine, preferred_element_type=jnp.float32).astype(jnp.bfloat16)
     low_other = jnp.dot(pooled, down_other, preferred_element_type=jnp.float32).astype(jnp.bfloat16)
     low_mine, low_other = lax.optimization_barrier((low_mine, low_other))
+    contract = (((1,), (1,)), ((), ()))
     gate_value = (
-        jnp.dot(low_mine, up_mine, preferred_element_type=jnp.float32)
-        + jnp.dot(low_other, up_other, preferred_element_type=jnp.float32)
+        lax.dot_general(low_mine, up_t_mine, contract, preferred_element_type=jnp.float32)
+        + lax.dot_general(low_other, up_t_other, contract, preferred_element_type=jnp.float32)
         + cross_bias
     )
-    contract = (((1,), (1,)), ((), ()))
-    grad_low_mine = lax.dot_general(
-        grad_gate, up_mine, contract, preferred_element_type=jnp.float32
-    ).astype(jnp.bfloat16)
-    grad_low_other = lax.dot_general(
-        grad_gate, up_other, contract, preferred_element_type=jnp.float32
-    ).astype(jnp.bfloat16)
+    grad_low_mine = jnp.dot(grad_gate, up_t_mine, preferred_element_type=jnp.float32).astype(
+        jnp.bfloat16
+    )
+    grad_low_other = jnp.dot(grad_gate, up_t_other, preferred_element_type=jnp.float32).astype(
+        jnp.bfloat16
+    )
     grad_low_mine, grad_low_other = lax.optimization_barrier((grad_low_mine, grad_low_other))
     back_term = lax.dot_general(
         grad_low_mine, down_mine, contract, preferred_element_type=jnp.float32

time: 356 us -> 356 us (level)
  no operation moved by 1% of the time
where the time goes in v6:
time: 356 us
  waiting for transfers between devices  148 us (42%)
  Pallas kernels  84.1 us (24%)
  blocking collectives  46.4 us (13%)
  matrix products  24.5 us (7%)
  starting transfers between devices  17.2 us (5%)
  local copies, waits for them, and re-layouts  15.3 us (4%)
  between operations  13.3 us (4%)
  other arithmetic  7.61 us (2%)
    all_gather x1, waiting for transfers between devices, on_device(): up_t_mine = lax.all_gather(up_t_mine, 'fsdp', axis=0, tiled=True)  93.3 us
    all_to_all x1, blocking collectives, on_device(): lax.all_to_all(grad_pooled, 'dp', split_axis=1, concat_axis=0, tiled=True)  46.4 us
    reduce_scatter x1, waiting for transfers between devices, on_device(): lax.psum_scatter(partial_value, 'fsdp', scatter_dimension=0, tiled=True)  44.3 us
    pallas_call x1, Pallas kernels, pool_rows(): pl.pallas_call(functools.partial(pool_kernel, blk=blk, slots=slots), grid...  42.4 us
    pallas_call x1, Pallas kernels, scatter_rows(): pl.pallas_call(functools.partial(scatter_kernel, slots=slots), grid_spec=...  41.7 us
    all_to_all x1, starting transfers between devices, on_device(): lax.all_to_all(send_ids, 'dp', split_axis=1, concat_axis=0, tiled=True)  10.3 us
  transfers between devices with their start and end apart: 7, of which 4 were waited for; matrix products, arithmetic and copies ran while one was open for 7% of the time, Pallas kernels for 12%

profile of v6, /device:TPU:1, one launch (start us, length us, event | category | flops | bytes accessed | tf_op | source)
XLA Modules:
  0.0 355.8 jit_solution(6541972431318574123)
XLA Ops:
  6.5 0.0 copy-start.4
  6.5 0.0 copy-start.6
  6.5 0.0 all-gather.3.cloned.1.call-start
  6.5 2.4 constant_dynamic-slice_fusion
  9.0 0.0 all-gather.3.cloned.1.call-update
  9.0 0.0 all-gather.5.cloned.1.call-start
  9.0 2.4 dynamic-slice_bitcast_fusion
  11.4 0.0 all-gather.5.cloned.1.call-update
  11.5 0.0 copy-done.4
  11.5 0.0 copy-done.6
  11.5 0.7 fusion.21
  12.2 10.3 %all-to-all-start = ((s32[128,64,4]{0,2,1:T(4,128)}), s32[128,64,4]{0,2,1:T(4,128)S(1)}, u32[]{:S(2)}, u32[]{:S(2)}) async-start(s32[128,64,4]{0,2,1:T(4,128)} %fusion.21), calls=%async_computation | async-start | bytes 262144 | tf_op jit(solution)/shard_map/all_to_all | solution.py:108
  22.5 0.0 copy-done.3
  22.5 2.3 pad_convert_fusion.tab_ref
  24.8 6.2 %all-to-all-done = s32[128,64,4]{0,2,1:T(4,128)S(1)} async-done(((s32[128,64,4]{0,2,1:T(4,128)}), s32[128,64,4]{0,2,1:T(4,128)S(1)}, u32[]{:S(2)}, u32[]{:S(2)}) %all-to-all-start) | async-done | bytes 131104 | tf_op jit(solution)/shard_map/all_to_all | solution.py:108
  31.1 2.6 copy.10
  33.7 5.5 %reshape.19.ids_ref = s32[32768]{0:T(1024)} reshape(s32[64,128,4]{2,1,0:T(8,128)} %copy.10) | data formatting | bytes 262144 | tf_op jit(solution)/shard_map/reshape | solution.py:110
  39.2 42.4 %shard_map.73 = bf16[8192,128]{1,0:T(8,128)(2,1)} custom-call(s32[32768]{0:T(1024)} %reshape.19.ids_ref, f32[8200,128]{1,0:T(8,128)} %pad_convert_fusion.tab_ref), custom_call_target="tpu_custom_call" | custom-call | tf_op jit(solution)/shard_map/pallas_call | solution.py:32
  81.5 5.3 %all-to-all-start.1 = ((bf16[64,128,128]{2,1,0:T(8,128)(2,1)}), bf16[64,128,128]{2,1,0:T(8,128)(2,1)}, u32[]{:S(2)}, u32[]{:S(2)}) async-start(bf16[64,128,128]{2,1,0:T(8,128)(2,1)} %bitcast.52), calls=%async_computation.1 | async-start | bytes 4194304 | tf_op jit(solution)/shard_map/all_to_all | solution.py:116
  86.9 0.0 copy-start
  86.9 0.0 reduce-scatter.2.cloned.1.call-start
  86.9 3.6 %all-gather.3.cloned.1.call-done = bf16[8192,256]{1,0:T(8,128)(2,1)} async-done(((bf16[2048,256]{1,0:T(8,128)(2,1)}), bf16[8192,256]{1,0:T(8,128)(2,1)}) %all-gather.3.cloned.1.call-update) | async-done | bytes 4194320 | tf_op jit(solution)/shard_map/all_gather | solution.py:99
  90.6 0.7 collective-permute-start
  91.3 93.3 %all-gather.5.cloned.1.call-done = bf16[8192,256]{0,1:T(8,128)(2,1)} async-done(((bf16[2048,256]{0,1:T(8,128)(2,1)}), bf16[8192,256]{0,1:T(8,128)(2,1)}) %all-gather.5.cloned.1.call-update) | async-done | bytes 4194320 | tf_op jit(solution)/shard_map/all_gather | solution.py:100
  184.6 0.7 collective-permute-start.1
  185.3 0.0 all-to-all-done.1
  185.3 3.7 %fusion.13 = bf16[128,256]{1,0:T(8,128)(2,1)S(1)} fusion(bf16[8192,256]{1,0:T(8,128)(2,1)} %all-gather.3.cloned.1.call-done, bf16[64,128,128]{2,1,0:T(8,128)(2,1)} %all-to-all-done.1), kind=kOutput, calls=%fused_computation.18 | convolution fusion | flops 536903680 | bytes 6356992 | tf_op jit(solution)/shard_map/dot_general | solution.py:120
  189.0 0.0 copy-done
  189.0 0.3 copy-done.1
  189.3 3.2 convolution_convert_fusion.1
  192.6 0.0 collective-permute-done
  192.6 3.5 fusion.16
  196.1 0.0 collective-permute-done.1
  196.1 4.4 %convolution_convert_fusion = bf16[128,256]{1,0:T(8,128)(2,1)S(1)} fusion(bf16[8192,256]{0,1:T(8,128)(2,1)} %collective-permute-done.1, bf16[128,8192]{1,0:T(8,128)(2,1)S(1)} %copy-done, bf16[64,128,128]{2,1,0:T(8,128)(2,1)} %all-to-all-done.1), kind=kOutput, calls=%fused_computation.20 | convolution fusion | flops 541097984 | bytes 8454144 | tf_op jit(solution)/shard_map/dot_general | solution.py:132
  200.5 0.0 copy-start.2
  200.5 0.7 fusion.22
  201.2 1.4 copy-done.2
  202.7 1.5 fusion.23
  204.2 0.0 copy-done.5
  204.2 3.7 %fusion.3 = f32[128,8192]{1,0:T(8,128)S(1)} fusion(f32[128,8192]{1,0:T(8,128)S(1)} %fusion.22, bf16[128,256]{1,0:T(8,128)(2,1)S(1)} %fusion.16, bf16[8192,256]{0,1:T(8,128)(2,1)} %collective-permute-done.1, bf16[128,8192]{1,0:T(8,128)(2,1)S(1)} %copy-done, f32[8192]{0:T(1024)S(1)} %copy-done.5), kind=kOutput, calls=%fused_computation.5 | convolution fusion | flops 542113792 | bytes 14778368 | tf_op jit(solution)/shard_map/dot_general | solution.py:126
  207.9 3.8 %fusion.10 = bf16[16,64,8,128]{3,2,1,0:T(8,128)(2,1)S(1)} fusion(f32[128,8192]{1,0:T(8,128)S(1)} %fusion.3, f32[128,8192]{1,0:T(8,128)S(1)} %fusion.23, bf16[128,256]{1,0:T(8,128)(2,1)S(1)} %convolution_convert_fusion, bf16[8192,256]{1,0:T(8,128)(2,1)} %collective-permute-done), kind=kOutput, calls=%fused_computation.15 | convolution fusion | flops 540016640 | bytes 14745600 | tf_op jit(solution)/shard_map/dot_general | solution.py:138
  211.7 0.6 copy.31
  212.3 46.4 %all_to_all.45 = bf16[128,64,128]{2,0,1:T(8,128)(2,1)S(1)} all-to-all(bf16[128,64,128]{2,0,1:T(8,128)(2,1)S(1)} %bitcast.51), channel_id=1, replica_groups=mesh['dp'=64,'fsdp'=4] {'dp'}, dimensions={1} | all-to-all | bytes 4194304 | tf_op jit(solution)/shard_map/all_to_all | solution.py:140
  258.6 2.5 convert_element_type.48
  261.2 41.7 %shard_map.74 = bf16[8192,128]{1,0:T(8,128)(2,1)} custom-call(s32[32768]{0:T(1024)} %reshape.19.ids_ref, f32[8192,128]{1,0:T(8,128)} %bitcast.50), custom_call_target="tpu_custom_call" | custom-call | tf_op jit(solution)/shard_map/pallas_call | solution.py:71
  302.9 0.0 reduce-scatter.2.cloned.1.call-update
  303.0 44.3 %reduce-scatter.2.cloned.1.call-done = bf16[2048,128]{1,0:T(8,128)(2,1)} async-done(((bf16[8192,128]{1,0:T(8,128)(2,1)}), bf16[2048,128]{1,0:T(8,128)(2,1)}) %reduce-scatter.2.cloned.1.call-update) | async-done | bytes 524304 | tf_op jit(solution)/shard_map/reduce_scatter | solution.py:144
  347.2 2.1 convert_element_type.46
  (3 shorter events, 0.0 us)
Async XLA Ops:
  6.5 4.9 %copy-start.4 = (s32[128,64,4]{0,2,1:T(4,128)S(1)}, s32[128,64,4]{0,2,1:T(4,128)}, u32[]{:S(2)}) copy-start(s32[128,64,4]{0,2,1:T(4,128)} %param.7) | copy-start | bytes 393220
  6.5 4.9 %copy-start.6 = (s32[128,64]{0,1:T(8,128)S(1)}, s32[128,64]{0,1:T(8,128)}, u32[]{:S(2)}) copy-start(s32[128,64]{0,1:T(8,128)} %param.8) | copy-start | bytes 98308
  6.5 16.0 %copy-start.3 = (bf16[8192,128]{1,0:T(8,128)(2,1)S(1)}, bf16[8192,128]{1,0:T(8,128)(2,1)}, u32[]{:S(2)}) copy-start(bf16[8192,128]{1,0:T(8,128)(2,1)} %param.9) | copy-start | bytes 6291460
  6.5 84.0 %all-gather.3.cloned.1.call-start = ((), (), s32[]{:S(2)}) async-start(), calls=%async_computation.4 | async-start | bytes 5242880 | tf_op jit(solution)/shard_map/all_gather | solution.py:99
  9.0 175.6 %all-gather.5.cloned.1.call-start = ((), (), s32[]{:S(2)}) async-start(), calls=%async_computation.5 | async-start | bytes 5242880 | tf_op jit(solution)/shard_map/all_gather | solution.py:100
  12.2 18.9 %all-to-all-start = ((s32[128,64,4]{0,2,1:T(4,128)}), s32[128,64,4]{0,2,1:T(4,128)S(1)}, u32[]{:S(2)}, u32[]{:S(2)}) async-start(s32[128,64,4]{0,2,1:T(4,128)} %fusion.21), calls=%async_computation | async-start | bytes 262144 | tf_op jit(solution)/shard_map/all_to_all | solution.py:108
  81.5 103.8 %all-to-all-start.1 = ((bf16[64,128,128]{2,1,0:T(8,128)(2,1)}), bf16[64,128,128]{2,1,0:T(8,128)(2,1)}, u32[]{:S(2)}, u32[]{:S(2)}) async-start(bf16[64,128,128]{2,1,0:T(8,128)(2,1)} %bitcast.52), calls=%async_computation.1 | async-start | bytes 4194304 | tf_op jit(solution)/shard_map/all_to_all | solution.py:116
  86.9 102.1 %copy-start = (bf16[128,8192]{1,0:T(8,128)(2,1)S(1)}, bf16[128,8192]{1,0:T(8,128)(2,1)}, u32[]{:S(2)}) copy-start(bf16[128,8192]{1,0:T(8,128)(2,1)} %param.13) | copy-start | bytes 6291460
  86.9 260.3 %reduce-scatter.2.cloned.1.call-start = ((), (), s32[]{:S(2)}) async-start(), calls=%async_computation.6 | async-start | bytes 2621440 | tf_op jit(solution)/shard_map/reduce_scatter | solution.py:144
  90.6 102.0 %collective-permute-start = (bf16[8192,256]{1,0:T(8,128)(2,1)}, bf16[8192,256]{1,0:T(8,128)(2,1)}, u32[]{:S(2)}, u32[]{:S(2)}) collective-permute-start(bf16[8192,256]{1,0:T(8,128)(2,1)} %all-gather.3.cloned.1.call-done), channel_id=1, source_target_pairs={{0,4},{4,0},{8,12},{12,8},{16,20},{20,16},{24,28},{28,24},{32,36},... | collective-permute-start | bytes 12582920 | tf_op jit(solution)/shard_map/ppermute | solution.py:102
  184.6 11.6 %collective-permute-start.1 = (bf16[8192,256]{0,1:T(8,128)(2,1)}, bf16[8192,256]{0,1:T(8,128)(2,1)}, u32[]{:S(2)}, u32[]{:S(2)}) collective-permute-start(bf16[8192,256]{0,1:T(8,128)(2,1)} %all-gather.5.cloned.1.call-done), channel_id=1, source_target_pairs={{0,4},{4,0},{8,12},{12,8},{16,20},{20,16},{24,28},{28,24},{32,36},... | collective-permute-start | bytes 12582920 | tf_op jit(solution)/shard_map/ppermute | solution.py:103
  185.3 4.0 %copy-start.1 = (bf16[8192,256]{0,1:T(8,128)(2,1)S(1)}, bf16[8192,256]{0,1:T(8,128)(2,1)}, u32[]{:S(2)}) copy-start(bf16[8192,256]{0,1:T(8,128)(2,1)} %all-gather.5.cloned.1.call-done) | copy-start | bytes 12582916
  200.5 2.2 copy-start.2
  202.7 1.5 copy-start.5
Sparse Core Ops, SparseCore 0:
  9.2 81.3 all-gather.2
  92.4 92.1 all-gather.4
  303.1 44.0 reduce-scatter.1

commit v7 on v3

--- a/solution.py
+++ b/solution.py
@@ -141,10 +141,12 @@
     partial_value = scatter_rows(
         ids_flat, grad_local.astype(jnp.float32), vocab_rows, slot_count
     )
-    summed = lax.psum_scatter(
-        partial_value, "fsdp", scatter_dimension=0, tiled=True
+    fsdp_size = lax.axis_size("fsdp")
+    pieces = lax.all_to_all(
+        partial_value.reshape(fsdp_size, vocab_rows // fsdp_size, col_piece),
+        "fsdp", split_axis=0, concat_axis=0, tiled=True,
     )
-    return summed.astype(jnp.float32)
+    return jnp.sum(pieces.astype(jnp.float32), axis=0)
 
 
 def solution(mesh):

time: 356 us -> 365 us (1.025)
  blocking collectives: 46.4 us -> 99.5 us
  waiting for transfers between devices: 148 us -> 103 us
    all_to_all x0 -> x1, blocking collectives: none -> 53.1 us  [on_device(): lax.all_to_all(partial_value.reshape(fsdp_size, vocab_rows // fsdp_size,...]
    reduce_scatter x1 -> x0, waiting for transfers between devices: 44.3 us -> none  [on_device(): lax.psum_scatter(partial_value, 'fsdp', scatter_dimension=0, tiled=True)]
  transfers between devices with their start and end apart: 7 -> 6, of which waited for: 4 -> 2; matrix products, arithmetic and copies ran while one was open for 7% -> 7% of each run, Pallas kernels for 12% -> 12%
where the time goes in v7:
time: 365 us; the launch traced here: 364 us
  waiting for transfers between devices  103 us (28%)
  blocking collectives  99.5 us (27%)
  Pallas kernels  84.1 us (23%)
  matrix products  24.5 us (7%)
  starting transfers between devices  17.2 us (5%)
  local copies, waits for them, and re-layouts  15.3 us (4%)
  between operations  13.6 us (4%)
  other arithmetic  6.78 us (2%)
    all_gather x1, waiting for transfers between devices, on_device(): up_mine = lax.all_gather(up_mine, 'fsdp', axis=1, tiled=True)  97 us
    all_to_all x1, blocking collectives, on_device(): lax.all_to_all(partial_value.reshape(fsdp_size, vocab_rows // fsdp_size,...  53.1 us
    all_to_all x1, blocking collectives, on_device(): lax.all_to_all(grad_pooled, 'dp', split_axis=1, concat_axis=0, tiled=True)  46.4 us
    pallas_call x1, Pallas kernels, pool_rows(): pl.pallas_call(functools.partial(pool_kernel, blk=blk, slots=slots), grid...  42.4 us
    pallas_call x1, Pallas kernels, scatter_rows(): pl.pallas_call(functools.partial(scatter_kernel, slots=slots), grid_spec=...  41.7 us
    all_to_all x1, starting transfers between devices, on_device(): lax.all_to_all(send_ids, 'dp', split_axis=1, concat_axis=0, tiled=True)  10.3 us
  transfers between devices with their start and end apart: 6, of which 2 were waited for; matrix products, arithmetic and copies ran while one was open for 7% of the time, Pallas kernels for 12%

profile of v7, /device:TPU:1, one launch (start us, length us, event | category | flops | bytes accessed | tf_op | source)
XLA Modules:
  0.0 364.1 jit_solution(16734785809290116686)
XLA Ops:
  6.5 0.0 copy-start.6
  6.5 0.0 copy-start.3
  6.5 0.0 all-gather.3.cloned.1.call-start
  6.5 2.4 constant_dynamic-slice_fusion.1
  9.0 0.0 all-gather.3.cloned.1.call-update
  9.0 0.0 all-gather.5.cloned.1.call-start
  9.0 2.4 constant_dynamic-slice_fusion
  11.4 0.0 all-gather.5.cloned.1.call-update
  11.4 0.0 copy-done.4
  11.5 0.0 copy-done.6
  11.5 0.7 fusion.21
  12.2 10.3 %all-to-all-start = ((s32[128,64,4]{0,2,1:T(4,128)}), s32[128,64,4]{0,2,1:T(4,128)S(1)}, u32[]{:S(2)}, u32[]{:S(2)}) async-start(s32[128,64,4]{0,2,1:T(4,128)} %fusion.21), calls=%async_computation | async-start | bytes 262144 | tf_op jit(solution)/shard_map/all_to_all | solution.py:108
  22.5 0.0 copy-done.3
  22.5 2.3 pad_convert_fusion.tab_ref
  24.8 6.2 %all-to-all-done = s32[128,64,4]{0,2,1:T(4,128)S(1)} async-done(((s32[128,64,4]{0,2,1:T(4,128)}), s32[128,64,4]{0,2,1:T(4,128)S(1)}, u32[]{:S(2)}, u32[]{:S(2)}) %all-to-all-start) | async-done | bytes 131104 | tf_op jit(solution)/shard_map/all_to_all | solution.py:108
  31.0 2.6 copy.10
  33.7 5.5 %reshape.22.ids_ref = s32[32768]{0:T(1024)} reshape(s32[64,128,4]{2,1,0:T(8,128)} %copy.10) | data formatting | bytes 262144 | tf_op jit(solution)/shard_map/reshape | solution.py:110
  39.2 42.4 %shard_map.73 = bf16[8192,128]{1,0:T(8,128)(2,1)} custom-call(s32[32768]{0:T(1024)} %reshape.22.ids_ref, f32[8200,128]{1,0:T(8,128)} %pad_convert_fusion.tab_ref), custom_call_target="tpu_custom_call" | custom-call | tf_op jit(solution)/shard_map/pallas_call | solution.py:32
  81.5 5.3 %all-to-all-start.1 = ((bf16[64,128,128]{2,1,0:T(8,128)(2,1)}), bf16[64,128,128]{2,1,0:T(8,128)(2,1)}, u32[]{:S(2)}, u32[]{:S(2)}) async-start(bf16[64,128,128]{2,1,0:T(8,128)(2,1)} %bitcast.52), calls=%async_computation.1 | async-start | bytes 4194304 | tf_op jit(solution)/shard_map/all_to_all | solution.py:116
  86.9 0.0 copy-start
  86.9 0.0 all-gather.3.cloned.1.call-done
  86.9 0.7 collective-permute-start
  87.6 97.0 %all-gather.5.cloned.1.call-done = bf16[256,8192]{1,0:T(8,128)(2,1)} async-done(((bf16[256,2048]{1,0:T(8,128)(2,1)}), bf16[256,8192]{1,0:T(8,128)(2,1)}) %all-gather.5.cloned.1.call-update) | async-done | bytes 4194320 | tf_op jit(solution)/shard_map/all_gather | solution.py:100
  184.6 0.7 collective-permute-start.1
  185.3 0.0 all-to-all-done.1
  185.3 0.0 copy-start.1
  185.3 3.7 %fusion.13 = bf16[128,256]{1,0:T(8,128)(2,1)S(1)} fusion(bf16[8192,256]{1,0:T(8,128)(2,1)} %all-gather.3.cloned.1.call-done, bf16[64,128,128]{2,1,0:T(8,128)(2,1)} %all-to-all-done.1), kind=kOutput, calls=%fused_computation.19 | convolution fusion | flops 536903680 | bytes 6356992 | tf_op jit(solution)/shard_map/dot_general | solution.py:120
  189.0 0.0 copy-done
  189.0 0.3 copy-done.1
  189.3 3.2 convolution_convert_fusion.1
  192.6 0.0 collective-permute-done
  192.6 3.5 fusion.16
  196.1 0.0 collective-permute-done.1
  196.1 4.4 %convolution_convert_fusion = bf16[128,256]{1,0:T(8,128)(2,1)S(1)} fusion(bf16[256,8192]{1,0:T(8,128)(2,1)} %collective-permute-done.1, bf16[128,8192]{1,0:T(8,128)(2,1)S(1)} %copy-done, bf16[64,128,128]{2,1,0:T(8,128)(2,1)} %all-to-all-done.1), kind=kOutput, calls=%fused_computation.21 | convolution fusion | flops 541097984 | bytes 8454144 | tf_op jit(solution)/shard_map/dot_general | solution.py:132
  200.5 0.0 copy-start.2
  200.5 0.7 fusion.22
  201.2 1.4 copy-done.2
  202.7 0.0 copy-start.5
  202.7 1.5 fusion.23
  204.2 0.0 copy-done.5
  204.2 3.7 %fusion.3 = f32[128,8192]{1,0:T(8,128)S(1)} fusion(f32[128,8192]{1,0:T(8,128)S(1)} %fusion.22, bf16[128,256]{1,0:T(8,128)(2,1)S(1)} %fusion.16, bf16[256,8192]{1,0:T(8,128)(2,1)} %collective-permute-done.1, bf16[128,8192]{1,0:T(8,128)(2,1)S(1)} %copy-done, f32[8192]{0:T(1024)S(1)} %copy-done.5), kind=kOutput, calls=%fused_computation.5 | convolution fusion | flops 542113792 | bytes 14778368 | tf_op jit(solution)/shard_map/dot_general | solution.py:125
  207.9 3.8 %fusion.10 = bf16[16,64,8,128]{3,2,1,0:T(8,128)(2,1)S(1)} fusion(f32[128,8192]{1,0:T(8,128)S(1)} %fusion.3, f32[128,8192]{1,0:T(8,128)S(1)} %fusion.23, bf16[128,256]{1,0:T(8,128)(2,1)S(1)} %convolution_convert_fusion, bf16[8192,256]{1,0:T(8,128)(2,1)} %collective-permute-done), kind=kOutput, calls=%fused_computation.16 | convolution fusion | flops 540016640 | bytes 14745600 | tf_op jit(solution)/shard_map/dot_general | solution.py:138
  211.7 0.6 copy.31
  212.3 46.4 %all_to_all.50 = bf16[128,64,128]{2,0,1:T(8,128)(2,1)S(1)} all-to-all(bf16[128,64,128]{2,0,1:T(8,128)(2,1)S(1)} %bitcast.51), channel_id=1, replica_groups=mesh['dp'=64,'fsdp'=4] {'dp'}, dimensions={1} | all-to-all | bytes 4194304 | tf_op jit(solution)/shard_map/all_to_all | solution.py:140
  258.6 2.5 convert_element_type.48
  261.1 41.7 %shard_map.74 = bf16[8192,128]{1,0:T(8,128)(2,1)} custom-call(s32[32768]{0:T(1024)} %reshape.22.ids_ref, f32[8192,128]{1,0:T(8,128)} %bitcast.49), custom_call_target="tpu_custom_call" | custom-call | tf_op jit(solution)/shard_map/pallas_call | solution.py:71
  302.9 53.1 %all_to_all.51 = bf16[4,2048,128]{2,1,0:T(8,128)(2,1)S(1)} all-to-all(bf16[4,2048,128]{2,1,0:T(8,128)(2,1)} %bitcast.50), channel_id=1, replica_groups=mesh['dp'=64,'fsdp'=4] {'fsdp'}, dimensions={0} | all-to-all | bytes 4194304 | tf_op jit(solution)/shard_map/all_to_all | solution.py:145
  356.0 1.3 convert_reduce_fusion
  (1 shorter events, 0.0 us)
Async XLA Ops:
  6.5 4.9 %copy-start.4 = (s32[128,64,4]{0,2,1:T(4,128)S(1)}, s32[128,64,4]{0,2,1:T(4,128)}, u32[]{:S(2)}) copy-start(s32[128,64,4]{0,2,1:T(4,128)} %param.7) | copy-start | bytes 393220
  6.5 4.9 %copy-start.6 = (s32[128,64]{0,1:T(8,128)S(1)}, s32[128,64]{0,1:T(8,128)}, u32[]{:S(2)}) copy-start(s32[128,64]{0,1:T(8,128)} %param.8) | copy-start | bytes 98308
  6.5 16.0 %copy-start.3 = (bf16[8192,128]{1,0:T(8,128)(2,1)S(1)}, bf16[8192,128]{1,0:T(8,128)(2,1)}, u32[]{:S(2)}) copy-start(bf16[8192,128]{1,0:T(8,128)(2,1)} %param.9) | copy-start | bytes 6291460
  6.5 80.3 %all-gather.3.cloned.1.call-start = ((), (), s32[]{:S(2)}) async-start(), calls=%async_computation.4 | async-start | bytes 5242880 | tf_op jit(solution)/shard_map/all_gather | solution.py:99
  9.0 175.6 %all-gather.5.cloned.1.call-start = ((), (), s32[]{:S(2)}) async-start(), calls=%async_computation.5 | async-start | bytes 5242880 | tf_op jit(solution)/shard_map/all_gather | solution.py:100
  12.2 18.9 %all-to-all-start = ((s32[128,64,4]{0,2,1:T(4,128)}), s32[128,64,4]{0,2,1:T(4,128)S(1)}, u32[]{:S(2)}, u32[]{:S(2)}) async-start(s32[128,64,4]{0,2,1:T(4,128)} %fusion.21), calls=%async_computation | async-start | bytes 262144 | tf_op jit(solution)/shard_map/all_to_all | solution.py:108
  81.5 103.8 %all-to-all-start.1 = ((bf16[64,128,128]{2,1,0:T(8,128)(2,1)}), bf16[64,128,128]{2,1,0:T(8,128)(2,1)}, u32[]{:S(2)}, u32[]{:S(2)}) async-start(bf16[64,128,128]{2,1,0:T(8,128)(2,1)} %bitcast.52), calls=%async_computation.1 | async-start | bytes 4194304 | tf_op jit(solution)/shard_map/all_to_all | solution.py:116
  86.9 102.1 %copy-start = (bf16[128,8192]{1,0:T(8,128)(2,1)S(1)}, bf16[128,8192]{1,0:T(8,128)(2,1)}, u32[]{:S(2)}) copy-start(bf16[128,8192]{1,0:T(8,128)(2,1)} %param.13) | copy-start | bytes 6291460
  86.9 105.7 %collective-permute-start = (bf16[8192,256]{1,0:T(8,128)(2,1)}, bf16[8192,256]{1,0:T(8,128)(2,1)}, u32[]{:S(2)}, u32[]{:S(2)}) collective-permute-start(bf16[8192,256]{1,0:T(8,128)(2,1)} %all-gather.3.cloned.1.call-done), channel_id=1, source_target_pairs={{0,4},{4,0},{8,12},{12,8},{16,20},{20,16},{24,28},{28,24},{32,36},... | collective-permute-start | bytes 12582920 | tf_op jit(solution)/shard_map/ppermute | solution.py:102
  184.6 11.6 %collective-permute-start.1 = (bf16[256,8192]{1,0:T(8,128)(2,1)}, bf16[256,8192]{1,0:T(8,128)(2,1)}, u32[]{:S(2)}, u32[]{:S(2)}) collective-permute-start(bf16[256,8192]{1,0:T(8,128)(2,1)} %all-gather.5.cloned.1.call-done), channel_id=1, source_target_pairs={{0,4},{4,0},{8,12},{12,8},{16,20},{20,16},{24,28},{28,24},{32,36},... | collective-permute-start | bytes 12582920 | tf_op jit(solution)/shard_map/ppermute | solution.py:103
  185.3 4.0 %copy-start.1 = (bf16[256,8192]{1,0:T(8,128)(2,1)S(1)}, bf16[256,8192]{1,0:T(8,128)(2,1)}, u32[]{:S(2)}) copy-start(bf16[256,8192]{1,0:T(8,128)(2,1)} %all-gather.5.cloned.1.call-done) | copy-start | bytes 12582916
  200.5 2.2 copy-start.2
  202.7 1.5 copy-start.5
Sparse Core Ops, SparseCore 0:
  9.2 76.0 all-gather.2
  87.1 97.4 all-gather.4

commit v8 on v3

--- a/solution.py
+++ b/solution.py
@@ -49,25 +49,29 @@
     for a in accs:
         a[...] = jnp.zeros(a.shape, jnp.float32)
 
-    def body(s2, carry):
-        for k in range(2):
-            s = s2 * 2 + k
-            row = g_ref[pl.ds(s, 1), :]
+    tile_rows = 16
+
+    def body(t, carry):
+        tile = g_ref[pl.ds(pl.multiple_of(t * tile_rows, tile_rows), tile_rows), :]
+        tile = tile.astype(jnp.float32)
+        for k in range(tile_rows):
+            s = t * tile_rows + k
+            row = tile[k:k + 1, :]
             for h in range(slots):
-                a = accs[(k * slots + h) % nacc]
+                a = accs[((k % 2) * slots + h) % nacc]
                 idx = ids_ref[s * slots + h]
                 a[pl.ds(idx, 1), :] = a[pl.ds(idx, 1), :] + row
         return carry
 
-    lax.fori_loop(0, count // 2, body, 0, unroll=4)
+    lax.fori_loop(0, count // tile_rows, body, 0)
     total = accs[0][pl.ds(0, rows), :]
     for a in accs[1:]:
         total = total + a[pl.ds(0, rows), :]
     out_ref[...] = total.astype(out_ref.dtype)
 
 
-def scatter_rows(ids_flat, g_f32, rows, slots):
-    count, width = g_f32.shape
+def scatter_rows(ids_flat, grads, rows, slots):
+    count, width = grads.shape
     return pl.pallas_call(
         functools.partial(scatter_kernel, slots=slots),
         grid_spec=pltpu.PrefetchScalarGridSpec(
@@ -82,7 +86,7 @@
         ),
         out_shape=jax.ShapeDtypeStruct((rows, width), jnp.bfloat16),
         compiler_params=pltpu.CompilerParams(vmem_limit_bytes=62 * 1024 * 1024),
-    )(ids_flat, g_f32)
+    )(ids_flat, grads)
 
 
 def on_device(bag_ids, bag_counts, emb_table, cross_down, cross_up, cross_bias, cotangent):
@@ -139,7 +143,7 @@
     grad_pooled = (upstream * (gate_value + 1.0) + back_term).astype(jnp.bfloat16)
     grad_local = lax.all_to_all(grad_pooled, "dp", split_axis=1, concat_axis=0, tiled=True)
     partial_value = scatter_rows(
-        ids_flat, grad_local.astype(jnp.float32), vocab_rows, slot_count
+        ids_flat, grad_local, vocab_rows, slot_count
     )
     summed = lax.psum_scatter(
         partial_value, "fsdp", scatter_dimension=0, tiled=True

time: 356 us -> 352 us (0.989)
  no operation moved by 1% of the time
where the time goes in v8:
time: 352 us; the launch traced here: 351 us
  waiting for transfers between devices  148 us (42%)
  Pallas kernels  81.7 us (23%)
  blocking collectives  46.5 us (13%)
  matrix products  24.5 us (7%)
  starting transfers between devices  17.2 us (5%)
  local copies, waits for them, and re-layouts  15.3 us (4%)
  between operations  13.3 us (4%)
  other arithmetic  5.06 us (1%)
    all_gather x1, waiting for transfers between devices, on_device(): up_mine = lax.all_gather(up_mine, 'fsdp', axis=1, tiled=True)  93.3 us
    all_to_all x1, blocking collectives, on_device(): lax.all_to_all(grad_pooled, 'dp', split_axis=1, concat_axis=0, tiled=True)  46.5 us
    reduce_scatter x1, waiting for transfers between devices, on_device(): lax.psum_scatter(partial_value, 'fsdp', scatter_dimension=0, tiled=True)  44.3 us
    pallas_call x1, Pallas kernels, pool_rows(): pl.pallas_call(functools.partial(pool_kernel, blk=blk, slots=slots), grid...  42.4 us
    pallas_call x1, Pallas kernels, scatter_rows(): pl.pallas_call(functools.partial(scatter_kernel, slots=slots), grid_spec=...  39.4 us
    all_to_all x1, starting transfers between devices, on_device(): lax.all_to_all(send_ids, 'dp', split_axis=1, concat_axis=0, tiled=True)  10.3 us
  transfers between devices with their start and end apart: 7, of which 4 were waited for; matrix products, arithmetic and copies ran while one was open for 7% of the time, Pallas kernels for 12%

profile of v8, /device:TPU:1, one launch (start us, length us, event | category | flops | bytes accessed | tf_op | source)
XLA Modules:
  0.0 351.0 jit_solution(8504490835857674480)
XLA Ops:
  6.5 0.0 copy-start.4
  6.5 0.0 copy-start.6
  6.5 0.0 copy-start.3
  6.5 0.0 all-gather.3.cloned.1.call-start
  6.5 2.4 constant_dynamic-slice_fusion.1
  9.0 0.0 all-gather.3.cloned.1.call-update
  9.0 0.0 all-gather.5.cloned.1.call-start
  9.0 2.4 constant_dynamic-slice_fusion
  11.4 0.0 all-gather.5.cloned.1.call-update
  11.5 0.0 copy-done.4
  11.5 0.0 copy-done.6
  11.5 0.7 fusion.21
  12.2 10.3 %all-to-all-start = ((s32[128,64,4]{0,2,1:T(4,128)}), s32[128,64,4]{0,2,1:T(4,128)S(1)}, u32[]{:S(2)}, u32[]{:S(2)}) async-start(s32[128,64,4]{0,2,1:T(4,128)} %fusion.21), calls=%async_computation | async-start | bytes 262144 | tf_op jit(solution)/shard_map/all_to_all | solution.py:112
  22.5 0.0 copy-done.3
  22.5 2.3 pad_convert_fusion.tab_ref
  24.8 6.2 %all-to-all-done = s32[128,64,4]{0,2,1:T(4,128)S(1)} async-done(((s32[128,64,4]{0,2,1:T(4,128)}), s32[128,64,4]{0,2,1:T(4,128)S(1)}, u32[]{:S(2)}, u32[]{:S(2)}) %all-to-all-start) | async-done | bytes 131104 | tf_op jit(solution)/shard_map/all_to_all | solution.py:112
  31.1 2.6 copy.10
  33.7 5.5 %reshape.17.ids_ref = s32[32768]{0:T(1024)} reshape(s32[64,128,4]{2,1,0:T(8,128)} %copy.10) | data formatting | bytes 262144 | tf_op jit(solution)/shard_map/reshape | solution.py:114
  39.2 42.4 %shard_map.73 = bf16[8192,128]{1,0:T(8,128)(2,1)} custom-call(s32[32768]{0:T(1024)} %reshape.17.ids_ref, f32[8200,128]{1,0:T(8,128)} %pad_convert_fusion.tab_ref), custom_call_target="tpu_custom_call" | custom-call | tf_op jit(solution)/shard_map/pallas_call | solution.py:32
  81.5 5.3 %all-to-all-start.1 = ((bf16[64,128,128]{2,1,0:T(8,128)(2,1)}), bf16[64,128,128]{2,1,0:T(8,128)(2,1)}, u32[]{:S(2)}, u32[]{:S(2)}) async-start(bf16[64,128,128]{2,1,0:T(8,128)(2,1)} %bitcast.50), calls=%async_computation.1 | async-start | bytes 4194304 | tf_op jit(solution)/shard_map/all_to_all | solution.py:120
  86.9 0.0 copy-start
  86.9 0.0 reduce-scatter.2.cloned.1.call-start
  86.9 3.6 %all-gather.3.cloned.1.call-done = bf16[8192,256]{1,0:T(8,128)(2,1)} async-done(((bf16[2048,256]{1,0:T(8,128)(2,1)}), bf16[8192,256]{1,0:T(8,128)(2,1)}) %all-gather.3.cloned.1.call-update) | async-done | bytes 4194320 | tf_op jit(solution)/shard_map/all_gather | solution.py:103
  90.6 0.7 collective-permute-start
  91.3 93.3 %all-gather.5.cloned.1.call-done = bf16[256,8192]{1,0:T(8,128)(2,1)} async-done(((bf16[256,2048]{1,0:T(8,128)(2,1)}), bf16[256,8192]{1,0:T(8,128)(2,1)}) %all-gather.5.cloned.1.call-update) | async-done | bytes 4194320 | tf_op jit(solution)/shard_map/all_gather | solution.py:104
  184.6 0.7 collective-permute-start.1
  185.3 0.0 all-to-all-done.1
  185.3 3.7 %fusion.13 = bf16[128,256]{1,0:T(8,128)(2,1)S(1)} fusion(bf16[8192,256]{1,0:T(8,128)(2,1)} %all-gather.3.cloned.1.call-done, bf16[64,128,128]{2,1,0:T(8,128)(2,1)} %all-to-all-done.1), kind=kOutput, calls=%fused_computation.18 | convolution fusion | flops 536903680 | bytes 6356992 | tf_op jit(solution)/shard_map/dot_general | solution.py:124
  189.0 0.0 copy-done
  189.0 0.3 copy-done.1
  189.3 3.2 convolution_convert_fusion.1
  192.6 0.0 collective-permute-done
  192.6 3.5 %fusion.16 = bf16[128,256]{1,0:T(8,128)(2,1)S(1)} fusion(bf16[8192,256]{1,0:T(8,128)(2,1)} %collective-permute-done, bf16[64,128,128]{2,1,0:T(8,128)(2,1)} %all-to-all-done.1), kind=kOutput, calls=%fused_computation.19 | convolution fusion | flops 536903680 | bytes 6356992 | tf_op jit(solution)/shard_map/dot_general | solution.py:125
  196.1 0.0 collective-permute-done.1
  196.1 4.4 %convolution_convert_fusion = bf16[128,256]{1,0:T(8,128)(2,1)S(1)} fusion(bf16[256,8192]{1,0:T(8,128)(2,1)} %collective-permute-done.1, bf16[128,8192]{1,0:T(8,128)(2,1)S(1)} %copy-done, bf16[64,128,128]{2,1,0:T(8,128)(2,1)} %all-to-all-done.1), kind=kOutput, calls=%fused_computation.20 | convolution fusion | flops 541097984 | bytes 8454144 | tf_op jit(solution)/shard_map/dot_general | solution.py:136
  200.5 0.0 copy-start.2
  200.5 0.7 fusion.22
  201.2 1.4 copy-done.2
  202.7 1.5 fusion.23
  204.2 0.0 copy-done.5
  204.2 3.7 %fusion.3 = f32[128,8192]{1,0:T(8,128)S(1)} fusion(f32[128,8192]{1,0:T(8,128)S(1)} %fusion.22, bf16[128,256]{1,0:T(8,128)(2,1)S(1)} %fusion.16, bf16[256,8192]{1,0:T(8,128)(2,1)} %collective-permute-done.1, bf16[128,8192]{1,0:T(8,128)(2,1)S(1)} %copy-done, f32[8192]{0:T(1024)S(1)} %copy-done.5), kind=kOutput, calls=%fused_computation.5 | convolution fusion | flops 542113792 | bytes 14778368 | tf_op jit(solution)/shard_map/dot_general | solution.py:129
  207.9 3.8 %fusion.10 = bf16[16,64,8,128]{3,2,1,0:T(8,128)(2,1)S(1)} fusion(f32[128,8192]{1,0:T(8,128)S(1)} %fusion.3, f32[128,8192]{1,0:T(8,128)S(1)} %fusion.23, bf16[128,256]{1,0:T(8,128)(2,1)S(1)} %convolution_convert_fusion, bf16[8192,256]{1,0:T(8,128)(2,1)} %collective-permute-done), kind=kOutput, calls=%fused_computation.15 | convolution fusion | flops 540016640 | bytes 14745600 | tf_op jit(solution)/shard_map/dot_general | solution.py:142
  211.7 0.6 copy.31
  212.3 46.5 %all_to_all.51 = bf16[128,64,128]{2,0,1:T(8,128)(2,1)} all-to-all(bf16[128,64,128]{2,0,1:T(8,128)(2,1)S(1)} %bitcast.49), channel_id=1, replica_groups=mesh['dp'=64,'fsdp'=4] {'dp'}, dimensions={1} | all-to-all | bytes 4194304 | tf_op jit(solution)/shard_map/all_to_all | solution.py:144
  258.8 39.4 %shard_map.74 = bf16[8192,128]{1,0:T(8,128)(2,1)} custom-call(s32[32768]{0:T(1024)} %reshape.17.ids_ref, bf16[8192,128]{1,0:T(8,128)(2,1)} %bitcast.48), custom_call_target="tpu_custom_call" | custom-call | tf_op jit(solution)/shard_map/pallas_call | solution.py:75
  298.1 0.0 reduce-scatter.2.cloned.1.call-update
  298.1 44.3 %reduce-scatter.2.cloned.1.call-done = bf16[2048,128]{1,0:T(8,128)(2,1)} async-done(((bf16[8192,128]{1,0:T(8,128)(2,1)}), bf16[2048,128]{1,0:T(8,128)(2,1)}) %reduce-scatter.2.cloned.1.call-update) | async-done | bytes 524304 | tf_op jit(solution)/shard_map/reduce_scatter | solution.py:148
  342.4 2.1 convert_element_type.36
  (2 shorter events, 0.0 us)
Async XLA Ops:
  6.5 4.9 %copy-start.4 = (s32[128,64,4]{0,2,1:T(4,128)S(1)}, s32[128,64,4]{0,2,1:T(4,128)}, u32[]{:S(2)}) copy-start(s32[128,64,4]{0,2,1:T(4,128)} %param.7) | copy-start | bytes 393220
  6.5 4.9 %copy-start.6 = (s32[128,64]{0,1:T(8,128)S(1)}, s32[128,64]{0,1:T(8,128)}, u32[]{:S(2)}) copy-start(s32[128,64]{0,1:T(8,128)} %param.8) | copy-start | bytes 98308
  6.5 16.0 %copy-start.3 = (bf16[8192,128]{1,0:T(8,128)(2,1)S(1)}, bf16[8192,128]{1,0:T(8,128)(2,1)}, u32[]{:S(2)}) copy-start(bf16[8192,128]{1,0:T(8,128)(2,1)} %param.9) | copy-start | bytes 6291460
  6.5 84.0 %all-gather.3.cloned.1.call-start = ((), (), s32[]{:S(2)}) async-start(), calls=%async_computation.4 | async-start | bytes 5242880 | tf_op jit(solution)/shard_map/all_gather | solution.py:103
  9.0 175.6 %all-gather.5.cloned.1.call-start = ((), (), s32[]{:S(2)}) async-start(), calls=%async_computation.5 | async-start | bytes 5242880 | tf_op jit(solution)/shard_map/all_gather | solution.py:104
  12.2 18.9 %all-to-all-start = ((s32[128,64,4]{0,2,1:T(4,128)}), s32[128,64,4]{0,2,1:T(4,128)S(1)}, u32[]{:S(2)}, u32[]{:S(2)}) async-start(s32[128,64,4]{0,2,1:T(4,128)} %fusion.21), calls=%async_computation | async-start | bytes 262144 | tf_op jit(solution)/shard_map/all_to_all | solution.py:112
  81.5 103.8 %all-to-all-start.1 = ((bf16[64,128,128]{2,1,0:T(8,128)(2,1)}), bf16[64,128,128]{2,1,0:T(8,128)(2,1)}, u32[]{:S(2)}, u32[]{:S(2)}) async-start(bf16[64,128,128]{2,1,0:T(8,128)(2,1)} %bitcast.50), calls=%async_computation.1 | async-start | bytes 4194304 | tf_op jit(solution)/shard_map/all_to_all | solution.py:120
  86.9 102.1 %copy-start = (bf16[128,8192]{1,0:T(8,128)(2,1)S(1)}, bf16[128,8192]{1,0:T(8,128)(2,1)}, u32[]{:S(2)}) copy-start(bf16[128,8192]{1,0:T(8,128)(2,1)} %param.13) | copy-start | bytes 6291460
  86.9 255.6 %reduce-scatter.2.cloned.1.call-start = ((), (), s32[]{:S(2)}) async-start(), calls=%async_computation.6 | async-start | bytes 2621440 | tf_op jit(solution)/shard_map/reduce_scatter | solution.py:148
  90.6 102.0 %collective-permute-start = (bf16[8192,256]{1,0:T(8,128)(2,1)}, bf16[8192,256]{1,0:T(8,128)(2,1)}, u32[]{:S(2)}, u32[]{:S(2)}) collective-permute-start(bf16[8192,256]{1,0:T(8,128)(2,1)} %all-gather.3.cloned.1.call-done), channel_id=1, source_target_pairs={{0,4},{4,0},{8,12},{12,8},{16,20},{20,16},{24,28},{28,24},{32,36},... | collective-permute-start | bytes 12582920 | tf_op jit(solution)/shard_map/ppermute | solution.py:106
  184.6 11.6 %collective-permute-start.1 = (bf16[256,8192]{1,0:T(8,128)(2,1)}, bf16[256,8192]{1,0:T(8,128)(2,1)}, u32[]{:S(2)}, u32[]{:S(2)}) collective-permute-start(bf16[256,8192]{1,0:T(8,128)(2,1)} %all-gather.5.cloned.1.call-done), channel_id=1, source_target_pairs={{0,4},{4,0},{8,12},{12,8},{16,20},{20,16},{24,28},{28,24},{32,36},... | collective-permute-start | bytes 12582920 | tf_op jit(solution)/shard_map/ppermute | solution.py:107
  185.3 4.0 %copy-start.1 = (bf16[256,8192]{1,0:T(8,128)(2,1)S(1)}, bf16[256,8192]{1,0:T(8,128)(2,1)}, u32[]{:S(2)}) copy-start(bf16[256,8192]{1,0:T(8,128)(2,1)} %all-gather.5.cloned.1.call-done) | copy-start | bytes 12582916
  200.5 2.2 copy-start.2
  202.7 1.5 copy-start.5
Sparse Core Ops, SparseCore 0:
  9.2 81.3 all-gather.2
  92.4 92.1 all-gather.4
  298.3 44.1 reduce-scatter.1

commit v9 on v8

--- a/solution.py
+++ b/solution.py
@@ -99,12 +99,15 @@
     dp_idx = lax.axis_index("dp")
     core = dp_idx % 2
     down_mine = lax.dynamic_slice_in_dim(cross_down, core * half, half, 1)
-    up_mine = lax.dynamic_slice_in_dim(cross_up, core * half, half, 0)
+    quarter = half // 2
     down_mine = lax.all_gather(down_mine, "fsdp", axis=0, tiled=True)
-    up_mine = lax.all_gather(up_mine, "fsdp", axis=1, tiled=True)
     partner = [(i, i ^ 1) for i in range(dp_size)]
     down_other = lax.ppermute(down_mine, "dp", partner)
-    up_other = lax.ppermute(up_mine, "dp", partner)
+    up_parts = []
+    for q in range(2):
+        piece = lax.dynamic_slice_in_dim(cross_up, core * half + q * quarter, quarter, 0)
+        piece = lax.all_gather(piece, "fsdp", axis=1, tiled=True)
+        up_parts.append((piece, lax.ppermute(piece, "dp", partner)))
 
     slot_iota = lax.broadcasted_iota(jnp.int32, bag_ids.shape, 2)
     live_ids = jnp.where(slot_iota < bag_counts[:, :, None], bag_ids, vocab_rows)
@@ -124,18 +127,24 @@
     low_mine = jnp.dot(pooled, down_mine, preferred_element_type=jnp.float32).astype(jnp.bfloat16)
     low_other = jnp.dot(pooled, down_other, preferred_element_type=jnp.float32).astype(jnp.bfloat16)
     low_mine, low_other = lax.optimization_barrier((low_mine, low_other))
-    gate_value = (
-        jnp.dot(low_mine, up_mine, preferred_element_type=jnp.float32)
-        + jnp.dot(low_other, up_other, preferred_element_type=jnp.float32)
-        + cross_bias
-    )
     contract = (((1,), (1,)), ((), ()))
-    grad_low_mine = lax.dot_general(
-        grad_gate, up_mine, contract, preferred_element_type=jnp.float32
-    ).astype(jnp.bfloat16)
-    grad_low_other = lax.dot_general(
-        grad_gate, up_other, contract, preferred_element_type=jnp.float32
-    ).astype(jnp.bfloat16)
+    gate_value = cross_bias
+    grad_low_mine, grad_low_other = [], []
+    for q, (up_q_mine, up_q_other) in enumerate(up_parts):
+        cols = slice(q * quarter, (q + 1) * quarter)
+        gate_value = (
+            gate_value
+            + jnp.dot(low_mine[:, cols], up_q_mine, preferred_element_type=jnp.float32)
+            + jnp.dot(low_other[:, cols], up_q_other, preferred_element_type=jnp.float32)
+        )
+        grad_low_mine.append(lax.dot_general(
+            grad_gate, up_q_mine, contract, preferred_element_type=jnp.float32
+        ).astype(jnp.bfloat16))
+        grad_low_other.append(lax.dot_general(
+            grad_gate, up_q_other, contract, preferred_element_type=jnp.float32
+        ).astype(jnp.bfloat16))
+    grad_low_mine = jnp.concatenate(grad_low_mine, axis=1)
+    grad_low_other = jnp.concatenate(grad_low_other, axis=1)
     grad_low_mine, grad_low_other = lax.optimization_barrier((grad_low_mine, grad_low_other))
     back_term = lax.dot_general(
         grad_low_mine, down_mine, contract, preferred_element_type=jnp.float32

time: 352 us -> 373 us (1.060)
  waiting for transfers between devices: 148 us -> 166 us
    all_gather x1, waiting for transfers between devices: 3.65 us -> 77.3 us  [on_device(): down_mine = lax.all_gather(down_mine, 'fsdp', axis=0, tiled=True)]
    all_gather x1 -> x2, waiting for transfers between devices: 93.3 us -> 37 us  [on_device(): piece = lax.all_gather(piece, 'fsdp', axis=1, tiled=True)]
    dot_general x4 -> x8, matrix products: 12 us -> 13.1 us  [the longest x2 5.57 us: on_device(): jnp.dot(low_other[:, cols], up_q_other, preferred_element_type=jnp.float32)]
  transfers between devices with their start and end apart: 7 -> 9, of which waited for: 4 -> 4; matrix products, arithmetic and copies ran while one was open for 7% -> 7% of each run, Pallas kernels for 12% -> 11%
where the time goes in v9:
time: 373 us; the launch traced here: 372 us
  waiting for transfers between devices  166 us (45%)
  Pallas kernels  81.7 us (22%)
  blocking collectives  46.5 us (12%)
  matrix products  24.3 us (7%)
  starting transfers between devices  18.5 us (5%)
  local copies, waits for them, and re-layouts  14.6 us (4%)
  between operations  13.4 us (4%)
  other arithmetic  7.19 us (2%)
    all_gather x1, waiting for transfers between devices, on_device(): down_mine = lax.all_gather(down_mine, 'fsdp', axis=0, tiled=True)  77.3 us
    all_to_all x1, blocking collectives, on_device(): lax.all_to_all(grad_pooled, 'dp', split_axis=1, concat_axis=0, tiled=True)  46.5 us
    reduce_scatter x1, waiting for transfers between devices, on_device(): lax.psum_scatter(partial_value, 'fsdp', scatter_dimension=0, tiled=True)  44.3 us
    pallas_call x1, Pallas kernels, pool_rows(): pl.pallas_call(functools.partial(pool_kernel, blk=blk, slots=slots), grid...  42.4 us
    pallas_call x1, Pallas kernels, scatter_rows(): pl.pallas_call(functools.partial(scatter_kernel, slots=slots), grid_spec=...  39.4 us
    all_gather x2, waiting for transfers between devices, on_device(): piece = lax.all_gather(piece, 'fsdp', axis=1, tiled=True)  37 us
    all_to_all x1, starting transfers between devices, on_device(): lax.all_to_all(send_ids, 'dp', split_axis=1, concat_axis=0, tiled=True)  10.3 us
  transfers between devices with their start and end apart: 9, of which 4 were waited for; matrix products, arithmetic and copies ran while one was open for 7% of the time, Pallas kernels for 11%

profile of v9, /device:TPU:1, one launch (start us, length us, event | category | flops | bytes accessed | tf_op | source)
XLA Modules:
  0.0 371.9 jit_solution(1483582001348116610)
XLA Ops:
  6.5 2.3 constant_dynamic-slice_fusion.1
  8.8 0.0 all-gather.8.cloned.1.call-update
  8.9 0.0 all-gather.6.cloned.1.call-start
  8.9 0.0 copy-start.4
  8.9 0.7 all-gather.6.cloned.1.call-update
  9.6 0.0 all-gather.4.cloned.1.call-start
  9.7 2.3 constant_dynamic-slice_fusion.2
  11.9 0.0 all-gather.4.cloned.1.call-update
  12.0 0.7 fusion.19
  12.7 10.3 %all-to-all-start = ((s32[128,64,4]{0,2,1:T(4,128)}), s32[128,64,4]{0,2,1:T(4,128)S(1)}, u32[]{:S(2)}, u32[]{:S(2)}) async-start(s32[128,64,4]{0,2,1:T(4,128)} %fusion.19), calls=%async_computation | async-start | bytes 262144 | tf_op jit(solution)/shard_map/all_to_all | solution.py:115
  23.0 2.2 pad_convert_fusion.tab_ref
  25.2 6.4 %all-to-all-done = s32[128,64,4]{0,2,1:T(4,128)S(1)} async-done(((s32[128,64,4]{0,2,1:T(4,128)}), s32[128,64,4]{0,2,1:T(4,128)S(1)}, u32[]{:S(2)}, u32[]{:S(2)}) %all-to-all-start) | async-done | bytes 131104 | tf_op jit(solution)/shard_map/all_to_all | solution.py:115
  31.6 2.7 copy.10
  34.2 5.5 %reshape.17.ids_ref = s32[32768]{0:T(1024)} reshape(s32[64,128,4]{2,1,0:T(8,128)} %copy.10) | data formatting | bytes 262144 | tf_op jit(solution)/shard_map/reshape | solution.py:117
  39.7 42.4 %shard_map.73 = bf16[8192,128]{1,0:T(8,128)(2,1)} custom-call(s32[32768]{0:T(1024)} %reshape.17.ids_ref, f32[8200,128]{1,0:T(8,128)} %pad_convert_fusion.tab_ref), custom_call_target="tpu_custom_call" | custom-call | tf_op jit(solution)/shard_map/pallas_call | solution.py:32
  82.1 5.5 %all-to-all-start.1 = ((bf16[64,128,128]{2,1,0:T(8,128)(2,1)}), bf16[64,128,128]{2,1,0:T(8,128)(2,1)}, u32[]{:S(2)}, u32[]{:S(2)}) async-start(bf16[64,128,128]{2,1,0:T(8,128)(2,1)} %bitcast.50), calls=%async_computation.1 | async-start | bytes 4194304 | tf_op jit(solution)/shard_map/all_to_all | solution.py:123
  87.6 0.0 reduce-scatter.2.cloned.1.call-start
  87.6 0.0 all-gather.8.cloned.1.call-done
  87.6 0.7 collective-permute-start.2
  88.4 37.0 %all-gather.6.cloned.1.call-done = bf16[128,8192]{1,0:T(8,128)(2,1)} async-done(((bf16[128,2048]{1,0:T(8,128)(2,1)}), bf16[128,8192]{1,0:T(8,128)(2,1)}) %all-gather.6.cloned.1.call-update) | async-done | bytes 2097168 | tf_op jit(solution)/shard_map/all_gather | solution.py:109
  125.4 1.2 collective-permute-start.1
  126.5 77.3 %all-gather.4.cloned.1.call-done = bf16[8192,256]{1,0:T(8,128)(2,1)} async-done(((bf16[2048,256]{1,0:T(8,128)(2,1)}), bf16[8192,256]{1,0:T(8,128)(2,1)}) %all-gather.4.cloned.1.call-update) | async-done | bytes 4194320 | tf_op jit(solution)/shard_map/all_gather | solution.py:103
  203.9 0.7 collective-permute-start
  204.6 2.2 fusion.5
  206.8 0.7 convolution_convert_fusion.2
  207.5 0.9 copy-done.2
  208.4 0.7 convolution_convert_fusion.3
  209.1 0.0 collective-permute-done.2
  209.1 2.3 convolution_convert_fusion
  211.5 0.0 collective-permute-done.1
  211.5 2.4 convolution_convert_fusion.1
  213.9 0.3 copy-done.3
  214.3 2.3 fusion.13
  216.6 1.5 fusion.25
  218.1 3.5 fusion.16
  221.7 0.0 copy-start.6
  221.7 0.7 fusion.21
  222.4 0.1 copy-done.6
  222.4 0.7 convolution_add_fusion.3
  223.1 3.8 %convolution_add_fusion = f32[128,8192]{1,0:T(8,128)S(1)} fusion(f32[128,8192]{1,0:T(8,128)S(1)} %fusion.25, bf16[128,256]{0,1:T(8,128)(2,1)S(1)} %pad_maximum_fusion.1, bf16[8192,256]{1,0:T(8,128)(2,1)} %collective-permute-done), kind=kOutput, calls=%fused_computation | convolution fusion | flops 537919488 | bytes 12648448 | tf_op jit(solution)/shard_map/dot_general | solution.py:151
  226.9 2.5 fusion.1
  229.4 3.1 fusion.10
  232.5 0.6 copy.29
  233.1 46.5 %all_to_all.51 = bf16[128,64,128]{2,0,1:T(8,128)(2,1)} all-to-all(bf16[128,64,128]{2,0,1:T(8,128)(2,1)S(1)} %bitcast.49), channel_id=1, replica_groups=mesh['dp'=64,'fsdp'=4] {'dp'}, dimensions={1} | all-to-all | bytes 4194304 | tf_op jit(solution)/shard_map/all_to_all | solution.py:153
  279.6 39.4 %shard_map.74 = bf16[8192,128]{1,0:T(8,128)(2,1)} custom-call(s32[32768]{0:T(1024)} %reshape.17.ids_ref, bf16[8192,128]{1,0:T(8,128)(2,1)} %bitcast.48), custom_call_target="tpu_custom_call" | custom-call | tf_op jit(solution)/shard_map/pallas_call | solution.py:75
  319.0 0.0 reduce-scatter.2.cloned.1.call-update
  319.0 44.3 %reduce-scatter.2.cloned.1.call-done = bf16[2048,128]{1,0:T(8,128)(2,1)} async-done(((bf16[8192,128]{1,0:T(8,128)(2,1)}), bf16[2048,128]{1,0:T(8,128)(2,1)}) %reduce-scatter.2.cloned.1.call-update) | async-done | bytes 524304 | tf_op jit(solution)/shard_map/reduce_scatter | solution.py:157
  363.3 2.1 convert_element_type.44
  (16 shorter events, 0.0 us)
Async XLA Ops:
  6.5 81.1 %all-gather.8.cloned.1.call-start = ((), (), s32[]{:S(2)}) async-start(), calls=%async_computation.6 | async-start | bytes 2621440 | tf_op jit(solution)/shard_map/all_gather | solution.py:109
  8.8 3.1 copy-start.5
  8.8 3.1 copy-start.7
  8.9 116.5 %all-gather.6.cloned.1.call-start = ((), (), s32[]{:S(2)}) async-start(), calls=%async_computation.5 | async-start | bytes 2621440 | tf_op jit(solution)/shard_map/all_gather | solution.py:109
  8.9 14.1 %copy-start.4 = (bf16[8192,128]{1,0:T(8,128)(2,1)S(1)}, bf16[8192,128]{1,0:T(8,128)(2,1)}, u32[]{:S(2)}) copy-start(bf16[8192,128]{1,0:T(8,128)(2,1)} %param.9) | copy-start | bytes 6291460
  9.6 194.3 %all-gather.4.cloned.1.call-start = ((), (), s32[]{:S(2)}) async-start(), calls=%async_computation.4 | async-start | bytes 5242880 | tf_op jit(solution)/shard_map/all_gather | solution.py:103
  12.7 18.9 %all-to-all-start = ((s32[128,64,4]{0,2,1:T(4,128)}), s32[128,64,4]{0,2,1:T(4,128)S(1)}, u32[]{:S(2)}, u32[]{:S(2)}) async-start(s32[128,64,4]{0,2,1:T(4,128)} %fusion.19), calls=%async_computation | async-start | bytes 262144 | tf_op jit(solution)/shard_map/all_to_all | solution.py:115
  82.1 122.5 %copy-start = (bf16[128,8192]{1,0:T(8,128)(2,1)S(1)}, bf16[128,8192]{1,0:T(8,128)(2,1)}, u32[]{:S(2)}) copy-start(bf16[128,8192]{1,0:T(8,128)(2,1)} %param.13) | copy-start | bytes 6291460
  82.1 122.5 %all-to-all-start.1 = ((bf16[64,128,128]{2,1,0:T(8,128)(2,1)}), bf16[64,128,128]{2,1,0:T(8,128)(2,1)}, u32[]{:S(2)}, u32[]{:S(2)}) async-start(bf16[64,128,128]{2,1,0:T(8,128)(2,1)} %bitcast.50), calls=%async_computation.1 | async-start | bytes 4194304 | tf_op jit(solution)/shard_map/all_to_all | solution.py:123
  87.6 275.7 %reduce-scatter.2.cloned.1.call-start = ((), (), s32[]{:S(2)}) async-start(), calls=%async_computation.7 | async-start | bytes 2621440 | tf_op jit(solution)/shard_map/reduce_scatter | solution.py:157
  87.6 121.5 %collective-permute-start.2 = (bf16[128,8192]{1,0:T(8,128)(2,1)}, bf16[128,8192]{1,0:T(8,128)(2,1)}, u32[]{:S(2)}, u32[]{:S(2)}) collective-permute-start(bf16[128,8192]{1,0:T(8,128)(2,1)} %all-gather.8.cloned.1.call-done), channel_id=1, source_target_pairs={{0,4},{4,0},{8,12},{12,8},{16,20},{20,16},{24,28},{28,24},{32,36},... | collective-permute-start | bytes 6291464 | tf_op jit(solution)/shard_map/ppermute | solution.py:110
  125.4 86.1 %collective-permute-start.1 = (bf16[128,8192]{1,0:T(8,128)(2,1)}, bf16[128,8192]{1,0:T(8,128)(2,1)}, u32[]{:S(2)}, u32[]{:S(2)}) collective-permute-start(bf16[128,8192]{1,0:T(8,128)(2,1)} %all-gather.6.cloned.1.call-done), channel_id=1, source_target_pairs={{0,4},{4,0},{8,12},{12,8},{16,20},{20,16},{24,28},{28,24},{32,36},... | collective-permute-start | bytes 6291464 | tf_op jit(solution)/shard_map/ppermute | solution.py:110
  203.9 14.3 %collective-permute-start = (bf16[8192,256]{1,0:T(8,128)(2,1)}, bf16[8192,256]{1,0:T(8,128)(2,1)}, u32[]{:S(2)}, u32[]{:S(2)}) collective-permute-start(bf16[8192,256]{1,0:T(8,128)(2,1)} %all-gather.4.cloned.1.call-done), channel_id=1, source_target_pairs={{0,4},{4,0},{8,12},{12,8},{16,20},{20,16},{24,28},{28,24},{32,36},... | collective-permute-start | bytes 12582920 | tf_op jit(solution)/shard_map/ppermute | solution.py:105
  204.6 2.3 copy-start.1
  206.8 1.6 copy-start.2
  211.4 2.8 copy-start.3
  221.7 0.8 copy-start.6
Sparse Core Ops, SparseCore 0:
  9.2 49.9 all-gather.7
  61.0 64.3 all-gather.5
  127.2 76.6 all-gather.3
  319.1 44.1 reduce-scatter.1

commit v10 on v8

--- a/solution.py
+++ b/solution.py
@@ -42,24 +42,32 @@
     )(ids_flat, table_f32)
 
 
-def scatter_kernel(ids_ref, g_ref, out_ref, *accs, slots):
+def scatter_kernel(ids_ref, g_ref, *rest, slots, per_source, run, offset, has_init):
+    if has_init:
+        init_ref, out_ref, *accs = rest
+    else:
+        out_ref, *accs = rest
     nacc = len(accs)
     count = g_ref.shape[0]
     rows = out_ref.shape[0]
     for a in accs:
         a[...] = jnp.zeros(a.shape, jnp.float32)
+    if has_init:
+        accs[0][pl.ds(0, rows), :] = init_ref[...]
 
     tile_rows = 16
+    tiles_per_source = per_source // tile_rows
 
     def body(t, carry):
         tile = g_ref[pl.ds(pl.multiple_of(t * tile_rows, tile_rows), tile_rows), :]
         tile = tile.astype(jnp.float32)
+        source = t // tiles_per_source
+        first = source * run + offset + (t % tiles_per_source) * tile_rows
         for k in range(tile_rows):
-            s = t * tile_rows + k
             row = tile[k:k + 1, :]
             for h in range(slots):
                 a = accs[((k % 2) * slots + h) % nacc]
-                idx = ids_ref[s * slots + h]
+                idx = ids_ref[(first + k) * slots + h]
                 a[pl.ds(idx, 1), :] = a[pl.ds(idx, 1), :] + row
         return carry
 
@@ -70,23 +78,33 @@
     out_ref[...] = total.astype(out_ref.dtype)
 
 
-def scatter_rows(ids_flat, grads, rows, slots):
+def scatter_rows(ids_flat, grads, rows, slots, per_source, run, offset, init=None):
     count, width = grads.shape
+    whole = lambda i, ids: (0, 0)
+    in_specs = [pl.BlockSpec((count, width), whole)]
+    operands = [ids_flat, grads]
+    if init is not None:
+        in_specs.append(pl.BlockSpec((rows, width), whole))
+        operands.append(init)
+    out_dtype = jnp.float32 if init is None else jnp.bfloat16
     return pl.pallas_call(
-        functools.partial(scatter_kernel, slots=slots),
+        functools.partial(
+            scatter_kernel, slots=slots, per_source=per_source, run=run, offset=offset,
+            has_init=init is not None,
+        ),
         grid_spec=pltpu.PrefetchScalarGridSpec(
             num_scalar_prefetch=1,
             grid=(1,),
-            in_specs=[pl.BlockSpec((count, width), lambda i, ids: (0, 0))],
-            out_specs=pl.BlockSpec((rows, width), lambda i, ids: (0, 0)),
+            in_specs=in_specs,
+            out_specs=pl.BlockSpec((rows, width), whole),
             scratch_shapes=[
                 pltpu.VMEM((rows + ZERO_ROWS, width), jnp.float32)
                 for _ in range(SCATTER_ACCS)
             ],
         ),
-        out_shape=jax.ShapeDtypeStruct((rows, width), jnp.bfloat16),
+        out_shape=jax.ShapeDtypeStruct((rows, width), out_dtype),
         compiler_params=pltpu.CompilerParams(vmem_limit_bytes=62 * 1024 * 1024),
-    )(ids_flat, grads)
+    )(*operands)
 
 
 def on_device(bag_ids, bag_counts, emb_table, cross_down, cross_up, cross_bias, cotangent):
@@ -141,9 +159,19 @@
         grad_low_mine, down_mine, contract, preferred_element_type=jnp.float32
     ) + lax.dot_general(grad_low_other, down_other, contract, preferred_element_type=jnp.float32)
     grad_pooled = (upstream * (gate_value + 1.0) + back_term).astype(jnp.bfloat16)
-    grad_local = lax.all_to_all(grad_pooled, "dp", split_axis=1, concat_axis=0, tiled=True)
+    split = row_count // 2
+    first_half = lax.all_to_all(
+        grad_pooled[:split], "dp", split_axis=1, concat_axis=0, tiled=True
+    )
+    second_half = lax.all_to_all(
+        grad_pooled[split:], "dp", split_axis=1, concat_axis=0, tiled=True
+    )
     partial_value = scatter_rows(
-        ids_flat, grad_local, vocab_rows, slot_count
+        ids_flat, first_half, vocab_rows, slot_count, split, row_count, 0
+    )
+    partial_value = scatter_rows(
+        ids_flat, second_half, vocab_rows, slot_count, split, row_count, split,
+        init=partial_value,
     )
     summed = lax.psum_scatter(
         partial_value, "fsdp", scatter_dimension=0, tiled=True

time: 352 us -> 366 us (1.040)
  blocking collectives: 46.5 us -> 0 us
  starting transfers between devices: 17.2 us -> 39.6 us
  waiting for transfers between devices: 148 us -> 168 us
  Pallas kernels: 81.7 us -> 94.7 us
  local copies, waits for them, and re-layouts: 15.3 us -> 19.4 us
    all_to_all x1 -> x0, blocking collectives: 46.5 us -> none  [on_device(): lax.all_to_all(grad_pooled, 'dp', split_axis=1, concat_axis=0, tiled=True)]
    all_to_all x0 -> x2, starting transfers between devices: none -> 22.2 us  [the longest x1 17.5 us: on_device(): lax.all_to_all(grad_pooled[:split], 'dp', split_axis=1, concat_axis=0, ti...]
    all_to_all x0 -> x2, waiting for transfers between devices: none -> 16.7 us  [the longest x1 16.7 us: on_device(): lax.all_to_all(grad_pooled[:split], 'dp', split_axis=1, concat_axis=0, ti...]
    pallas_call x1 -> x2, Pallas kernels: 39.4 us -> 52.4 us  [scatter_rows(): pl.pallas_call(functools.partial(scatter_kernel, slots=slots, per_source=...]
    reduce_scatter x1, waiting for transfers between devices: 44.3 us -> 48.3 us  [on_device(): lax.psum_scatter(partial_value, 'fsdp', scatter_dimension=0, tiled=True)]
  transfers between devices with their start and end apart: 7 -> 9, of which waited for: 4 -> 5; matrix products, arithmetic and copies ran while one was open for 7% -> 7% of each run, Pallas kernels for 12% -> 19%
where the time goes in v10:
time: 366 us; the launch traced here: 365 us
  waiting for transfers between devices  168 us (46%)
  Pallas kernels  94.7 us (26%)
  starting transfers between devices  39.6 us (11%)
  matrix products  24.5 us (7%)
  local copies, waits for them, and re-layouts  19.4 us (5%)
  between operations  13.3 us (4%)
  other arithmetic  5.04 us (1%)
    all_gather x1, waiting for transfers between devices, on_device(): up_mine = lax.all_gather(up_mine, 'fsdp', axis=1, tiled=True)  93.4 us
    pallas_call x2, Pallas kernels, scatter_rows(): pl.pallas_call(functools.partial(scatter_kernel, slots=slots, per_source=...  52.4 us
    reduce_scatter x1, waiting for transfers between devices, on_device(): lax.psum_scatter(partial_value, 'fsdp', scatter_dimension=0, tiled=True)  48.3 us
    pallas_call x1, Pallas kernels, pool_rows(): pl.pallas_call(functools.partial(pool_kernel, blk=blk, slots=slots), grid...  42.4 us
    all_to_all x1, starting transfers between devices, on_device(): lax.all_to_all(grad_pooled[:split], 'dp', split_axis=1, concat_axis=0, ti...  17.5 us
    all_to_all x1, waiting for transfers between devices, on_device(): lax.all_to_all(grad_pooled[:split], 'dp', split_axis=1, concat_axis=0, ti...  16.7 us
    all_to_all x1, starting transfers between devices, on_device(): lax.all_to_all(send_ids, 'dp', split_axis=1, concat_axis=0, tiled=True)  10.3 us
  transfers between devices with their start and end apart: 9, of which 5 were waited for; matrix products, arithmetic and copies ran while one was open for 7% of the time, Pallas kernels for 19%

profile of v10, /device:TPU:1, one launch (start us, length us, event | category | flops | bytes accessed | tf_op | source)
XLA Modules:
  0.0 364.9 jit_solution(14920285463197764330)
XLA Ops:
  6.5 0.0 all-gather.3.cloned.1.call-start
  6.5 2.4 constant_dynamic-slice_fusion.1
  9.0 0.0 all-gather.3.cloned.1.call-update
  9.0 0.0 all-gather.5.cloned.1.call-start
  9.0 2.4 constant_dynamic-slice_fusion
  11.4 0.0 all-gather.5.cloned.1.call-update
  11.4 0.7 fusion.20
  12.1 10.3 %all-to-all-start = ((s32[128,64,4]{0,2,1:T(4,128)}), s32[128,64,4]{0,2,1:T(4,128)S(1)}, u32[]{:S(2)}, u32[]{:S(2)}) async-start(s32[128,64,4]{0,2,1:T(4,128)} %fusion.20), calls=%async_computation | async-start | bytes 262144 | tf_op jit(solution)/shard_map/all_to_all | solution.py:130
  22.5 0.0 copy-done.5
  22.5 2.3 pad_convert_fusion.tab_ref
  24.8 6.3 %all-to-all-done = s32[128,64,4]{0,2,1:T(4,128)S(1)} async-done(((s32[128,64,4]{0,2,1:T(4,128)}), s32[128,64,4]{0,2,1:T(4,128)S(1)}, u32[]{:S(2)}, u32[]{:S(2)}) %all-to-all-start) | async-done | bytes 131104 | tf_op jit(solution)/shard_map/all_to_all | solution.py:130
  31.0 2.6 copy.11
  33.7 5.5 %reshape.20.ids_ref = s32[32768]{0:T(1024)} reshape(s32[64,128,4]{2,1,0:T(8,128)} %copy.11) | data formatting | bytes 262144 | tf_op jit(solution)/shard_map/reshape | solution.py:132
  39.1 42.4 %shard_map.73 = bf16[8192,128]{1,0:T(8,128)(2,1)} custom-call(s32[32768]{0:T(1024)} %reshape.20.ids_ref, f32[8200,128]{1,0:T(8,128)} %pad_convert_fusion.tab_ref), custom_call_target="tpu_custom_call" | custom-call | tf_op jit(solution)/shard_map/pallas_call | solution.py:32
  81.5 5.3 %all-to-all-start.1 = ((bf16[64,128,128]{2,1,0:T(8,128)(2,1)}), bf16[64,128,128]{2,1,0:T(8,128)(2,1)}, u32[]{:S(2)}, u32[]{:S(2)}) async-start(bf16[64,128,128]{2,1,0:T(8,128)(2,1)} %bitcast.56), calls=%async_computation.1 | async-start | bytes 4194304 | tf_op jit(solution)/shard_map/all_to_all | solution.py:138
  86.8 0.0 copy-start
  86.8 3.7 %all-gather.3.cloned.1.call-done = bf16[8192,256]{1,0:T(8,128)(2,1)} async-done(((bf16[2048,256]{1,0:T(8,128)(2,1)}), bf16[8192,256]{1,0:T(8,128)(2,1)}) %all-gather.3.cloned.1.call-update) | async-done | bytes 4194320 | tf_op jit(solution)/shard_map/all_gather | solution.py:121
  90.5 0.7 collective-permute-start
  91.2 93.4 %all-gather.5.cloned.1.call-done = bf16[256,8192]{1,0:T(8,128)(2,1)} async-done(((bf16[256,2048]{1,0:T(8,128)(2,1)}), bf16[256,8192]{1,0:T(8,128)(2,1)}) %all-gather.5.cloned.1.call-update) | async-done | bytes 4194320 | tf_op jit(solution)/shard_map/all_gather | solution.py:122
  184.6 0.7 collective-permute-start.1
  185.3 0.0 all-to-all-done.1
  185.3 3.7 %fusion.12 = bf16[128,256]{1,0:T(8,128)(2,1)S(1)} fusion(bf16[8192,256]{1,0:T(8,128)(2,1)} %all-gather.3.cloned.1.call-done, bf16[64,128,128]{2,1,0:T(8,128)(2,1)} %all-to-all-done.1), kind=kOutput, calls=%fused_computation.16 | convolution fusion | flops 536903680 | bytes 6356992 | tf_op jit(solution)/shard_map/dot_general | solution.py:142
  189.0 0.3 copy-done.1
  189.3 3.2 convolution_convert_fusion.1
  192.6 0.0 collective-permute-done
  192.6 3.5 fusion.15
  196.2 0.0 collective-permute-done.1
  196.2 4.4 %convolution_convert_fusion = bf16[128,256]{1,0:T(8,128)(2,1)S(1)} fusion(bf16[256,8192]{1,0:T(8,128)(2,1)} %collective-permute-done.1, bf16[128,8192]{1,0:T(8,128)(2,1)S(1)} %copy-done, bf16[64,128,128]{2,1,0:T(8,128)(2,1)} %all-to-all-done.1), kind=kOutput, calls=%fused_computation.18 | convolution fusion | flops 541097984 | bytes 8454144 | tf_op jit(solution)/shard_map/dot_general | solution.py:154
  200.5 0.7 fusion.21
  201.3 1.4 copy-done.3
  202.7 1.5 fusion.22
  204.2 3.7 %fusion.3 = f32[128,8192]{1,0:T(8,128)S(1)} fusion(f32[128,8192]{1,0:T(8,128)S(1)} %fusion.21, bf16[128,256]{1,0:T(8,128)(2,1)S(1)} %fusion.15, bf16[256,8192]{1,0:T(8,128)(2,1)} %collective-permute-done.1, bf16[128,8192]{1,0:T(8,128)(2,1)S(1)} %copy-done, f32[8192]{0:T(1024)S(1)} %copy-done.7), kind=kOutput, calls=%fused_computation.5 | convolution fusion | flops 542113792 | bytes 14778368 | tf_op jit(solution)/shard_map/dot_general | solution.py:147
  207.9 3.8 %fusion.4 = bf16[128,8192]{1,0:T(8,128)(2,1)S(1)} fusion(f32[128,8192]{1,0:T(8,128)S(1)} %fusion.3, f32[128,8192]{1,0:T(8,128)S(1)} %fusion.22, bf16[128,256]{1,0:T(8,128)(2,1)S(1)} %convolution_convert_fusion, bf16[8192,256]{1,0:T(8,128)(2,1)} %collective-permute-done), kind=kOutput, calls=%fused_computation.6 | convolution fusion | flops 540016640 | bytes 14745600 | tf_op jit(solution)/shard_map/dot_general | solution.py:160
  211.7 0.2 slice_bitcast_fusion
  211.9 1.3 copy.35
  213.2 17.5 %all-to-all-start.3 = ((bf16[64,64,128]{2,0,1:T(8,128)(2,1)}), bf16[64,64,128]{2,0,1:T(8,128)(2,1)S(1)}, u32[]{:S(2)}, u32[]{:S(2)}) async-start(bf16[64,64,128]{2,0,1:T(8,128)(2,1)} %bitcast.54), calls=%async_computation.3 | async-start | bytes 2097152 | tf_op jit(solution)/shard_map/all_to_all | solution.py:163
  230.7 1.3 copy.36
  232.0 16.7 %all-to-all-done.3 = bf16[64,64,128]{2,0,1:T(8,128)(2,1)S(1)} async-done(((bf16[64,64,128]{2,0,1:T(8,128)(2,1)}), bf16[64,64,128]{2,0,1:T(8,128)(2,1)S(1)}, u32[]{:S(2)}, u32[]{:S(2)}) %all-to-all-start.3) | async-done | bytes 1048608 | tf_op jit(solution)/shard_map/all_to_all | solution.py:163
  248.7 1.0 copy-done.4
  249.7 4.7 %all-to-all-start.2 = ((bf16[64,64,128]{2,0,1:T(8,128)(2,1)}), bf16[64,64,128]{2,0,1:T(8,128)(2,1)S(1)}, u32[]{:S(2)}, u32[]{:S(2)}) async-start(bf16[64,64,128]{2,0,1:T(8,128)(2,1)} %bitcast.55), calls=%async_computation.2 | async-start | bytes 2097152 | tf_op jit(solution)/shard_map/all_to_all | solution.py:166
  254.4 0.3 reduce-scatter.2.cloned.1.call-start
  254.7 25.8 %shard_map.74.rest_0_ = f32[8192,128]{1,0:T(8,128)} custom-call(s32[32768]{0:T(1024)} %reshape.20.ids_ref, bf16[4096,128]{1,0:T(8,128)(2,1)} %bitcast.58), custom_call_target="tpu_custom_call" | custom-call | tf_op jit(solution)/shard_map/pallas_call | solution.py:90
  280.4 0.0 all-to-all-done.2
  280.4 1.0 copy-done.2
  281.4 26.6 %shard_map.75 = bf16[8192,128]{1,0:T(8,128)(2,1)} custom-call(s32[32768]{0:T(1024)} %reshape.20.ids_ref, bf16[4096,128]{1,0:T(8,128)(2,1)} %bitcast.57, f32[8192,128]{1,0:T(8,128)} %shard_map.74.rest_0_), custom_call_target="tpu_custom_call" | custom-call | tf_op jit(solution)/shard_map/pallas_call | solution.py:90
  308.0 0.0 reduce-scatter.2.cloned.1.call-update
  308.0 48.3 %reduce-scatter.2.cloned.1.call-done = bf16[2048,128]{1,0:T(8,128)(2,1)} async-done(((bf16[8192,128]{1,0:T(8,128)(2,1)}), bf16[2048,128]{1,0:T(8,128)(2,1)}) %reduce-scatter.2.cloned.1.call-update) | async-done | bytes 524304 | tf_op jit(solution)/shard_map/reduce_scatter | solution.py:176
  356.3 2.1 convert_element_type.36
  (12 shorter events, 0.0 us)
Async XLA Ops:
  6.5 4.9 %copy-start.6 = (s32[128,64,4]{0,2,1:T(4,128)S(1)}, s32[128,64,4]{0,2,1:T(4,128)}, u32[]{:S(2)}) copy-start(s32[128,64,4]{0,2,1:T(4,128)} %param.7) | copy-start | bytes 393220
  6.5 4.9 %copy-start.8 = (s32[128,64]{0,1:T(8,128)S(1)}, s32[128,64]{0,1:T(8,128)}, u32[]{:S(2)}) copy-start(s32[128,64]{0,1:T(8,128)} %param.8) | copy-start | bytes 98308
  6.5 16.0 %copy-start.5 = (bf16[8192,128]{1,0:T(8,128)(2,1)S(1)}, bf16[8192,128]{1,0:T(8,128)(2,1)}, u32[]{:S(2)}) copy-start(bf16[8192,128]{1,0:T(8,128)(2,1)} %param.9) | copy-start | bytes 6291460
  6.5 84.0 %all-gather.3.cloned.1.call-start = ((), (), s32[]{:S(2)}) async-start(), calls=%async_computation.5 | async-start | bytes 5242880 | tf_op jit(solution)/shard_map/all_gather | solution.py:121
  9.0 175.6 %all-gather.5.cloned.1.call-start = ((), (), s32[]{:S(2)}) async-start(), calls=%async_computation.6 | async-start | bytes 5242880 | tf_op jit(solution)/shard_map/all_gather | solution.py:122
  12.1 18.9 %all-to-all-start = ((s32[128,64,4]{0,2,1:T(4,128)}), s32[128,64,4]{0,2,1:T(4,128)S(1)}, u32[]{:S(2)}, u32[]{:S(2)}) async-start(s32[128,64,4]{0,2,1:T(4,128)} %fusion.20), calls=%async_computation | async-start | bytes 262144 | tf_op jit(solution)/shard_map/all_to_all | solution.py:130
  81.5 103.8 %all-to-all-start.1 = ((bf16[64,128,128]{2,1,0:T(8,128)(2,1)}), bf16[64,128,128]{2,1,0:T(8,128)(2,1)}, u32[]{:S(2)}, u32[]{:S(2)}) async-start(bf16[64,128,128]{2,1,0:T(8,128)(2,1)} %bitcast.56), calls=%async_computation.1 | async-start | bytes 4194304 | tf_op jit(solution)/shard_map/all_to_all | solution.py:138
  86.8 102.2 %copy-start = (bf16[128,8192]{1,0:T(8,128)(2,1)S(1)}, bf16[128,8192]{1,0:T(8,128)(2,1)}, u32[]{:S(2)}) copy-start(bf16[128,8192]{1,0:T(8,128)(2,1)} %param.13) | copy-start | bytes 6291460
  90.5 102.1 %collective-permute-start = (bf16[8192,256]{1,0:T(8,128)(2,1)}, bf16[8192,256]{1,0:T(8,128)(2,1)}, u32[]{:S(2)}, u32[]{:S(2)}) collective-permute-start(bf16[8192,256]{1,0:T(8,128)(2,1)} %all-gather.3.cloned.1.call-done), channel_id=1, source_target_pairs={{0,4},{4,0},{8,12},{12,8},{16,20},{20,16},{24,28},{28,24},{32,36},... | collective-permute-start | bytes 12582920 | tf_op jit(solution)/shard_map/ppermute | solution.py:124
  184.6 11.6 %collective-permute-start.1 = (bf16[256,8192]{1,0:T(8,128)(2,1)}, bf16[256,8192]{1,0:T(8,128)(2,1)}, u32[]{:S(2)}, u32[]{:S(2)}) collective-permute-start(bf16[256,8192]{1,0:T(8,128)(2,1)} %all-gather.5.cloned.1.call-done), channel_id=1, source_target_pairs={{0,4},{4,0},{8,12},{12,8},{16,20},{20,16},{24,28},{28,24},{32,36},... | collective-permute-start | bytes 12582920 | tf_op jit(solution)/shard_map/ppermute | solution.py:125
  185.3 4.0 %copy-start.1 = (bf16[256,8192]{1,0:T(8,128)(2,1)S(1)}, bf16[256,8192]{1,0:T(8,128)(2,1)}, u32[]{:S(2)}) copy-start(bf16[256,8192]{1,0:T(8,128)(2,1)} %all-gather.5.cloned.1.call-done) | copy-start | bytes 12582916
  200.5 2.2 copy-start.3
  202.7 1.5 copy-start.7
  213.2 35.5 %all-to-all-start.3 = ((bf16[64,64,128]{2,0,1:T(8,128)(2,1)}), bf16[64,64,128]{2,0,1:T(8,128)(2,1)S(1)}, u32[]{:S(2)}, u32[]{:S(2)}) async-start(bf16[64,64,128]{2,0,1:T(8,128)(2,1)} %bitcast.54), calls=%async_computation.3 | async-start | bytes 2097152 | tf_op jit(solution)/shard_map/all_to_all | solution.py:163
  248.7 1.0 copy-start.4
  249.7 30.7 %all-to-all-start.2 = ((bf16[64,64,128]{2,0,1:T(8,128)(2,1)}), bf16[64,64,128]{2,0,1:T(8,128)(2,1)S(1)}, u32[]{:S(2)}, u32[]{:S(2)}) async-start(bf16[64,64,128]{2,0,1:T(8,128)(2,1)} %bitcast.55), calls=%async_computation.2 | async-start | bytes 2097152 | tf_op jit(solution)/shard_map/all_to_all | solution.py:166
  254.4 101.9 %reduce-scatter.2.cloned.1.call-start = ((), (), s32[]{:S(2)}) async-start(), calls=%async_computation.7 | async-start | bytes 2621440 | tf_op jit(solution)/shard_map/reduce_scatter | solution.py:176
  280.4 1.0 copy-start.2
Sparse Core Ops, SparseCore 0:
  9.2 81.3 all-gather.2
  92.4 92.2 all-gather.4
  308.1 48.0 reduce-scatter.1

commit v11 on v8

--- a/solution.py
+++ b/solution.py
@@ -123,7 +123,8 @@
     grad_gate = (upstream * pooled.astype(jnp.float32)).astype(jnp.bfloat16)
     low_mine = jnp.dot(pooled, down_mine, preferred_element_type=jnp.float32).astype(jnp.bfloat16)
     low_other = jnp.dot(pooled, down_other, preferred_element_type=jnp.float32).astype(jnp.bfloat16)
-    low_mine, low_other = lax.optimization_barrier((low_mine, low_other))
+    low_mine = lax.optimization_barrier(low_mine)
+    low_other = lax.optimization_barrier(low_other)
     gate_value = (
         jnp.dot(low_mine, up_mine, preferred_element_type=jnp.float32)
         + jnp.dot(low_other, up_other, preferred_element_type=jnp.float32)
@@ -136,7 +137,8 @@
     grad_low_other = lax.dot_general(
         grad_gate, up_other, contract, preferred_element_type=jnp.float32
     ).astype(jnp.bfloat16)
-    grad_low_mine, grad_low_other = lax.optimization_barrier((grad_low_mine, grad_low_other))
+    grad_low_mine = lax.optimization_barrier(grad_low_mine)
+    grad_low_other = lax.optimization_barrier(grad_low_other)
     back_term = lax.dot_general(
         grad_low_mine, down_mine, contract, preferred_element_type=jnp.float32
     ) + lax.dot_general(grad_low_other, down_other, contract, preferred_element_type=jnp.float32)

time: 352 us -> 350 us (level)
    all_gather x1, waiting for transfers between devices: 93.3 us -> 3.54 us  [on_device(): up_mine = lax.all_gather(up_mine, 'fsdp', axis=1, tiled=True)]
    all_gather x1, waiting for transfers between devices: 3.65 us -> 93.3 us  [on_device(): down_mine = lax.all_gather(down_mine, 'fsdp', axis=0, tiled=True)]
  transfers between devices with their start and end apart: 7 -> 7, of which waited for: 4 -> 4; matrix products, arithmetic and copies ran while one was open for 7% -> 8% of each run, Pallas kernels for 12% -> 12%
where the time goes in v11:
time: 350 us
  waiting for transfers between devices  147 us (42%)
  Pallas kernels  81.8 us (23%)
  blocking collectives  46.5 us (13%)
  matrix products  24.6 us (7%)
  starting transfers between devices  17.1 us (5%)
  local copies, waits for them, and re-layouts  13.8 us (4%)
  between operations  13.3 us (4%)
  other arithmetic  5.06 us (1%)
    all_gather x1, waiting for transfers between devices, on_device(): down_mine = lax.all_gather(down_mine, 'fsdp', axis=0, tiled=True)  93.3 us
    all_to_all x1, blocking collectives, on_device(): lax.all_to_all(grad_pooled, 'dp', split_axis=1, concat_axis=0, tiled=True)  46.5 us
    reduce_scatter x1, waiting for transfers between devices, on_device(): lax.psum_scatter(partial_value, 'fsdp', scatter_dimension=0, tiled=True)  44.3 us
    pallas_call x1, Pallas kernels, pool_rows(): pl.pallas_call(functools.partial(pool_kernel, blk=blk, slots=slots), grid...  42.5 us
    pallas_call x1, Pallas kernels, scatter_rows(): pl.pallas_call(functools.partial(scatter_kernel, slots=slots), grid_spec=...  39.3 us
    all_to_all x1, starting transfers between devices, on_device(): lax.all_to_all(send_ids, 'dp', split_axis=1, concat_axis=0, tiled=True)  10.3 us
  transfers between devices with their start and end apart: 7, of which 4 were waited for; matrix products, arithmetic and copies ran while one was open for 8% of the time, Pallas kernels for 12%

profile of v11, /device:TPU:1, one launch (start us, length us, event | category | flops | bytes accessed | tf_op | source)
XLA Modules:
  0.0 349.6 jit_solution(16044336905995932981)
XLA Ops:
  6.5 0.0 copy-start.6
  6.5 0.0 copy-start.4
  6.5 0.0 copy-start.3
  6.5 0.0 all-gather.5.cloned.1.call-start
  6.5 2.6 constant_dynamic-slice_fusion
  9.1 0.0 all-gather.5.cloned.1.call-update
  9.1 0.0 all-gather.3.cloned.1.call-start
  9.2 2.3 constant_dynamic-slice_fusion.1
  11.4 0.0 all-gather.3.cloned.1.call-update
  11.5 0.0 copy-done.6
  11.5 0.0 copy-done.4
  11.5 0.7 fusion.21
  12.2 10.3 %all-to-all-start = ((s32[128,64,4]{0,2,1:T(4,128)}), s32[128,64,4]{0,2,1:T(4,128)S(1)}, u32[]{:S(2)}, u32[]{:S(2)}) async-start(s32[128,64,4]{0,2,1:T(4,128)} %fusion.21), calls=%async_computation | async-start | bytes 262144 | tf_op jit(solution)/shard_map/all_to_all | solution.py:112
  22.5 0.0 copy-done.3
  22.5 2.3 pad_convert_fusion.tab_ref
  24.8 6.2 %all-to-all-done = s32[128,64,4]{0,2,1:T(4,128)S(1)} async-done(((s32[128,64,4]{0,2,1:T(4,128)}), s32[128,64,4]{0,2,1:T(4,128)S(1)}, u32[]{:S(2)}, u32[]{:S(2)}) %all-to-all-start) | async-done | bytes 131104 | tf_op jit(solution)/shard_map/all_to_all | solution.py:112
  31.1 2.6 copy.10
  33.7 5.5 %reshape.17.ids_ref = s32[32768]{0:T(1024)} reshape(s32[64,128,4]{2,1,0:T(8,128)} %copy.10) | data formatting | bytes 262144 | tf_op jit(solution)/shard_map/reshape | solution.py:114
  39.2 42.5 %shard_map.73 = bf16[8192,128]{1,0:T(8,128)(2,1)} custom-call(s32[32768]{0:T(1024)} %reshape.17.ids_ref, f32[8200,128]{1,0:T(8,128)} %pad_convert_fusion.tab_ref), custom_call_target="tpu_custom_call" | custom-call | tf_op jit(solution)/shard_map/pallas_call | solution.py:32
  81.7 5.3 %all-to-all-start.1 = ((bf16[64,128,128]{2,1,0:T(8,128)(2,1)}), bf16[64,128,128]{2,1,0:T(8,128)(2,1)}, u32[]{:S(2)}, u32[]{:S(2)}) async-start(bf16[64,128,128]{2,1,0:T(8,128)(2,1)} %bitcast.50), calls=%async_computation.1 | async-start | bytes 4194304 | tf_op jit(solution)/shard_map/all_to_all | solution.py:120
  87.0 0.0 reduce-scatter.2.cloned.1.call-start
  87.0 3.5 %all-gather.5.cloned.1.call-done = bf16[256,8192]{1,0:T(8,128)(2,1)} async-done(((bf16[256,2048]{1,0:T(8,128)(2,1)}), bf16[256,8192]{1,0:T(8,128)(2,1)}) %all-gather.5.cloned.1.call-update) | async-done | bytes 4194320 | tf_op jit(solution)/shard_map/all_gather | solution.py:104
  90.6 0.7 collective-permute-start.1
  91.3 93.3 %all-gather.3.cloned.1.call-done = bf16[8192,256]{1,0:T(8,128)(2,1)} async-done(((bf16[2048,256]{1,0:T(8,128)(2,1)}), bf16[8192,256]{1,0:T(8,128)(2,1)}) %all-gather.3.cloned.1.call-update) | async-done | bytes 4194320 | tf_op jit(solution)/shard_map/all_gather | solution.py:103
  184.6 0.7 collective-permute-start
  185.3 0.0 all-to-all-done.1
  185.3 0.0 copy-done
  185.3 4.5 %convolution_convert_fusion.1 = bf16[128,256]{1,0:T(8,128)(2,1)S(1)} fusion(bf16[256,8192]{1,0:T(8,128)(2,1)} %all-gather.5.cloned.1.call-done, bf16[128,8192]{1,0:T(8,128)(2,1)S(1)} %copy-done, bf16[64,128,128]{2,1,0:T(8,128)(2,1)} %all-to-all-done.1), kind=kOutput, calls=%fused_computation.21 | convolution fusion | flops 541097984 | bytes 8454144 | tf_op jit(solution)/shard_map/dot_general | solution.py:134
  189.8 0.0 copy-done.2
  189.8 0.0 copy-start.1
  189.8 2.5 fusion.13
  192.3 0.3 copy-done.1
  192.6 0.7 fusion.22
  193.4 1.5 fusion.23
  194.9 0.0 collective-permute-done.1
  194.9 4.4 %convolution_convert_fusion = bf16[128,256]{1,0:T(8,128)(2,1)S(1)} fusion(bf16[256,8192]{1,0:T(8,128)(2,1)} %collective-permute-done.1, bf16[128,8192]{1,0:T(8,128)(2,1)S(1)} %copy-done, bf16[64,128,128]{2,1,0:T(8,128)(2,1)} %all-to-all-done.1), kind=kOutput, calls=%fused_computation.20 | convolution fusion | flops 541097984 | bytes 8454144 | tf_op jit(solution)/shard_map/dot_general | solution.py:137
  199.2 0.0 copy-start.5
  199.3 0.0 collective-permute-done
  199.3 3.5 %fusion.16 = bf16[128,256]{1,0:T(8,128)(2,1)S(1)} fusion(bf16[8192,256]{1,0:T(8,128)(2,1)} %collective-permute-done, bf16[64,128,128]{2,1,0:T(8,128)(2,1)} %all-to-all-done.1), kind=kOutput, calls=%fused_computation.19 | convolution fusion | flops 536903680 | bytes 6356992 | tf_op jit(solution)/shard_map/dot_general | solution.py:125
  202.8 0.0 copy-done.5
  202.8 3.7 %fusion.3 = f32[128,8192]{1,0:T(8,128)S(1)} fusion(f32[128,8192]{1,0:T(8,128)S(1)} %fusion.22, bf16[128,256]{1,0:T(8,128)(2,1)S(1)} %fusion.16, bf16[256,8192]{1,0:T(8,128)(2,1)} %collective-permute-done.1, bf16[128,8192]{1,0:T(8,128)(2,1)S(1)} %copy-done, f32[8192]{0:T(1024)S(1)} %copy-done.5), kind=kOutput, calls=%fused_computation.5 | convolution fusion | flops 542113792 | bytes 14778368 | tf_op jit(solution)/shard_map/dot_general | solution.py:130
  206.5 3.8 %fusion.10 = bf16[16,64,8,128]{3,2,1,0:T(8,128)(2,1)S(1)} fusion(f32[128,8192]{1,0:T(8,128)S(1)} %fusion.3, f32[128,8192]{1,0:T(8,128)S(1)} %fusion.23, bf16[128,256]{1,0:T(8,128)(2,1)S(1)} %convolution_convert_fusion, bf16[8192,256]{1,0:T(8,128)(2,1)} %collective-permute-done), kind=kOutput, calls=%fused_computation.15 | convolution fusion | flops 540016640 | bytes 14745600 | tf_op jit(solution)/shard_map/dot_general | solution.py:144
  210.3 0.6 copy.31
  210.9 46.5 %all_to_all.51 = bf16[128,64,128]{2,0,1:T(8,128)(2,1)} all-to-all(bf16[128,64,128]{2,0,1:T(8,128)(2,1)S(1)} %bitcast.49), channel_id=1, replica_groups=mesh['dp'=64,'fsdp'=4] {'dp'}, dimensions={1} | all-to-all | bytes 4194304 | tf_op jit(solution)/shard_map/all_to_all | solution.py:146
  257.4 39.3 %shard_map.74 = bf16[8192,128]{1,0:T(8,128)(2,1)} custom-call(s32[32768]{0:T(1024)} %reshape.17.ids_ref, bf16[8192,128]{1,0:T(8,128)(2,1)} %bitcast.48), custom_call_target="tpu_custom_call" | custom-call | tf_op jit(solution)/shard_map/pallas_call | solution.py:75
  296.7 0.0 reduce-scatter.2.cloned.1.call-update
  296.7 44.3 %reduce-scatter.2.cloned.1.call-done = bf16[2048,128]{1,0:T(8,128)(2,1)} async-done(((bf16[8192,128]{1,0:T(8,128)(2,1)}), bf16[2048,128]{1,0:T(8,128)(2,1)}) %reduce-scatter.2.cloned.1.call-update) | async-done | bytes 524304 | tf_op jit(solution)/shard_map/reduce_scatter | solution.py:150
  341.0 2.1 convert_element_type.36
  (2 shorter events, 0.0 us)
Async XLA Ops:
  6.5 4.9 %copy-start.6 = (s32[128,64]{0,1:T(8,128)S(1)}, s32[128,64]{0,1:T(8,128)}, u32[]{:S(2)}) copy-start(s32[128,64]{0,1:T(8,128)} %param.8) | copy-start | bytes 98308
  6.5 4.9 %copy-start.4 = (s32[128,64,4]{0,2,1:T(4,128)S(1)}, s32[128,64,4]{0,2,1:T(4,128)}, u32[]{:S(2)}) copy-start(s32[128,64,4]{0,2,1:T(4,128)} %param.7) | copy-start | bytes 393220
  6.5 16.0 %copy-start.3 = (bf16[8192,128]{1,0:T(8,128)(2,1)S(1)}, bf16[8192,128]{1,0:T(8,128)(2,1)}, u32[]{:S(2)}) copy-start(bf16[8192,128]{1,0:T(8,128)(2,1)} %param.9) | copy-start | bytes 6291460
  6.5 84.0 %all-gather.5.cloned.1.call-start = ((), (), s32[]{:S(2)}) async-start(), calls=%async_computation.5 | async-start | bytes 5242880 | tf_op jit(solution)/shard_map/all_gather | solution.py:104
  9.1 175.5 %all-gather.3.cloned.1.call-start = ((), (), s32[]{:S(2)}) async-start(), calls=%async_computation.4 | async-start | bytes 5242880 | tf_op jit(solution)/shard_map/all_gather | solution.py:103
  12.2 18.9 %all-to-all-start = ((s32[128,64,4]{0,2,1:T(4,128)}), s32[128,64,4]{0,2,1:T(4,128)S(1)}, u32[]{:S(2)}, u32[]{:S(2)}) async-start(s32[128,64,4]{0,2,1:T(4,128)} %fusion.21), calls=%async_computation | async-start | bytes 262144 | tf_op jit(solution)/shard_map/all_to_all | solution.py:112
  39.2 146.1 %copy-start = (bf16[128,8192]{1,0:T(8,128)(2,1)S(1)}, bf16[128,8192]{1,0:T(8,128)(2,1)}, u32[]{:S(2)}) copy-start(bf16[128,8192]{1,0:T(8,128)(2,1)} %param.13) | copy-start | bytes 6291460
  81.7 103.6 %all-to-all-start.1 = ((bf16[64,128,128]{2,1,0:T(8,128)(2,1)}), bf16[64,128,128]{2,1,0:T(8,128)(2,1)}, u32[]{:S(2)}, u32[]{:S(2)}) async-start(bf16[64,128,128]{2,1,0:T(8,128)(2,1)} %bitcast.50), calls=%async_computation.1 | async-start | bytes 4194304 | tf_op jit(solution)/shard_map/all_to_all | solution.py:120
  87.0 254.0 %reduce-scatter.2.cloned.1.call-start = ((), (), s32[]{:S(2)}) async-start(), calls=%async_computation.6 | async-start | bytes 2621440 | tf_op jit(solution)/shard_map/reduce_scatter | solution.py:150
  90.6 104.3 %collective-permute-start.1 = (bf16[256,8192]{1,0:T(8,128)(2,1)}, bf16[256,8192]{1,0:T(8,128)(2,1)}, u32[]{:S(2)}, u32[]{:S(2)}) collective-permute-start(bf16[256,8192]{1,0:T(8,128)(2,1)} %all-gather.5.cloned.1.call-done), channel_id=1, source_target_pairs={{0,4},{4,0},{8,12},{12,8},{16,20},{20,16},{24,28},{28,24},{32,36},... | collective-permute-start | bytes 12582920 | tf_op jit(solution)/shard_map/ppermute | solution.py:107
  184.6 14.6 %collective-permute-start = (bf16[8192,256]{1,0:T(8,128)(2,1)}, bf16[8192,256]{1,0:T(8,128)(2,1)}, u32[]{:S(2)}, u32[]{:S(2)}) collective-permute-start(bf16[8192,256]{1,0:T(8,128)(2,1)} %all-gather.3.cloned.1.call-done), channel_id=1, source_target_pairs={{0,4},{4,0},{8,12},{12,8},{16,20},{20,16},{24,28},{28,24},{32,36},... | collective-permute-start | bytes 12582920 | tf_op jit(solution)/shard_map/ppermute | solution.py:106
  185.3 4.5 %copy-start.2 = (bf16[8192,256]{1,0:T(8,128)(2,1)S(1)}, bf16[8192,256]{1,0:T(8,128)(2,1)}, u32[]{:S(2)}) copy-start(bf16[8192,256]{1,0:T(8,128)(2,1)} %all-gather.3.cloned.1.call-done) | copy-start | bytes 12582916
  189.8 2.8 copy-start.1
  199.2 3.6 %copy-start.5 = (f32[8192]{0:T(1024)S(1)}, f32[8192]{0:T(1024)}, u32[]{:S(2)}) copy-start(f32[8192]{0:T(1024)} %param.12) | copy-start | bytes 98308
Sparse Core Ops, SparseCore 0:
  9.2 81.2 all-gather.4
  92.4 92.1 all-gather.2
  296.9 44.0 reduce-scatter.1

commit v12 on v11

--- a/solution.py
+++ b/solution.py
@@ -103,8 +103,17 @@
     down_mine = lax.all_gather(down_mine, "fsdp", axis=0, tiled=True)
     up_mine = lax.all_gather(up_mine, "fsdp", axis=1, tiled=True)
     partner = [(i, i ^ 1) for i in range(dp_size)]
-    down_other = lax.ppermute(down_mine, "dp", partner)
-    up_other = lax.ppermute(up_mine, "dp", partner)
+
+    def swap(x, axis, chunks=4):
+        size = x.shape[axis] // chunks
+        parts = [
+            lax.ppermute(lax.slice_in_dim(x, c * size, (c + 1) * size, axis=axis), "dp", partner)
+            for c in range(chunks)
+        ]
+        return jnp.concatenate(parts, axis=axis)
+
+    down_other = swap(down_mine, 0)
+    up_other = swap(up_mine, 1)
 
     slot_iota = lax.broadcasted_iota(jnp.int32, bag_ids.shape, 2)
     live_ids = jnp.where(slot_iota < bag_counts[:, :, None], bag_ids, vocab_rows)

time: 350 us -> 356 us (1.017)
  local copies, waits for them, and re-layouts: 13.8 us -> 28 us
  matrix products: 24.6 us -> 17.7 us
  waiting for transfers between devices: 147 us -> 143 us
    slice x0 -> x2, local copies, waits for them, and re-layouts: none -> 8.73 us  [swap(): lax.slice_in_dim(x, c * size, (c + 1) * size, axis=axis)]
    all_gather x1, waiting for transfers between devices: 93.3 us -> 87 us  [on_device(): down_mine = lax.all_gather(down_mine, 'fsdp', axis=0, tiled=True)]
    unnamed x14 -> x26, local copies, waits for them, and re-layouts: 0.33 us -> 4.46 us
  transfers between devices with their start and end apart: 7 -> 13, of which waited for: 4 -> 4; matrix products, arithmetic and copies ran while one was open for 8% -> 11% of each run, Pallas kernels for 12% -> 12%
where the time goes in v12:
time: 356 us; the launch traced here: 355 us
  waiting for transfers between devices  143 us (40%)
  Pallas kernels  81.8 us (23%)
  blocking collectives  46.5 us (13%)
  local copies, waits for them, and re-layouts  28 us (8%)
  starting transfers between devices  19.3 us (5%)
  matrix products  17.7 us (5%)
  between operations  13.4 us (4%)
  other arithmetic  4.95 us (1%)
    all_gather x1, waiting for transfers between devices, on_device(): down_mine = lax.all_gather(down_mine, 'fsdp', axis=0, tiled=True)  87 us
    all_to_all x1, blocking collectives, on_device(): lax.all_to_all(grad_pooled, 'dp', split_axis=1, concat_axis=0, tiled=True)  46.5 us
    reduce_scatter x1, waiting for transfers between devices, on_device(): lax.psum_scatter(partial_value, 'fsdp', scatter_dimension=0, tiled=True)  44.3 us
    pallas_call x1, Pallas kernels, pool_rows(): pl.pallas_call(functools.partial(pool_kernel, blk=blk, slots=slots), grid...  42.3 us
    pallas_call x1, Pallas kernels, scatter_rows(): pl.pallas_call(functools.partial(scatter_kernel, slots=slots), grid_spec=...  39.4 us
    all_to_all x1, starting transfers between devices, on_device(): lax.all_to_all(send_ids, 'dp', split_axis=1, concat_axis=0, tiled=True)  10.3 us
    slice x2, local copies, waits for them, and re-layouts, swap(): lax.slice_in_dim(x, c * size, (c + 1) * size, axis=axis)  8.73 us
  transfers between devices with their start and end apart: 13, of which 4 were waited for; matrix products, arithmetic and copies ran while one was open for 11% of the time, Pallas kernels for 12%

profile of v12, /device:TPU:1, one launch (start us, length us, event | category | flops | bytes accessed | tf_op | source)
XLA Modules:
  0.0 354.8 jit_solution(4357982076364999813)
XLA Ops:
  6.5 2.5 constant_dynamic-slice_fusion
  9.0 0.0 all-gather.5.cloned.1.call-update
  9.0 0.0 all-gather.3.cloned.1.call-start
  9.1 2.3 constant_dynamic-slice_fusion.1
  11.3 0.0 all-gather.3.cloned.1.call-update
  11.4 0.7 fusion.21
  12.1 10.3 %all-to-all-start = ((s32[128,64,4]{0,2,1:T(4,128)}), s32[128,64,4]{0,2,1:T(4,128)S(1)}, u32[]{:S(2)}, u32[]{:S(2)}) async-start(s32[128,64,4]{0,2,1:T(4,128)} %fusion.21), calls=%async_computation | async-start | bytes 262144 | tf_op jit(solution)/shard_map/all_to_all | solution.py:121
  22.4 2.2 pad_convert_fusion.tab_ref
  24.6 6.3 %all-to-all-done = s32[128,64,4]{0,2,1:T(4,128)S(1)} async-done(((s32[128,64,4]{0,2,1:T(4,128)}), s32[128,64,4]{0,2,1:T(4,128)S(1)}, u32[]{:S(2)}, u32[]{:S(2)}) %all-to-all-start) | async-done | bytes 131104 | tf_op jit(solution)/shard_map/all_to_all | solution.py:121
  31.0 2.6 copy.10
  33.6 5.5 %reshape.17.ids_ref = s32[32768]{0:T(1024)} reshape(s32[64,128,4]{2,1,0:T(8,128)} %copy.10) | data formatting | bytes 262144 | tf_op jit(solution)/shard_map/reshape | solution.py:123
  39.1 42.3 %shard_map.73 = bf16[8192,128]{1,0:T(8,128)(2,1)} custom-call(s32[32768]{0:T(1024)} %reshape.17.ids_ref, f32[8200,128]{1,0:T(8,128)} %pad_convert_fusion.tab_ref), custom_call_target="tpu_custom_call" | custom-call | tf_op jit(solution)/shard_map/pallas_call | solution.py:32
  81.4 5.3 %all-to-all-start.1 = ((bf16[64,128,128]{2,1,0:T(8,128)(2,1)}), bf16[64,128,128]{2,1,0:T(8,128)(2,1)}, u32[]{:S(2)}, u32[]{:S(2)}) async-start(bf16[64,128,128]{2,1,0:T(8,128)(2,1)} %bitcast.50), calls=%async_computation.1 | async-start | bytes 4194304 | tf_op jit(solution)/shard_map/all_to_all | solution.py:129
  86.7 0.0 reduce-scatter.2.cloned.1.call-start
  86.8 5.6 %all-gather.5.cloned.1.call-done = bf16[256,8192]{1,0:T(8,128)(2,1)} async-done(((bf16[256,2048]{1,0:T(8,128)(2,1)}), bf16[256,8192]{1,0:T(8,128)(2,1)}) %all-gather.5.cloned.1.call-update) | async-done | bytes 4194320 | tf_op jit(solution)/shard_map/all_gather | solution.py:104
  92.4 4.5 %fusion.22 = (bf16[256,2048]{1,0:T(8,128)(2,1)}, bf16[256,2048]{1,0:T(8,128)(2,1)}, bf16[256,2048]{1,0:T(8,128)(2,1)}, bf16[256,2048]{1,0:T(8,128)(2,1)}) fusion(bf16[256,8192]{1,0:T(8,128)(2,1)} %all-gather.5.cloned.1.call-done), kind=kLoop, calls=%fused_computation.34 | loop fusion | bytes 8388608 | tf_op jit(solution)/shard_map/slice | solution.py:110
  96.8 0.9 collective-permute-start.4
  97.7 87.0 %all-gather.3.cloned.1.call-done = bf16[8192,256]{1,0:T(8,128)(2,1)} async-done(((bf16[2048,256]{1,0:T(8,128)(2,1)}), bf16[8192,256]{1,0:T(8,128)(2,1)}) %all-gather.3.cloned.1.call-update) | async-done | bytes 4194320 | tf_op jit(solution)/shard_map/all_gather | solution.py:103
  184.7 4.3 %fusion.23 = (bf16[2048,256]{1,0:T(8,128)(2,1)}, bf16[2048,256]{1,0:T(8,128)(2,1)}, bf16[2048,256]{1,0:T(8,128)(2,1)}, bf16[2048,256]{1,0:T(8,128)(2,1)}) fusion(bf16[8192,256]{1,0:T(8,128)(2,1)} %all-gather.3.cloned.1.call-done), kind=kLoop, calls=%fused_computation.35 | loop fusion | bytes 8388608 | tf_op jit(solution)/shard_map/slice | solution.py:110
  189.0 0.7 collective-permute-start
  189.7 0.5 collective-permute-start.2
  190.2 4.5 %convolution_convert_fusion.1 = bf16[128,256]{1,0:T(8,128)(2,1)S(1)} fusion(bf16[256,8192]{1,0:T(8,128)(2,1)} %all-gather.5.cloned.1.call-done, bf16[128,8192]{1,0:T(8,128)(2,1)S(1)} %copy-done.1, bf16[64,128,128]{2,1,0:T(8,128)(2,1)} %all-to-all-done.1), kind=kOutput, calls=%fused_computation.21 | convolution fusion | flops 541097984 | bytes 8454144 | tf_op jit(solution)/shard_map/dot_general | solution.py:143
  194.7 2.5 fusion.13
  197.2 0.3 copy-done
  197.5 0.7 fusion.24
  198.3 1.5 fusion.25
  199.8 0.8 collective-permute-start.5
  200.6 1.3 constant_dynamic-update-slice_fusion.3
  201.9 0.1 collective-permute-start.6
  202.0 1.3 constant_dynamic-update-slice_fusion.2
  203.3 0.6 collective-permute-start.7
  203.9 1.3 constant_dynamic-update-slice_fusion.1
  205.2 1.3 constant_dynamic-update-slice_fusion
  206.5 2.3 fusion.16
  208.9 0.1 constant_dynamic-update-slice_fusion.7
  209.0 0.1 constant_dynamic-update-slice_fusion.6
  209.1 0.1 constant_dynamic-update-slice_fusion.5
  209.1 0.1 constant_dynamic-update-slice_fusion.4
  209.2 0.0 copy-start.8
  209.2 3.2 convolution_convert_fusion
  212.4 1.5 fusion.3
  213.9 1.5 fusion.10
  215.4 0.6 copy.31
  216.0 46.5 %all_to_all.51 = bf16[128,64,128]{2,0,1:T(8,128)(2,1)} all-to-all(bf16[128,64,128]{2,0,1:T(8,128)(2,1)S(1)} %bitcast.49), channel_id=1, replica_groups=mesh['dp'=64,'fsdp'=4] {'dp'}, dimensions={1} | all-to-all | bytes 4194304 | tf_op jit(solution)/shard_map/all_to_all | solution.py:155
  262.5 39.4 %shard_map.74 = bf16[8192,128]{1,0:T(8,128)(2,1)} custom-call(s32[32768]{0:T(1024)} %reshape.17.ids_ref, bf16[8192,128]{1,0:T(8,128)(2,1)} %bitcast.48), custom_call_target="tpu_custom_call" | custom-call | tf_op jit(solution)/shard_map/pallas_call | solution.py:75
  301.9 0.0 reduce-scatter.2.cloned.1.call-update
  302.0 44.3 %reduce-scatter.2.cloned.1.call-done = bf16[2048,128]{1,0:T(8,128)(2,1)} async-done(((bf16[8192,128]{1,0:T(8,128)(2,1)}), bf16[2048,128]{1,0:T(8,128)(2,1)}) %reduce-scatter.2.cloned.1.call-update) | async-done | bytes 524304 | tf_op jit(solution)/shard_map/reduce_scatter | solution.py:159
  346.2 2.1 convert_element_type.36
  (30 shorter events, 0.1 us)
Async XLA Ops:
  6.5 4.8 %copy-start.7 = (s32[128,64,4]{0,2,1:T(4,128)S(1)}, s32[128,64,4]{0,2,1:T(4,128)}, u32[]{:S(2)}) copy-start(s32[128,64,4]{0,2,1:T(4,128)} %param.7) | copy-start | bytes 393220
  6.5 4.8 %copy-start.9 = (s32[128,64]{0,1:T(8,128)S(1)}, s32[128,64]{0,1:T(8,128)}, u32[]{:S(2)}) copy-start(s32[128,64]{0,1:T(8,128)} %param.8) | copy-start | bytes 98308
  6.5 15.9 %copy-start.3 = (bf16[8192,128]{1,0:T(8,128)(2,1)S(1)}, bf16[8192,128]{1,0:T(8,128)(2,1)}, u32[]{:S(2)}) copy-start(bf16[8192,128]{1,0:T(8,128)(2,1)} %param.9) | copy-start | bytes 6291460
  6.5 85.8 %all-gather.5.cloned.1.call-start = ((), (), s32[]{:S(2)}) async-start(), calls=%async_computation.5 | async-start | bytes 5242880 | tf_op jit(solution)/shard_map/all_gather | solution.py:104
  9.0 175.7 %all-gather.3.cloned.1.call-start = ((), (), s32[]{:S(2)}) async-start(), calls=%async_computation.4 | async-start | bytes 5242880 | tf_op jit(solution)/shard_map/all_gather | solution.py:103
  12.1 18.9 %all-to-all-start = ((s32[128,64,4]{0,2,1:T(4,128)}), s32[128,64,4]{0,2,1:T(4,128)S(1)}, u32[]{:S(2)}, u32[]{:S(2)}) async-start(s32[128,64,4]{0,2,1:T(4,128)} %fusion.21), calls=%async_computation | async-start | bytes 262144 | tf_op jit(solution)/shard_map/all_to_all | solution.py:121
  81.4 108.8 %all-to-all-start.1 = ((bf16[64,128,128]{2,1,0:T(8,128)(2,1)}), bf16[64,128,128]{2,1,0:T(8,128)(2,1)}, u32[]{:S(2)}, u32[]{:S(2)}) async-start(bf16[64,128,128]{2,1,0:T(8,128)(2,1)} %bitcast.50), calls=%async_computation.1 | async-start | bytes 4194304 | tf_op jit(solution)/shard_map/all_to_all | solution.py:129
  86.7 259.5 %reduce-scatter.2.cloned.1.call-start = ((), (), s32[]{:S(2)}) async-start(), calls=%async_computation.6 | async-start | bytes 2621440 | tf_op jit(solution)/shard_map/reduce_scatter | solution.py:159
  96.8 93.3 %copy-start.1 = (bf16[128,8192]{1,0:T(8,128)(2,1)S(1)}, bf16[128,8192]{1,0:T(8,128)(2,1)}, u32[]{:S(2)}) copy-start(bf16[128,8192]{1,0:T(8,128)(2,1)} %param.13) | copy-start | bytes 6291460
  96.8 112.0 %collective-permute-start.4 = (bf16[256,2048]{1,0:T(8,128)(2,1)}, bf16[256,2048]{1,0:T(8,128)(2,1)S(1)}, u32[]{:S(2)}, u32[]{:S(2)}) collective-permute-start(bf16[256,2048]{1,0:T(8,128)(2,1)} %get-tuple-element.8), channel_id=1, source_target_pairs={{0,4},{4,0},{8,12},{12,8},{16,20},{20,16},{24,28},{28,24},{32,36},... | collective-permute-start | bytes 3145736 | tf_op jit(solution)/shard_map/ppermute | solution.py:110
  189.0 10.8 %collective-permute-start = (bf16[2048,256]{1,0:T(8,128)(2,1)}, bf16[2048,256]{1,0:T(8,128)(2,1)}, u32[]{:S(2)}, u32[]{:S(2)}) collective-permute-start(bf16[2048,256]{1,0:T(8,128)(2,1)} %get-tuple-element.12), channel_id=1, source_target_pairs={{0,4},{4,0},{8,12},{12,8},{16,20},{20,16},{24,28},{28,24},{32,36},... | collective-permute-start | bytes 3145736 | tf_op jit(solution)/shard_map/ppermute | solution.py:110
  189.7 12.2 %collective-permute-start.1 = (bf16[2048,256]{1,0:T(8,128)(2,1)}, bf16[2048,256]{1,0:T(8,128)(2,1)}, u32[]{:S(2)}, u32[]{:S(2)}) collective-permute-start(bf16[2048,256]{1,0:T(8,128)(2,1)} %get-tuple-element.11), channel_id=1, source_target_pairs={{0,4},{4,0},{8,12},{12,8},{16,20},{20,16},{24,28},{28,24},{32,36},... | collective-permute-start | bytes 3145736 | tf_op jit(solution)/shard_map/ppermute | solution.py:110
  189.7 13.6 %collective-permute-start.2 = (bf16[2048,256]{1,0:T(8,128)(2,1)}, bf16[2048,256]{1,0:T(8,128)(2,1)}, u32[]{:S(2)}, u32[]{:S(2)}) collective-permute-start(bf16[2048,256]{1,0:T(8,128)(2,1)} %get-tuple-element.10), channel_id=1, source_target_pairs={{0,4},{4,0},{8,12},{12,8},{16,20},{20,16},{24,28},{28,24},{32,36},... | collective-permute-start | bytes 3145736 | tf_op jit(solution)/shard_map/ppermute | solution.py:110
  190.2 15.0 %collective-permute-start.3 = (bf16[2048,256]{1,0:T(8,128)(2,1)}, bf16[2048,256]{1,0:T(8,128)(2,1)}, u32[]{:S(2)}, u32[]{:S(2)}) collective-permute-start(bf16[2048,256]{1,0:T(8,128)(2,1)} %get-tuple-element.9), channel_id=1, source_target_pairs={{0,4},{4,0},{8,12},{12,8},{16,20},{20,16},{24,28},{28,24},{32,36},... | collective-permute-start | bytes 3145736 | tf_op jit(solution)/shard_map/ppermute | solution.py:110
  190.2 4.5 %copy-start.2 = (bf16[8192,256]{1,0:T(8,128)(2,1)S(1)}, bf16[8192,256]{1,0:T(8,128)(2,1)}, u32[]{:S(2)}) copy-start(bf16[8192,256]{1,0:T(8,128)(2,1)} %all-gather.3.cloned.1.call-done) | copy-start | bytes 12582916
  194.7 2.8 copy-start
  198.3 1.5 copy-start.6
  198.3 3.6 %copy-start.5 = (bf16[256,2048]{1,0:T(8,128)(2,1)S(1)}, bf16[256,2048]{1,0:T(8,128)(2,1)}, u32[]{:S(2)}) copy-start(bf16[256,2048]{1,0:T(8,128)(2,1)} %get-tuple-element.6) | copy-start | bytes 3145732
  199.8 3.6 %copy-start.4 = (bf16[256,2048]{1,0:T(8,128)(2,1)S(1)}, bf16[256,2048]{1,0:T(8,128)(2,1)}, u32[]{:S(2)}) copy-start(bf16[256,2048]{1,0:T(8,128)(2,1)} %get-tuple-element.5) | copy-start | bytes 3145732
  199.8 9.2 %collective-permute-start.5 = (bf16[256,2048]{1,0:T(8,128)(2,1)S(1)}, bf16[256,2048]{1,0:T(8,128)(2,1)S(1)}, u32[]{:S(2)}, u32[]{:S(2)}) collective-permute-start(bf16[256,2048]{1,0:T(8,128)(2,1)S(1)} %copy-done.6), channel_id=1, source_target_pairs={{0,4},{4,0},{8,12},{12,8},{16,20},{20,16},{24,28},{28,24},{32,36},... | collective-permute-start | bytes 3145736 | tf_op jit(solution)/shard_map/ppermute | solution.py:110
  201.9 7.2 %collective-permute-start.6 = (bf16[256,2048]{1,0:T(8,128)(2,1)S(1)}, bf16[256,2048]{1,0:T(8,128)(2,1)S(1)}, u32[]{:S(2)}, u32[]{:S(2)}) collective-permute-start(bf16[256,2048]{1,0:T(8,128)(2,1)S(1)} %copy-done.5), channel_id=1, source_target_pairs={{0,4},{4,0},{8,12},{12,8},{16,20},{20,16},{24,28},{28,24},{32,36},... | collective-permute-start | bytes 3145736 | tf_op jit(solution)/shard_map/ppermute | solution.py:110
  203.3 5.8 %collective-permute-start.7 = (bf16[256,2048]{1,0:T(8,128)(2,1)S(1)}, bf16[256,2048]{1,0:T(8,128)(2,1)S(1)}, u32[]{:S(2)}, u32[]{:S(2)}) collective-permute-start(bf16[256,2048]{1,0:T(8,128)(2,1)S(1)} %copy-done.4), channel_id=1, source_target_pairs={{0,4},{4,0},{8,12},{12,8},{16,20},{20,16},{24,28},{28,24},{32,36},... | collective-permute-start | bytes 3145736 | tf_op jit(solution)/shard_map/ppermute | solution.py:110
  209.2 3.2 copy-start.8
Sparse Core Ops, SparseCore 0:
  9.2 83.1 all-gather.4
  94.2 90.4 all-gather.2
  302.1 44.0 reduce-scatter.1

commit v13 on v11

--- a/solution.py
+++ b/solution.py
@@ -98,13 +98,18 @@
 
     dp_idx = lax.axis_index("dp")
     core = dp_idx % 2
-    down_mine = lax.dynamic_slice_in_dim(cross_down, core * half, half, 1)
-    up_mine = lax.dynamic_slice_in_dim(cross_up, core * half, half, 0)
-    down_mine = lax.all_gather(down_mine, "fsdp", axis=0, tiled=True)
-    up_mine = lax.all_gather(up_mine, "fsdp", axis=1, tiled=True)
+    quarter = half // 2
+    down_piece = lax.dynamic_slice_in_dim(cross_down, core * half, half, 1)
+    up_piece = lax.dynamic_slice_in_dim(cross_up, core * half, half, 0)
+    first = jnp.concatenate([up_piece.T, down_piece[:, :quarter]], axis=1)
+    first = lax.all_gather(first, "fsdp", axis=0, tiled=True)
+    second = lax.all_gather(down_piece[:, quarter:], "fsdp", axis=0, tiled=True)
     partner = [(i, i ^ 1) for i in range(dp_size)]
-    down_other = lax.ppermute(down_mine, "dp", partner)
-    up_other = lax.ppermute(up_mine, "dp", partner)
+    first_other = lax.ppermute(first, "dp", partner)
+    second_other = lax.ppermute(second, "dp", partner)
+    up_t_mine, up_t_other = first[:, :half], first_other[:, :half]
+    down_mine = (first[:, half:], second)
+    down_other = (first_other[:, half:], second_other)
 
     slot_iota = lax.broadcasted_iota(jnp.int32, bag_ids.shape, 2)
     live_ids = jnp.where(slot_iota < bag_counts[:, :, None], bag_ids, vocab_rows)
@@ -121,27 +126,37 @@
 
     upstream = cotangent.astype(jnp.float32)
     grad_gate = (upstream * pooled.astype(jnp.float32)).astype(jnp.bfloat16)
-    low_mine = jnp.dot(pooled, down_mine, preferred_element_type=jnp.float32).astype(jnp.bfloat16)
-    low_other = jnp.dot(pooled, down_other, preferred_element_type=jnp.float32).astype(jnp.bfloat16)
+    def low_of(downs):
+        return jnp.concatenate(
+            [jnp.dot(pooled, d, preferred_element_type=jnp.float32) for d in downs], axis=1
+        ).astype(jnp.bfloat16)
+
+    low_mine = low_of(down_mine)
+    low_other = low_of(down_other)
     low_mine = lax.optimization_barrier(low_mine)
     low_other = lax.optimization_barrier(low_other)
+    contract = (((1,), (1,)), ((), ()))
     gate_value = (
-        jnp.dot(low_mine, up_mine, preferred_element_type=jnp.float32)
-        + jnp.dot(low_other, up_other, preferred_element_type=jnp.float32)
+        lax.dot_general(low_mine, up_t_mine, contract, preferred_element_type=jnp.float32)
+        + lax.dot_general(low_other, up_t_other, contract, preferred_element_type=jnp.float32)
         + cross_bias
     )
-    contract = (((1,), (1,)), ((), ()))
-    grad_low_mine = lax.dot_general(
-        grad_gate, up_mine, contract, preferred_element_type=jnp.float32
-    ).astype(jnp.bfloat16)
-    grad_low_other = lax.dot_general(
-        grad_gate, up_other, contract, preferred_element_type=jnp.float32
-    ).astype(jnp.bfloat16)
+    grad_low_mine = jnp.dot(grad_gate, up_t_mine, preferred_element_type=jnp.float32).astype(
+        jnp.bfloat16
+    )
+    grad_low_other = jnp.dot(grad_gate, up_t_other, preferred_element_type=jnp.float32).astype(
+        jnp.bfloat16
+    )
     grad_low_mine = lax.optimization_barrier(grad_low_mine)
     grad_low_other = lax.optimization_barrier(grad_low_other)
-    back_term = lax.dot_general(
-        grad_low_mine, down_mine, contract, preferred_element_type=jnp.float32
-    ) + lax.dot_general(grad_low_other, down_other, contract, preferred_element_type=jnp.float32)
+    back_term = None
+    for grad_low, downs in ((grad_low_mine, down_mine), (grad_low_other, down_other)):
+        for q, d in enumerate(downs):
+            part = lax.dot_general(
+                grad_low[:, q * quarter:(q + 1) * quarter], d, contract,
+                preferred_element_type=jnp.float32,
+            )
+            back_term = part if back_term is None else back_term + part
     grad_pooled = (upstream * (gate_value + 1.0) + back_term).astype(jnp.bfloat16)
     grad_local = lax.all_to_all(grad_pooled, "dp", split_axis=1, concat_axis=0, tiled=True)
     partial_value = scatter_rows(

time: 350 us -> 367 us (1.049)
  waiting for transfers between devices: 147 us -> 165 us
  blocking collectives: 46.5 us -> 40.3 us
    all_gather x2, waiting for transfers between devices: 96.9 us -> 114 us  [the longest x1 62.3 us: on_device(): first = lax.all_gather(first, 'fsdp', axis=0, tiled=True)]
    all_to_all x1, blocking collectives: 46.5 us -> 40.3 us  [on_device(): lax.all_to_all(grad_pooled, 'dp', split_axis=1, concat_axis=0, tiled=True)]
    dynamic_slice x2 -> x0, local copies, waits for them, and re-layouts: 4.82 us -> none  [the longest x1 2.55 us: on_device(): up_mine = lax.dynamic_slice_in_dim(cross_up, core * half, half, 0)]
    dot_general x8 -> x12, matrix products: 24.6 us -> 27.8 us  [the longest x4 10.8 us: low_of(): jnp.dot(pooled, d, preferred_element_type=jnp.float32)]
  transfers between devices with their start and end apart: 7 -> 7, of which waited for: 4 -> 5; matrix products, arithmetic and copies ran while one was open for 8% -> 7% of each run, Pallas kernels for 12% -> 12%
where the time goes in v13:
time: 367 us; the launch traced here: 366 us
  waiting for transfers between devices  165 us (45%)
  Pallas kernels  81.8 us (22%)
  blocking collectives  40.3 us (11%)
  matrix products  27.8 us (8%)
  starting transfers between devices  17.7 us (5%)
  local copies, waits for them, and re-layouts  13.4 us (4%)
  between operations  13.3 us (4%)
  other arithmetic  6.36 us (2%)
    all_gather x1, waiting for transfers between devices, on_device(): first = lax.all_gather(first, 'fsdp', axis=0, tiled=True)  62.3 us
    all_gather x1, waiting for transfers between devices, on_device(): second = lax.all_gather(down_piece[:, quarter:], 'fsdp', axis=0, tiled=True)  52.2 us
    reduce_scatter x1, waiting for transfers between devices, on_device(): lax.psum_scatter(partial_value, 'fsdp', scatter_dimension=0, tiled=True)  44.8 us
    pallas_call x1, Pallas kernels, pool_rows(): pl.pallas_call(functools.partial(pool_kernel, blk=blk, slots=slots), grid...  42.4 us
    all_to_all x1, blocking collectives, on_device(): lax.all_to_all(grad_pooled, 'dp', split_axis=1, concat_axis=0, tiled=True)  40.3 us
    pallas_call x1, Pallas kernels, scatter_rows(): pl.pallas_call(functools.partial(scatter_kernel, slots=slots), grid_spec=...  39.4 us
    dot_general x4, matrix products, low_of(): jnp.dot(pooled, d, preferred_element_type=jnp.float32)  10.8 us
    all_to_all x1, starting transfers between devices, on_device(): lax.all_to_all(send_ids, 'dp', split_axis=1, concat_axis=0, tiled=True)  10.3 us
  transfers between devices with their start and end apart: 7, of which 5 were waited for; matrix products, arithmetic and copies ran while one was open for 7% of the time, Pallas kernels for 12%

profile of v13, /device:TPU:1, one launch (start us, length us, event | category | flops | bytes accessed | tf_op | source)
XLA Modules:
  0.0 366.1 jit_solution(5808376410079016326)
XLA Ops:
  6.5 1.3 constant_dynamic-slice_fusion
  7.8 0.2 copy.16
  8.0 1.3 dynamic-slice_bitcast_fusion
  9.3 0.0 copy-start.4
  9.4 0.0 copy-start.6
  9.4 1.3 pad_maximum_fusion
  10.7 0.0 all-gather.3.cloned.1.call-update
  10.7 0.0 copy-done.4
  10.7 0.7 fusion.58
  11.4 10.3 %all-to-all-start = ((s32[128,64,4]{0,2,1:T(4,128)}), s32[128,64,4]{0,2,1:T(4,128)S(1)}, u32[]{:S(2)}, u32[]{:S(2)}) async-start(s32[128,64,4]{0,2,1:T(4,128)} %fusion.58), calls=%async_computation | async-start | bytes 262144 | tf_op jit(solution)/shard_map/all_to_all | solution.py:117
  21.8 0.0 all-gather.5.cloned.1.call-start
  21.8 1.0 copy.17
  22.9 0.0 all-gather.5.cloned.1.call-update
  22.9 2.2 pad_convert_fusion.tab_ref
  25.1 5.2 %all-to-all-done = s32[128,64,4]{0,2,1:T(4,128)S(1)} async-done(((s32[128,64,4]{0,2,1:T(4,128)}), s32[128,64,4]{0,2,1:T(4,128)S(1)}, u32[]{:S(2)}, u32[]{:S(2)}) %all-to-all-start) | async-done | bytes 131104 | tf_op jit(solution)/shard_map/all_to_all | solution.py:117
  30.3 2.6 copy.11
  33.0 5.5 %reshape.17.ids_ref = s32[32768]{0:T(1024)} reshape(s32[64,128,4]{2,1,0:T(8,128)} %copy.11) | data formatting | bytes 262144 | tf_op jit(solution)/shard_map/reshape | solution.py:119
  38.4 42.4 %shard_map.73 = bf16[8192,128]{1,0:T(8,128)(2,1)} custom-call(s32[32768]{0:T(1024)} %reshape.17.ids_ref, f32[8200,128]{1,0:T(8,128)} %pad_convert_fusion.tab_ref), custom_call_target="tpu_custom_call" | custom-call | tf_op jit(solution)/shard_map/pallas_call | solution.py:32
  80.8 5.4 %all-to-all-start.1 = ((bf16[64,128,128]{2,1,0:T(8,128)(2,1)}), bf16[64,128,128]{2,1,0:T(8,128)(2,1)}, u32[]{:S(2)}, u32[]{:S(2)}) async-start(bf16[64,128,128]{2,1,0:T(8,128)(2,1)} %bitcast.60), calls=%async_computation.1 | async-start | bytes 4194304 | tf_op jit(solution)/shard_map/all_to_all | solution.py:125
  86.2 0.0 reduce-scatter.2.cloned.1.call-start
  86.3 62.3 %all-gather.3.cloned.1.call-done = bf16[8192,384]{0,1:T(8,128)(2,1)} async-done(((bf16[2048,384]{0,1:T(8,128)(2,1)}), bf16[8192,384]{0,1:T(8,128)(2,1)}) %all-gather.3.cloned.1.call-update) | async-done | bytes 6291472 | tf_op jit(solution)/shard_map/all_gather | solution.py:105
  148.6 1.1 collective-permute-start
  149.7 52.2 %all-gather.5.cloned.1.call-done = bf16[8192,128]{0,1:T(8,128)(2,1)} async-done(((bf16[2048,128]{0,1:T(8,128)(2,1)}), bf16[8192,128]{0,1:T(8,128)(2,1)}) %all-gather.5.cloned.1.call-update) | async-done | bytes 2097168 | tf_op jit(solution)/shard_map/all_gather | solution.py:106
  201.9 0.7 collective-permute-start.1
  202.6 0.0 all-to-all-done.1
  202.6 3.1 fusion.41
  205.7 0.9 collective-permute-done.1
  206.6 2.3 fusion.49
  208.9 0.0 copy-start.3
  208.9 2.5 fusion.36
  211.4 3.2 fusion.30
  214.6 0.7 fusion.24
  215.3 0.7 fusion.12
  216.1 0.8 copy-done.1
  216.9 0.7 convolution_add_fusion.1
  217.6 0.0 collective-permute-done
  217.6 4.5 %fusion.33 = bf16[128,256]{1,0:T(8,128)(2,1)S(1)} fusion(bf16[8192,384]{0,1:T(8,128)(2,1)} %collective-permute-done, bf16[128,8192]{1,0:T(8,128)(2,1)S(1)} %copy-done.3, bf16[64,128,128]{2,1,0:T(8,128)(2,1)} %all-to-all-done.1), kind=kOutput, calls=%fused_computation.36 | convolution fusion | flops 541097984 | bytes 8454144 | tf_op jit(solution)/shard_map/dot_general | solution.py:147
  222.1 2.9 fusion.44
  225.1 0.7 fusion.59
  225.8 0.0 copy-start.5
  225.8 2.6 fusion
  228.4 4.0 %fusion.27 = bf16[16,64,8,128]{3,2,1,0:T(8,128)(2,1)S(1)} fusion(f32[128,8192]{1,0:T(8,128)S(1)} %fusion, f32[8192]{0:T(1024)S(1)} %copy-done.5, f32[128,8192]{1,0:T(8,128)S(1)} %fusion.12, bf16[128,256]{1,0:T(8,128)(2,1)S(1)} %pad_maximum_fusion.2, bf16[8192,384]{0,1:T(8,128)(2,1)} %collective-permute-done, bf16[128,8192]{1,0:T(8,128)(2,1)S(1)} %copy-done.3), kind=kOutput, calls=%fused_computation.33 | convolution fusion | flops 544210944 | bytes 16875520 | tf_op jit(solution)/shard_map/dot_general | solution.py:141
  232.4 0.6 copy.40
  233.0 40.3 %all_to_all.51 = bf16[128,64,128]{2,0,1:T(8,128)(2,1)} all-to-all(bf16[128,64,128]{2,0,1:T(8,128)(2,1)S(1)} %bitcast.59), channel_id=1, replica_groups=mesh['dp'=64,'fsdp'=4] {'dp'}, dimensions={1} | all-to-all | bytes 4194304 | tf_op jit(solution)/shard_map/all_to_all | solution.py:161
  273.3 39.4 %shard_map.74 = bf16[8192,128]{1,0:T(8,128)(2,1)} custom-call(s32[32768]{0:T(1024)} %reshape.17.ids_ref, bf16[8192,128]{1,0:T(8,128)(2,1)} %bitcast.58), custom_call_target="tpu_custom_call" | custom-call | tf_op jit(solution)/shard_map/pallas_call | solution.py:75
  312.7 0.0 reduce-scatter.2.cloned.1.call-update
  312.7 44.8 %reduce-scatter.2.cloned.1.call-done = bf16[2048,128]{1,0:T(8,128)(2,1)} async-done(((bf16[8192,128]{1,0:T(8,128)(2,1)}), bf16[2048,128]{1,0:T(8,128)(2,1)}) %reduce-scatter.2.cloned.1.call-update) | async-done | bytes 524304 | tf_op jit(solution)/shard_map/reduce_scatter | solution.py:165
  357.4 2.1 convert_element_type.30
  (11 shorter events, 0.0 us)
Async XLA Ops:
  6.5 142.1 %all-gather.3.cloned.1.call-start = ((), (), s32[]{:S(2)}) async-start(), calls=%async_computation.4 | async-start | bytes 7864320 | tf_op jit(solution)/shard_map/all_gather | solution.py:105
  9.3 1.4 copy-start.4
  9.4 1.4 copy-start.6
  10.7 12.2 %copy-start.2 = (bf16[8192,128]{1,0:T(8,128)(2,1)S(1)}, bf16[8192,128]{1,0:T(8,128)(2,1)}, u32[]{:S(2)}) copy-start(bf16[8192,128]{1,0:T(8,128)(2,1)} %param.9) | copy-start | bytes 6291460
  11.4 18.9 %all-to-all-start = ((s32[128,64,4]{0,2,1:T(4,128)}), s32[128,64,4]{0,2,1:T(4,128)S(1)}, u32[]{:S(2)}, u32[]{:S(2)}) async-start(s32[128,64,4]{0,2,1:T(4,128)} %fusion.58), calls=%async_computation | async-start | bytes 262144 | tf_op jit(solution)/shard_map/all_to_all | solution.py:117
  21.8 180.1 %all-gather.5.cloned.1.call-start = ((), (), s32[]{:S(2)}) async-start(), calls=%async_computation.5 | async-start | bytes 2621440 | tf_op jit(solution)/shard_map/all_gather | solution.py:106
  80.8 121.8 %all-to-all-start.1 = ((bf16[64,128,128]{2,1,0:T(8,128)(2,1)}), bf16[64,128,128]{2,1,0:T(8,128)(2,1)}, u32[]{:S(2)}, u32[]{:S(2)}) async-start(bf16[64,128,128]{2,1,0:T(8,128)(2,1)} %bitcast.60), calls=%async_computation.1 | async-start | bytes 4194304 | tf_op jit(solution)/shard_map/all_to_all | solution.py:125
  86.2 271.2 %reduce-scatter.2.cloned.1.call-start = ((), (), s32[]{:S(2)}) async-start(), calls=%async_computation.6 | async-start | bytes 2621440 | tf_op jit(solution)/shard_map/reduce_scatter | solution.py:165
  148.6 69.0 %collective-permute-start = (bf16[8192,384]{0,1:T(8,128)(2,1)}, bf16[8192,384]{0,1:T(8,128)(2,1)}, u32[]{:S(2)}, u32[]{:S(2)}) collective-permute-start(bf16[8192,384]{0,1:T(8,128)(2,1)} %all-gather.3.cloned.1.call-done), channel_id=1, source_target_pairs={{0,4},{4,0},{8,12},{12,8},{16,20},{20,16},{24,28},{28,24},{32,36},... | collective-permute-start | bytes 18874376 | tf_op jit(solution)/shard_map/ppermute | solution.py:108
  201.9 4.7 %collective-permute-start.1 = (bf16[8192,128]{0,1:T(8,128)(2,1)}, bf16[8192,128]{0,1:T(8,128)(2,1)S(1)}, u32[]{:S(2)}, u32[]{:S(2)}) collective-permute-start(bf16[8192,128]{0,1:T(8,128)(2,1)} %all-gather.5.cloned.1.call-done), channel_id=1, source_target_pairs={{0,4},{4,0},{8,12},{12,8},{16,20},{20,16},{24,28},{28,24},{32,36},... | collective-permute-start | bytes 6291464 | tf_op jit(solution)/shard_map/ppermute | solution.py:109
  202.6 6.3 %copy-start = (bf16[8192,384]{0,1:T(8,128)(2,1)S(1)}, bf16[8192,384]{0,1:T(8,128)(2,1)}, u32[]{:S(2)}) copy-start(bf16[8192,384]{0,1:T(8,128)(2,1)} %all-gather.3.cloned.1.call-done) | copy-start | bytes 18874372
  208.9 2.5 copy-start.3
  215.3 1.6 copy-start.1
  225.8 2.6 copy-start.5
Sparse Core Ops, SparseCore 0:
  10.8 137.7 all-gather.2
  150.4 51.4 all-gather.4
  312.8 44.5 reduce-scatter.1

commit v14 on v11

--- a/solution.py
+++ b/solution.py
@@ -121,6 +121,16 @@
 
     upstream = cotangent.astype(jnp.float32)
     grad_gate = (upstream * pooled.astype(jnp.float32)).astype(jnp.bfloat16)
+    contract = (((1,), (1,)), ((), ()))
+    grad_low_mine = lax.dot_general(
+        grad_gate, up_mine, contract, preferred_element_type=jnp.float32
+    ).astype(jnp.bfloat16)
+    grad_low_other = lax.dot_general(
+        grad_gate, up_other, contract, preferred_element_type=jnp.float32
+    ).astype(jnp.bfloat16)
+    down_mine, grad_low_mine, grad_low_other = lax.optimization_barrier(
+        (down_mine, grad_low_mine, grad_low_other)
+    )
     low_mine = jnp.dot(pooled, down_mine, preferred_element_type=jnp.float32).astype(jnp.bfloat16)
     low_other = jnp.dot(pooled, down_other, preferred_element_type=jnp.float32).astype(jnp.bfloat16)
     low_mine = lax.optimization_barrier(low_mine)
@@ -130,15 +140,6 @@
         + jnp.dot(low_other, up_other, preferred_element_type=jnp.float32)
         + cross_bias
     )
-    contract = (((1,), (1,)), ((), ()))
-    grad_low_mine = lax.dot_general(
-        grad_gate, up_mine, contract, preferred_element_type=jnp.float32
-    ).astype(jnp.bfloat16)
-    grad_low_other = lax.dot_general(
-        grad_gate, up_other, contract, preferred_element_type=jnp.float32
-    ).astype(jnp.bfloat16)
-    grad_low_mine = lax.optimization_barrier(grad_low_mine)
-    grad_low_other = lax.optimization_barrier(grad_low_other)
     back_term = lax.dot_general(
         grad_low_mine, down_mine, contract, preferred_element_type=jnp.float32
     ) + lax.dot_general(grad_low_other, down_other, contract, preferred_element_type=jnp.float32)

time: 350 us -> 350 us (level)
  transfers between devices with their start and end apart: 7 -> 7, of which waited for: 4 -> 4; matrix products, arithmetic and copies ran while one was open for 8% -> 7% of each run, Pallas kernels for 12% -> 12%
where the time goes in v14:
time: 350 us
  waiting for transfers between devices  147 us (42%)
  Pallas kernels  81.8 us (23%)
  blocking collectives  46.5 us (13%)
  matrix products  24.3 us (7%)
  starting transfers between devices  17.1 us (5%)
  local copies, waits for them, and re-layouts  14.2 us (4%)
  between operations  13.3 us (4%)
  other arithmetic  5.06 us (1%)
    all_gather x1, waiting for transfers between devices, on_device(): down_mine = lax.all_gather(down_mine, 'fsdp', axis=0, tiled=True)  93.3 us
    all_to_all x1, blocking collectives, on_device(): lax.all_to_all(grad_pooled, 'dp', split_axis=1, concat_axis=0, tiled=True)  46.5 us
    reduce_scatter x1, waiting for transfers between devices, on_device(): lax.psum_scatter(partial_value, 'fsdp', scatter_dimension=0, tiled=True)  44.3 us
    pallas_call x1, Pallas kernels, pool_rows(): pl.pallas_call(functools.partial(pool_kernel, blk=blk, slots=slots), grid...  42.5 us
    pallas_call x1, Pallas kernels, scatter_rows(): pl.pallas_call(functools.partial(scatter_kernel, slots=slots), grid_spec=...  39.3 us
    all_to_all x1, starting transfers between devices, on_device(): lax.all_to_all(send_ids, 'dp', split_axis=1, concat_axis=0, tiled=True)  10.3 us
  transfers between devices with their start and end apart: 7, of which 4 were waited for; matrix products, arithmetic and copies ran while one was open for 7% of the time, Pallas kernels for 12%

profile of v14, /device:TPU:1, one launch (start us, length us, event | category | flops | bytes accessed | tf_op | source)
XLA Modules:
  0.0 349.7 jit_solution(3630187908602662521)
XLA Ops:
  6.5 0.0 copy-start.4
  6.5 0.0 copy-start.6
  6.5 0.0 copy-start.3
  6.5 0.0 all-gather.5.cloned.1.call-start
  6.5 2.6 constant_dynamic-slice_fusion
  9.1 0.0 all-gather.5.cloned.1.call-update
  9.1 0.0 all-gather.3.cloned.1.call-start
  9.2 2.3 constant_dynamic-slice_fusion.1
  11.4 0.0 all-gather.3.cloned.1.call-update
  11.5 0.0 copy-done.4
  11.5 0.0 copy-done.6
  11.5 0.7 fusion.21
  12.2 10.3 %all-to-all-start = ((s32[128,64,4]{0,2,1:T(4,128)}), s32[128,64,4]{0,2,1:T(4,128)S(1)}, u32[]{:S(2)}, u32[]{:S(2)}) async-start(s32[128,64,4]{0,2,1:T(4,128)} %fusion.21), calls=%async_computation | async-start | bytes 262144 | tf_op jit(solution)/shard_map/all_to_all | solution.py:112
  22.5 0.0 copy-done.3
  22.5 2.3 pad_convert_fusion.tab_ref
  24.8 6.2 %all-to-all-done = s32[128,64,4]{0,2,1:T(4,128)S(1)} async-done(((s32[128,64,4]{0,2,1:T(4,128)}), s32[128,64,4]{0,2,1:T(4,128)S(1)}, u32[]{:S(2)}, u32[]{:S(2)}) %all-to-all-start) | async-done | bytes 131104 | tf_op jit(solution)/shard_map/all_to_all | solution.py:112
  31.1 2.6 copy.10
  33.7 5.5 %reshape.17.ids_ref = s32[32768]{0:T(1024)} reshape(s32[64,128,4]{2,1,0:T(8,128)} %copy.10) | data formatting | bytes 262144 | tf_op jit(solution)/shard_map/reshape | solution.py:114
  39.2 42.5 %shard_map.73 = bf16[8192,128]{1,0:T(8,128)(2,1)} custom-call(s32[32768]{0:T(1024)} %reshape.17.ids_ref, f32[8200,128]{1,0:T(8,128)} %pad_convert_fusion.tab_ref), custom_call_target="tpu_custom_call" | custom-call | tf_op jit(solution)/shard_map/pallas_call | solution.py:32
  81.7 5.3 %all-to-all-start.1 = ((bf16[64,128,128]{2,1,0:T(8,128)(2,1)}), bf16[64,128,128]{2,1,0:T(8,128)(2,1)}, u32[]{:S(2)}, u32[]{:S(2)}) async-start(bf16[64,128,128]{2,1,0:T(8,128)(2,1)} %bitcast.50), calls=%async_computation.1 | async-start | bytes 4194304 | tf_op jit(solution)/shard_map/all_to_all | solution.py:120
  87.0 0.0 reduce-scatter.2.cloned.1.call-start
  87.0 3.5 %all-gather.5.cloned.1.call-done = bf16[256,8192]{1,0:T(8,128)(2,1)} async-done(((bf16[256,2048]{1,0:T(8,128)(2,1)}), bf16[256,8192]{1,0:T(8,128)(2,1)}) %all-gather.5.cloned.1.call-update) | async-done | bytes 4194320 | tf_op jit(solution)/shard_map/all_gather | solution.py:104
  90.6 0.7 collective-permute-start
  91.3 93.3 %all-gather.3.cloned.1.call-done = bf16[8192,256]{1,0:T(8,128)(2,1)} async-done(((bf16[2048,256]{1,0:T(8,128)(2,1)}), bf16[8192,256]{1,0:T(8,128)(2,1)}) %all-gather.3.cloned.1.call-update) | async-done | bytes 4194320 | tf_op jit(solution)/shard_map/all_gather | solution.py:103
  184.6 0.7 collective-permute-start.1
  185.3 0.0 all-to-all-done.1
  185.3 0.0 copy-done
  185.3 4.4 %convolution_convert_fusion.1 = bf16[128,256]{1,0:T(8,128)(2,1)S(1)} fusion(bf16[256,8192]{1,0:T(8,128)(2,1)} %all-gather.5.cloned.1.call-done, bf16[128,8192]{1,0:T(8,128)(2,1)S(1)} %copy-done, bf16[64,128,128]{2,1,0:T(8,128)(2,1)} %all-to-all-done.1), kind=kOutput, calls=%fused_computation.21 | convolution fusion | flops 541097984 | bytes 8454144 | tf_op jit(solution)/shard_map/dot_general | solution.py:125
  189.7 0.0 copy-start.2
  189.7 0.0 collective-permute-done
  189.7 4.5 %convolution_convert_fusion = bf16[128,256]{1,0:T(8,128)(2,1)S(1)} fusion(bf16[256,8192]{1,0:T(8,128)(2,1)} %collective-permute-done, bf16[128,8192]{1,0:T(8,128)(2,1)S(1)} %copy-done, bf16[64,128,128]{2,1,0:T(8,128)(2,1)} %all-to-all-done.1), kind=kOutput, calls=%fused_computation.20 | convolution fusion | flops 541097984 | bytes 8454144 | tf_op jit(solution)/shard_map/dot_general | solution.py:128
  194.2 0.0 copy-done.2
  194.2 2.3 fusion.13
  196.6 0.0 collective-permute-done.1
  196.6 3.5 %fusion.16 = bf16[128,256]{1,0:T(8,128)(2,1)S(1)} fusion(bf16[8192,256]{1,0:T(8,128)(2,1)} %collective-permute-done.1, bf16[64,128,128]{2,1,0:T(8,128)(2,1)} %all-to-all-done.1), kind=kOutput, calls=%fused_computation.19 | convolution fusion | flops 536903680 | bytes 6356992 | tf_op jit(solution)/shard_map/dot_general | solution.py:135
  200.1 0.0 copy-start.1
  200.1 1.5 fusion.23
  201.6 0.7 copy-done.1
  202.3 0.7 fusion.22
  203.0 0.0 copy-done.5
  203.1 3.5 %fusion.3 = f32[128,8192]{1,0:T(8,128)S(1)} fusion(f32[128,8192]{1,0:T(8,128)S(1)} %fusion.22, bf16[128,256]{1,0:T(8,128)(2,1)S(1)} %fusion.16, bf16[256,8192]{1,0:T(8,128)(2,1)} %collective-permute-done, bf16[128,8192]{1,0:T(8,128)(2,1)S(1)} %copy-done, f32[8192]{0:T(1024)S(1)} %copy-done.5), kind=kOutput, calls=%fused_computation.5 | convolution fusion | flops 542113792 | bytes 14778368 | tf_op jit(solution)/shard_map/dot_general | solution.py:140
  206.6 3.8 %fusion.10 = bf16[16,64,8,128]{3,2,1,0:T(8,128)(2,1)S(1)} fusion(f32[128,8192]{1,0:T(8,128)S(1)} %fusion.3, f32[128,8192]{1,0:T(8,128)S(1)} %fusion.23, bf16[128,256]{1,0:T(8,128)(2,1)S(1)} %convolution_convert_fusion, bf16[8192,256]{1,0:T(8,128)(2,1)} %collective-permute-done.1), kind=kOutput, calls=%fused_computation.15 | convolution fusion | flops 540016640 | bytes 14745600 | tf_op jit(solution)/shard_map/dot_general | solution.py:145
  210.4 0.6 copy.31
  211.0 46.5 %all_to_all.51 = bf16[128,64,128]{2,0,1:T(8,128)(2,1)} all-to-all(bf16[128,64,128]{2,0,1:T(8,128)(2,1)S(1)} %bitcast.49), channel_id=1, replica_groups=mesh['dp'=64,'fsdp'=4] {'dp'}, dimensions={1} | all-to-all | bytes 4194304 | tf_op jit(solution)/shard_map/all_to_all | solution.py:147
  257.5 39.3 %shard_map.74 = bf16[8192,128]{1,0:T(8,128)(2,1)} custom-call(s32[32768]{0:T(1024)} %reshape.17.ids_ref, bf16[8192,128]{1,0:T(8,128)(2,1)} %bitcast.48), custom_call_target="tpu_custom_call" | custom-call | tf_op jit(solution)/shard_map/pallas_call | solution.py:75
  296.8 0.0 reduce-scatter.2.cloned.1.call-update
  296.8 44.3 %reduce-scatter.2.cloned.1.call-done = bf16[2048,128]{1,0:T(8,128)(2,1)} async-done(((bf16[8192,128]{1,0:T(8,128)(2,1)}), bf16[2048,128]{1,0:T(8,128)(2,1)}) %reduce-scatter.2.cloned.1.call-update) | async-done | bytes 524304 | tf_op jit(solution)/shard_map/reduce_scatter | solution.py:151
  341.1 2.1 convert_element_type.36
  (2 shorter events, 0.0 us)
Async XLA Ops:
  6.5 4.9 %copy-start.4 = (s32[128,64,4]{0,2,1:T(4,128)S(1)}, s32[128,64,4]{0,2,1:T(4,128)}, u32[]{:S(2)}) copy-start(s32[128,64,4]{0,2,1:T(4,128)} %param.7) | copy-start | bytes 393220
  6.5 4.9 %copy-start.6 = (s32[128,64]{0,1:T(8,128)S(1)}, s32[128,64]{0,1:T(8,128)}, u32[]{:S(2)}) copy-start(s32[128,64]{0,1:T(8,128)} %param.8) | copy-start | bytes 98308
  6.5 16.0 %copy-start.3 = (bf16[8192,128]{1,0:T(8,128)(2,1)S(1)}, bf16[8192,128]{1,0:T(8,128)(2,1)}, u32[]{:S(2)}) copy-start(bf16[8192,128]{1,0:T(8,128)(2,1)} %param.9) | copy-start | bytes 6291460
  6.5 84.0 %all-gather.5.cloned.1.call-start = ((), (), s32[]{:S(2)}) async-start(), calls=%async_computation.5 | async-start | bytes 5242880 | tf_op jit(solution)/shard_map/all_gather | solution.py:104
  9.1 175.5 %all-gather.3.cloned.1.call-start = ((), (), s32[]{:S(2)}) async-start(), calls=%async_computation.4 | async-start | bytes 5242880 | tf_op jit(solution)/shard_map/all_gather | solution.py:103
  12.2 18.9 %all-to-all-start = ((s32[128,64,4]{0,2,1:T(4,128)}), s32[128,64,4]{0,2,1:T(4,128)S(1)}, u32[]{:S(2)}, u32[]{:S(2)}) async-start(s32[128,64,4]{0,2,1:T(4,128)} %fusion.21), calls=%async_computation | async-start | bytes 262144 | tf_op jit(solution)/shard_map/all_to_all | solution.py:112
  39.2 146.1 %copy-start = (bf16[128,8192]{1,0:T(8,128)(2,1)S(1)}, bf16[128,8192]{1,0:T(8,128)(2,1)}, u32[]{:S(2)}) copy-start(bf16[128,8192]{1,0:T(8,128)(2,1)} %param.13) | copy-start | bytes 6291460
  81.7 103.6 %all-to-all-start.1 = ((bf16[64,128,128]{2,1,0:T(8,128)(2,1)}), bf16[64,128,128]{2,1,0:T(8,128)(2,1)}, u32[]{:S(2)}, u32[]{:S(2)}) async-start(bf16[64,128,128]{2,1,0:T(8,128)(2,1)} %bitcast.50), calls=%async_computation.1 | async-start | bytes 4194304 | tf_op jit(solution)/shard_map/all_to_all | solution.py:120
  87.0 254.1 %reduce-scatter.2.cloned.1.call-start = ((), (), s32[]{:S(2)}) async-start(), calls=%async_computation.6 | async-start | bytes 2621440 | tf_op jit(solution)/shard_map/reduce_scatter | solution.py:151
  90.6 99.1 %collective-permute-start = (bf16[256,8192]{1,0:T(8,128)(2,1)}, bf16[256,8192]{1,0:T(8,128)(2,1)}, u32[]{:S(2)}, u32[]{:S(2)}) collective-permute-start(bf16[256,8192]{1,0:T(8,128)(2,1)} %all-gather.5.cloned.1.call-done), channel_id=1, source_target_pairs={{0,4},{4,0},{8,12},{12,8},{16,20},{20,16},{24,28},{28,24},{32,36},... | collective-permute-start | bytes 12582920 | tf_op jit(solution)/shard_map/ppermute | solution.py:107
  184.6 11.9 %collective-permute-start.1 = (bf16[8192,256]{1,0:T(8,128)(2,1)}, bf16[8192,256]{1,0:T(8,128)(2,1)}, u32[]{:S(2)}, u32[]{:S(2)}) collective-permute-start(bf16[8192,256]{1,0:T(8,128)(2,1)} %all-gather.3.cloned.1.call-done), channel_id=1, source_target_pairs={{0,4},{4,0},{8,12},{12,8},{16,20},{20,16},{24,28},{28,24},{32,36},... | collective-permute-start | bytes 12582920 | tf_op jit(solution)/shard_map/ppermute | solution.py:106
  189.7 4.5 %copy-start.2 = (bf16[8192,256]{1,0:T(8,128)(2,1)S(1)}, bf16[8192,256]{1,0:T(8,128)(2,1)}, u32[]{:S(2)}) copy-start(bf16[8192,256]{1,0:T(8,128)(2,1)} %all-gather.3.cloned.1.call-done) | copy-start | bytes 12582916
  200.1 2.2 copy-start.1
  202.3 0.8 copy-start.5
Sparse Core Ops, SparseCore 0:
  9.2 81.2 all-gather.4
  92.4 92.1 all-gather.2
  296.9 44.1 reduce-scatter.1
